TPU v7x, 768 devices: a whole 4x8x12 slice. The times are simulated.
768 devices in a mesh: ctx: 128 (over y, x, z_hi, core), fsdp: 6 (over z_lo).
Axes of the slice: x: 4, y: 8, z: 12 (z_hi: 2, z_lo: 6; z = z_hi * 6 + z_lo), core: 2. Of those that a mesh axis runs over, the one named last changes fastest.
Arguments:
- query_rows: bfloat16 [98304, 4096], P(('ctx', 'fsdp')), may hold values from -40 to 40
- key_rows: bfloat16 [98304, 512], P(('ctx', 'fsdp')), may hold values from -6 to 6
- value_matrix: bfloat16 [98304, 512], P(('ctx', 'fsdp')), may hold values from -6 to 6
- out_grad: bfloat16 [98304, 4096], P(('ctx', 'fsdp')), may hold values from -24 to 24
- segments: int32 [98304], P(('ctx', 'fsdp')), may hold values from 0 to 127, never falling along the last dimension, each value on 1 to 1536 neighbouring positions
Outputs:
- query_grad: bfloat16 [98304, 4096], P(('ctx', 'fsdp'))
- key_grad: bfloat16 [98304, 512], P(('ctx', 'fsdp'))
- value_grad: bfloat16 [98304, 512], P(('ctx', 'fsdp'))
Inputs may be any that keep to these rules, and one draw needn't show every extreme that they name: `segments`: segment numbers never fall along the sequence.
All inputs are finite; a program needn't handle non-finite values.
Results may differ from a plain program's by a relative error of at most 0.0085.
Values may be sent and summed in bfloat16 or wider, within the bound.
No kernel may reach another device: no remote copies, remote signals or barrier semaphores. Data moves between devices by JAX's collectives and lax.ppermute only.
A program may use at most 64 MiB of HBM per device.

v0:
```python
import math

import jax
import jax.numpy as jnp
from jax import lax
from jax.sharding import PartitionSpec as P

HEAD_WIDTH = 128
SPAN = 3


def from_behind(block, axis, distance):
    devices = range(lax.axis_size(axis))
    route = [(i - distance, i) for i in devices if i - distance in devices]
    return lax.ppermute(block, axis, route)


def band_grads(
    query_blk, grad_blk, key_win, value_win, query_seg, key_seg, query_first, key_first, window
):
    tok_rows = query_blk.shape[0]
    key_count = key_win.shape[0]
    kv_heads = key_win.shape[1] // HEAD_WIDTH
    heads_per_group = query_blk.shape[1] // key_win.shape[1]
    inv_root = 1.0 / math.sqrt(HEAD_WIDTH)
    query_pos = query_first + jnp.arange(tok_rows, dtype=jnp.int32)
    key_pos = key_first + jnp.arange(key_count, dtype=jnp.int32)
    allowed = (key_pos[None, :] > query_pos[:, None] - window) & (
        key_pos[None, :] <= query_pos[:, None]
    )
    allowed = allowed & (key_pos[None, :] >= 0) & (key_seg[None, :] == query_seg[:, None])
    query_parts = []
    key_parts = []
    value_parts = []
    for kv_head in range(kv_heads):
        k_head = key_win[:, kv_head * HEAD_WIDTH : (kv_head + 1) * HEAD_WIDTH]
        v_head = value_win[:, kv_head * HEAD_WIDTH : (kv_head + 1) * HEAD_WIDTH]
        lower = kv_head * heads_per_group * HEAD_WIDTH
        q_head = query_blk[:, lower : lower + heads_per_group * HEAD_WIDTH].reshape(
            tok_rows, heads_per_group, HEAD_WIDTH
        )
        o_grad = grad_blk[:, lower : lower + heads_per_group * HEAD_WIDTH].reshape(
            tok_rows, heads_per_group, HEAD_WIDTH
        )
        scores = (
            jnp.einsum("trd,kd->rtk", q_head, k_head, preferred_element_type=jnp.float32) * inv_root
        )
        scores = jnp.where(allowed[None], scores, -1e30)
        row_max = jnp.max(scores, axis=-1, keepdims=True)
        weights = jnp.exp(scores - row_max)
        probs = weights / jnp.sum(weights, axis=-1, keepdims=True)
        prob_grad = jnp.einsum("trd,kd->rtk", o_grad, v_head, preferred_element_type=jnp.float32)
        row_delta = jnp.sum(probs * prob_grad, axis=-1, keepdims=True)
        score_grad = (probs * (prob_grad - row_delta) * inv_root).astype(jnp.bfloat16)
        probs_low = probs.astype(jnp.bfloat16)
        query_parts.append(
            jnp.einsum(
                "rtk,kd->trd", score_grad, k_head, preferred_element_type=jnp.float32
            ).reshape(tok_rows, heads_per_group * HEAD_WIDTH)
        )
        key_parts.append(
            jnp.einsum("rtk,trd->kd", score_grad, q_head, preferred_element_type=jnp.float32)
        )
        value_parts.append(
            jnp.einsum("rtk,trd->kd", probs_low, o_grad, preferred_element_type=jnp.float32)
        )
    return (
        jnp.concatenate(query_parts, 1),
        jnp.concatenate(key_parts, 1),
        jnp.concatenate(value_parts, 1),
    )


def body(query_rows, key_rows, value_matrix, out_grad, segments):
    tok_rows = query_rows.shape[0]
    position = lax.axis_index(("ctx", "fsdp"))
    query_first = position * tok_rows
    window = SPAN * tok_rows
    nearby = [(key_rows, value_matrix, segments)]
    for hop_back in range(1, SPAN + 1):
        nearby.insert(0, from_behind((key_rows, value_matrix, segments), ("ctx", "fsdp"), hop_back))
    key_win = jnp.concatenate([member[0] for member in nearby], 0)
    value_win = jnp.concatenate([member[1] for member in nearby], 0)
    seg_win = jnp.concatenate([member[2] for member in nearby], 0)
    dq_part, dk_part, dv_part = band_grads(
        query_rows,
        out_grad,
        key_win,
        value_win,
        segments,
        seg_win,
        query_first,
        query_first - window,
        window,
    )
    carried = (dk_part[:tok_rows], dv_part[:tok_rows])
    for relay_step in range(1, SPAN + 1):
        received = from_behind((carried[0], carried[1]), ("ctx", "fsdp"), -1)
        lower = relay_step * tok_rows
        carried = (
            received[0] + dk_part[lower : lower + tok_rows],
            received[1] + dv_part[lower : lower + tok_rows],
        )
    key_own = carried[0]
    value_own = carried[1]
    return (
        dq_part.astype(jnp.bfloat16),
        key_own.astype(jnp.bfloat16),
        value_own.astype(jnp.bfloat16),
    )


def solution(mesh):
    return jax.shard_map(
        body,
        mesh=mesh,
        in_specs=(
            P(("ctx", "fsdp"), None),
            P(("ctx", "fsdp"), None),
            P(("ctx", "fsdp"), None),
            P(("ctx", "fsdp"), None),
            P(("ctx", "fsdp")),
        ),
        out_specs=(P(("ctx", "fsdp"), None), P(("ctx", "fsdp"), None), P(("ctx", "fsdp"), None)),
        check_vma=False,
    )
```

profile of v0, /device:TPU:33, one launch (start us, length us, event | category | flops | bytes accessed | tf_op | source)
XLA Modules:
  0.0 167.2 jit_solution(11322004554205975959)
XLA Ops:
  0.6 4.1 %collective-permute-start.5 = (s32[128]{0:T(128)}, s32[128]{0:T(128)}, u32[]{:S(2)}, u32[]{:S(2)}) collective-permute-start(s32[128]{0:T(128)} %param.9), channel_id=1, source_target_pairs={{0,1},{1,2},{2,3},{3,4},{4,5},{5,6},{6,7},{7,8},{8,9},{9,10},{10,1... | collective-permute-start | bytes 1544 | tf_op jit(solution)/shard_map/ppermute | solution.py:15
  4.8 5.8 %collective-permute-start.4 = (s32[128]{0:T(128)}, s32[128]{0:T(128)}, u32[]{:S(2)}, u32[]{:S(2)}) collective-permute-start(s32[128]{0:T(128)} %param.9), channel_id=1, source_target_pairs={{0,2},{1,3},{2,4},{3,5},{4,6},{5,7},{6,8},{7,9},{8,10},{9,11},{10,... | collective-permute-start | bytes 1544 | tf_op jit(solution)/shard_map/ppermute | solution.py:15
  10.6 9.4 %collective-permute-start.3 = (s32[128]{0:T(128)}, s32[128]{0:T(128)}, u32[]{:S(2)}, u32[]{:S(2)}) collective-permute-start(s32[128]{0:T(128)} %param.9), channel_id=1, source_target_pairs={{0,3},{1,4},{2,5},{3,6},{4,7},{5,8},{6,9},{7,10},{8,11},{9,12},{10... | collective-permute-start | bytes 1544 | tf_op jit(solution)/shard_map/ppermute | solution.py:15
  20.0 4.9 %collective-permute-start.1 = (bf16[128,512]{1,0:T(8,128)(2,1)}, bf16[128,512]{1,0:T(8,128)(2,1)}, u32[]{:S(2)}, u32[]{:S(2)}) collective-permute-start(bf16[128,512]{1,0:T(8,128)(2,1)} %param.6), channel_id=1, source_target_pairs={{0,2},{1,3},{2,4},{3,5},{4,6},{5,7},{6,8},{7,9},{8,10},{9,11},{10,... | collective-permute-start | bytes 393224 | tf_op jit(solution)/shard_map/ppermute | solution.py:15
  24.9 5.2 %collective-permute-start = (bf16[128,512]{1,0:T(8,128)(2,1)}, bf16[128,512]{1,0:T(8,128)(2,1)}, u32[]{:S(2)}, u32[]{:S(2)}) collective-permute-start(bf16[128,512]{1,0:T(8,128)(2,1)} %param.6), channel_id=1, source_target_pairs={{0,3},{1,4},{2,5},{3,6},{4,7},{5,8},{6,9},{7,10},{8,11},{9,12},{10... | collective-permute-start | bytes 393224 | tf_op jit(solution)/shard_map/ppermute | solution.py:15
  30.2 0.5 broadcast_compare_fusion
  30.7 1.3 fusion.86
  31.9 0.8 copy.104
  32.8 0.9 copy.108
  33.6 0.8 copy.106
  34.6 0.2 copy.110
  34.8 0.2 copy.105
  34.9 0.2 copy.109
  35.1 0.2 copy.107
  35.3 0.2 copy.111
  35.5 2.5 %collective-permute-start.2 = (bf16[128,512]{1,0:T(8,128)(2,1)S(1)}, bf16[128,512]{1,0:T(8,128)(2,1)S(1)}, u32[]{:S(2)}, u32[]{:S(2)}) collective-permute-start(bf16[128,512]{1,0:T(8,128)(2,1)S(1)} %copy-done.15), channel_id=1, source_target_pairs={{0,1},{1,2},{2,3},{3,4},{4,5},{5,6},{6,7},{7,8},{8,9},{9,10},{10,1... | collective-permute-start | bytes 393224 | tf_op jit(solution)/shard_map/ppermute | solution.py:15
  38.0 3.7 %collective-permute-start.7 = (bf16[128,512]{1,0:T(8,128)(2,1)S(1)}, bf16[128,512]{1,0:T(8,128)(2,1)S(1)}, u32[]{:S(2)}, u32[]{:S(2)}) collective-permute-start(bf16[128,512]{1,0:T(8,128)(2,1)S(1)} %copy-done.14), channel_id=1, source_target_pairs={{0,2},{1,3},{2,4},{3,5},{4,6},{5,7},{6,8},{7,9},{8,10},{9,11},{10,... | collective-permute-start | bytes 393224 | tf_op jit(solution)/shard_map/ppermute | solution.py:15
  41.7 2.8 %collective-permute-start.6 = (bf16[128,512]{1,0:T(8,128)(2,1)S(1)}, bf16[128,512]{1,0:T(8,128)(2,1)S(1)}, u32[]{:S(2)}, u32[]{:S(2)}) collective-permute-start(bf16[128,512]{1,0:T(8,128)(2,1)S(1)} %copy-done.14), channel_id=1, source_target_pairs={{0,3},{1,4},{2,5},{3,6},{4,7},{5,8},{6,9},{7,10},{8,11},{9,12},{10... | collective-permute-start | bytes 393224 | tf_op jit(solution)/shard_map/ppermute | solution.py:15
  44.6 0.7 pad_add_fusion
  45.2 0.9 compare_and_fusion
  46.2 8.0 %collective-permute-done.6 = bf16[128,512]{1,0:T(8,128)(2,1)S(1)} collective-permute-done((bf16[128,512]{1,0:T(8,128)(2,1)S(1)}, bf16[128,512]{1,0:T(8,128)(2,1)S(1)}, u32[]{:S(2)}, u32[]{:S(2)}) %collective-permute-start.6) | collective-permute-done | bytes 131104 | tf_op jit(solution)/shard_map/ppermute | solution.py:15
  54.1 1.9 %collective-permute-start.8 = (bf16[128,512]{1,0:T(8,128)(2,1)S(1)}, bf16[128,512]{1,0:T(8,128)(2,1)S(1)}, u32[]{:S(2)}, u32[]{:S(2)}) collective-permute-start(bf16[128,512]{1,0:T(8,128)(2,1)S(1)} %copy-done.14), channel_id=1, source_target_pairs={{0,1},{1,2},{2,3},{3,4},{4,5},{5,6},{6,7},{7,8},{8,9},{9,10},{10,1... | collective-permute-start | bytes 393224 | tf_op jit(solution)/shard_map/ppermute | solution.py:15
  56.1 11.1 %collective-permute-done.8 = bf16[128,512]{1,0:T(8,128)(2,1)S(1)} collective-permute-done((bf16[128,512]{1,0:T(8,128)(2,1)S(1)}, bf16[128,512]{1,0:T(8,128)(2,1)S(1)}, u32[]{:S(2)}, u32[]{:S(2)}) %collective-permute-start.8) | collective-permute-done | bytes 131104 | tf_op jit(solution)/shard_map/ppermute | solution.py:15
  67.3 1.1 constant_dynamic-update-slice_fusion.3
  68.4 0.9 constant_dynamic-update-slice_fusion.2
  69.3 0.8 copy-done.17
  70.1 0.4 fusion.54
  70.6 3.0 %fusion.88 = (f32[8,128]{1,0:T(8,128)S(1)}, f32[8,128,512]{1,2,0:T(8,128)}) fusion(pred[128,512]{0,1:T(8,128)(4,1)} %compare_and_fusion, bf16[128,8,128]{0,2,1:T(8,128)(2,1)S(1)} %bitcast.265, bf16[512,512]{1,0:T(8,128)(2,1)} %copy-done.17), kind=kOutput, calls=%fused_computation.147 | convolution fusion | flops 136315392 | bytes 2560000 | tf_op jit(solution)/shard_map/sub | solution.py:50
  73.6 2.8 %convolution_bitcast_fusion = f32[512,128]{0,1:T(8,128)} fusion(bf16[128,8,128]{0,2,1:T(8,128)(2,1)S(1)} %bitcast.255, f32[8,128]{1,0:T(8,128)S(1)} %get-tuple-element.17, pred[128,512]{0,1:T(8,128)(4,1)S(1)} %copy-done.16, bf16[128,8,128]{0,2,1:T(8,128)(2,1)S(1)} %bitcast.266, bf16[512,512]{1,0:T(8,128)(2,1)} %copy-done.17), kind=kOutput, calls=%fused_computation.44 | convolution fusion | flops 271058432 | bytes 987136 | tf_op jit(solution)/shard_map/rtk,trd->kd/dot_general | solution.py:65
  76.4 3.7 %convolution_bitcast_fusion.4 = f32[512,128]{0,1:T(8,128)} fusion(bf16[128,8,128]{0,2,1:T(8,128)(2,1)S(1)} %bitcast.267, f32[512,128,8]{1,0,2:T(8,128)S(1)} %fusion.54, f32[8,128,512]{1,2,0:T(8,128)} %get-tuple-element.18, f32[8,128]{1,0:T(8,128)S(1)} %get-tuple-element.17), kind=kOutput, calls=%fused_computation.48 | convolution fusion | flops 137889280 | bytes 4722688 | tf_op jit(solution)/shard_map/rtk,trd->kd/dot_general | solution.py:62
  80.1 3.8 %convolution_convert_fusion = bf16[128,8,128]{2,0,1:T(8,128)(2,1)} fusion(f32[512,128,8]{1,0,2:T(8,128)S(1)} %fusion.54, bf16[512,512]{1,0:T(8,128)(2,1)} %copy-done.17, f32[8,128,512]{1,2,0:T(8,128)} %get-tuple-element.18, f32[8,128]{1,0:T(8,128)S(1)} %get-tuple-element.17), kind=kOutput, calls=%fused_computation.40 | convolution fusion | flops 138020352 | bytes 8790016 | tf_op jit(solution)/shard_map/rtk,kd->trd/dot_general | solution.py:57
  83.9 0.4 fusion.56
  84.3 3.1 %fusion.90 = (f32[8,128]{1,0:T(8,128)S(1)}, f32[8,128,512]{1,2,0:T(8,128)}) fusion(pred[128,512]{0,1:T(8,128)(4,1)S(1)} %copy-done.16, bf16[128,8,128]{0,2,1:T(8,128)(2,1)} %bitcast.262, bf16[512,512]{1,0:T(8,128)(2,1)} %copy-done.17), kind=kOutput, calls=%fused_computation.149 | convolution fusion | flops 136315392 | bytes 2560000 | tf_op jit(solution)/shard_map/sub | solution.py:50
  87.5 2.9 %convolution_bitcast_fusion.2 = f32[512,128]{0,1:T(8,128)} fusion(bf16[128,8,128]{0,2,1:T(8,128)(2,1)S(1)} %bitcast.253, f32[8,128]{1,0:T(8,128)S(1)} %get-tuple-element.21, pred[128,512]{0,1:T(8,128)(4,1)S(1)} %copy-done.16, bf16[128,8,128]{0,2,1:T(8,128)(2,1)} %bitcast.263, bf16[512,512]{1,0:T(8,128)(2,1)} %copy-done.17), kind=kOutput, calls=%fused_computation.46 | convolution fusion | flops 271058432 | bytes 987136 | tf_op jit(solution)/shard_map/rtk,trd->kd/dot_general | solution.py:65
  90.3 3.7 %convolution_bitcast_fusion.6 = f32[512,128]{0,1:T(8,128)} fusion(bf16[128,8,128]{0,2,1:T(8,128)(2,1)} %bitcast.264, f32[512,128,8]{1,0,2:T(8,128)S(1)} %fusion.56, f32[8,128,512]{1,2,0:T(8,128)} %get-tuple-element.22, f32[8,128]{1,0:T(8,128)S(1)} %get-tuple-element.21), kind=kOutput, calls=%fused_computation.50 | convolution fusion | flops 137889280 | bytes 4722688 | tf_op jit(solution)/shard_map/rtk,trd->kd/dot_general | solution.py:62
  94.1 3.8 %convolution_convert_fusion.2 = bf16[128,8,128]{2,0,1:T(8,128)(2,1)} fusion(f32[512,128,8]{1,0,2:T(8,128)S(1)} %fusion.56, bf16[512,512]{1,0:T(8,128)(2,1)} %copy-done.17, f32[8,128,512]{1,2,0:T(8,128)} %get-tuple-element.22, f32[8,128]{1,0:T(8,128)S(1)} %get-tuple-element.21), kind=kOutput, calls=%fused_computation.42 | convolution fusion | flops 138020352 | bytes 8790016 | tf_op jit(solution)/shard_map/rtk,kd->trd/dot_general | solution.py:57
  97.8 1.8 %fusion.55 = f32[512,128,8]{1,0,2:T(8,128)} fusion(bf16[128,8,128]{0,2,1:T(8,128)(2,1)S(1)} %bitcast.250, bf16[512,512]{1,0:T(8,128)(2,1)S(1)} %copy-done.3), kind=kOutput, calls=%fused_computation.96 | convolution fusion | flops 134217728 | bytes 2490368 | tf_op jit(solution)/shard_map/trd,kd->rtk/dot_general | solution.py:52
  99.6 0.4 fusion.57
  100.0 3.3 %fusion.89 = (f32[8,128]{1,0:T(8,128)S(1)}, f32[8,128,512]{1,2,0:T(8,128)}) fusion(pred[128,512]{0,1:T(8,128)(4,1)S(1)} %copy-done.16, bf16[128,8,128]{0,2,1:T(8,128)(2,1)S(1)} %bitcast.259, bf16[512,512]{1,0:T(8,128)(2,1)} %copy-done.17), kind=kOutput, calls=%fused_computation.148 | convolution fusion | flops 136315392 | bytes 2560000 | tf_op jit(solution)/shard_map/sub | solution.py:50
  103.3 2.1 %convolution_bitcast_fusion.1 = f32[512,128]{0,1:T(8,128)S(1)} fusion(bf16[128,8,128]{0,2,1:T(8,128)(2,1)S(1)} %bitcast.251, f32[8,128]{1,0:T(8,128)S(1)} %get-tuple-element.19, pred[128,512]{0,1:T(8,128)(4,1)S(1)} %copy-done.16, bf16[128,8,128]{0,2,1:T(8,128)(2,1)S(1)} %bitcast.260, bf16[512,512]{1,0:T(8,128)(2,1)} %copy-done.17), kind=kOutput, calls=%fused_computation.45 | convolution fusion | flops 271058432 | bytes 987136 | tf_op jit(solution)/shard_map/rtk,trd->kd/dot_general | solution.py:65
  105.4 3.0 %fusion.91 = (f32[8,128]{1,0:T(8,128)S(1)}, f32[8,128,512]{1,2,0:T(8,128)}) fusion(pred[128,512]{0,1:T(8,128)(4,1)S(1)} %copy-done.16, bf16[128,8,128]{0,2,1:T(8,128)(2,1)S(1)} %bitcast.256, bf16[512,512]{1,0:T(8,128)(2,1)} %copy-done.17), kind=kOutput, calls=%fused_computation.150 | convolution fusion | flops 136315392 | bytes 2560000 | tf_op jit(solution)/shard_map/sub | solution.py:50
  108.4 2.8 %convolution_bitcast_fusion.3 = f32[512,128]{0,1:T(8,128)} fusion(bf16[128,8,128]{0,2,1:T(8,128)(2,1)S(1)} %bitcast.249, f32[8,128]{1,0:T(8,128)S(1)} %get-tuple-element.23, pred[128,512]{0,1:T(8,128)(4,1)S(1)} %copy-done.16, bf16[128,8,128]{0,2,1:T(8,128)(2,1)S(1)} %bitcast.257, bf16[512,512]{1,0:T(8,128)(2,1)} %copy-done.17), kind=kOutput, calls=%fused_computation.47 | convolution fusion | flops 271058432 | bytes 987136 | tf_op jit(solution)/shard_map/rtk,trd->kd/dot_general | solution.py:65
  111.1 5.0 %convolution_bitcast_fusion.5 = f32[512,128]{0,1:T(8,128)} fusion(bf16[128,8,128]{0,2,1:T(8,128)(2,1)S(1)} %bitcast.261, f32[512,128,8]{1,0,2:T(8,128)} %fusion.55, f32[8,128,512]{1,2,0:T(8,128)} %get-tuple-element.20, f32[8,128]{1,0:T(8,128)S(1)} %get-tuple-element.19), kind=kOutput, calls=%fused_computation.49 | convolution fusion | flops 137889280 | bytes 4722688 | tf_op jit(solution)/shard_map/rtk,trd->kd/dot_general | solution.py:62
  116.1 4.0 %convolution_bitcast_fusion.7 = f32[512,128]{0,1:T(8,128)} fusion(bf16[128,8,128]{0,2,1:T(8,128)(2,1)S(1)} %bitcast.258, f32[512,128,8]{1,0,2:T(8,128)S(1)} %fusion.57, f32[8,128,512]{1,2,0:T(8,128)} %get-tuple-element.24, f32[8,128]{1,0:T(8,128)S(1)} %get-tuple-element.23), kind=kOutput, calls=%fused_computation.51 | convolution fusion | flops 137889280 | bytes 4722688 | tf_op jit(solution)/shard_map/rtk,trd->kd/dot_general | solution.py:62
  120.1 1.2 pad_maximum_fusion.1
  121.3 4.4 %collective-permute-start.9 = (f32[128,512]{0,1:T(8,128)S(1)}, f32[128,512]{0,1:T(8,128)S(1)}, u32[]{:S(2)}, u32[]{:S(2)}) collective-permute-start(f32[128,512]{0,1:T(8,128)S(1)} %slice.104), channel_id=1, source_target_pairs={{1,0},{2,1},{3,2},{4,3},{5,4},{6,5},{7,6},{8,7},{9,8},{10,9},{11,1... | collective-permute-start | bytes 786440 | tf_op jit(solution)/shard_map/ppermute | solution.py:15
  125.8 0.8 slice.108
  126.6 1.9 %collective-permute-start.12 = (f32[128,512]{0,1:T(8,128)}, f32[128,512]{0,1:T(8,128)S(1)}, u32[]{:S(2)}, u32[]{:S(2)}) collective-permute-start(f32[128,512]{0,1:T(8,128)} %slice.108), channel_id=1, source_target_pairs={{1,0},{2,1},{3,2},{4,3},{5,4},{6,5},{7,6},{8,7},{9,8},{10,9},{11,1... | collective-permute-start | bytes 786440 | tf_op jit(solution)/shard_map/ppermute | solution.py:15
  128.5 4.3 %convolution_convert_fusion.1 = bf16[128,8,128]{2,0,1:T(8,128)(2,1)S(1)} fusion(f32[512,128,8]{1,0,2:T(8,128)} %fusion.55, bf16[512,512]{1,0:T(8,128)(2,1)} %copy-done.17, f32[8,128,512]{1,2,0:T(8,128)} %get-tuple-element.20, f32[8,128]{1,0:T(8,128)S(1)} %get-tuple-element.19), kind=kOutput, calls=%fused_computation.41 | convolution fusion | flops 138020352 | bytes 8790016 | tf_op jit(solution)/shard_map/rtk,kd->trd/dot_general | solution.py:57
  132.8 5.4 %collective-permute-start.10 = (f32[128,512]{0,1:T(8,128)S(1)}, f32[128,512]{0,1:T(8,128)}, u32[]{:S(2)}, u32[]{:S(2)}) collective-permute-start(f32[128,512]{0,1:T(8,128)S(1)} %slice_add_fusion.5), channel_id=1, source_target_pairs={{1,0},{2,1},{3,2},{4,3},{5,4},{6,5},{7,6},{8,7},{9,8},{10,9},{11,1... | collective-permute-start | bytes 786440 | tf_op jit(solution)/shard_map/ppermute | solution.py:15
  138.3 0.7 slice_add_fusion.2
  139.0 3.0 %collective-permute-start.13 = (f32[128,512]{0,1:T(8,128)}, f32[128,512]{0,1:T(8,128)}, u32[]{:S(2)}, u32[]{:S(2)}) collective-permute-start(f32[128,512]{0,1:T(8,128)} %slice_add_fusion.2), channel_id=1, source_target_pairs={{1,0},{2,1},{3,2},{4,3},{5,4},{6,5},{7,6},{8,7},{9,8},{10,9},{11,1... | collective-permute-start | bytes 786440 | tf_op jit(solution)/shard_map/ppermute | solution.py:15
  142.1 5.0 %convolution_convert_fusion.3 = bf16[128,8,128]{2,0,1:T(8,128)(2,1)} fusion(f32[512,128,8]{1,0,2:T(8,128)} %copy-done, bf16[512,512]{1,0:T(8,128)(2,1)} %copy-done.17, f32[8,128,512]{1,2,0:T(8,128)} %get-tuple-element.24, f32[8,128]{1,0:T(8,128)S(1)} %get-tuple-element.23), kind=kOutput, calls=%fused_computation.43 | convolution fusion | flops 138020352 | bytes 8790016 | tf_op jit(solution)/shard_map/rtk,kd->trd/dot_general | solution.py:57
  147.5 1.1 copy.62
  148.6 1.0 slice_add_fusion.4
  149.6 3.2 %collective-permute-start.11 = (f32[128,512]{0,1:T(8,128)S(1)}, f32[128,512]{0,1:T(8,128)S(1)}, u32[]{:S(2)}, u32[]{:S(2)}) collective-permute-start(f32[128,512]{0,1:T(8,128)S(1)} %slice_add_fusion.4), channel_id=1, source_target_pairs={{1,0},{2,1},{3,2},{4,3},{5,4},{6,5},{7,6},{8,7},{9,8},{10,9},{11,1... | collective-permute-start | bytes 786440 | tf_op jit(solution)/shard_map/ppermute | solution.py:15
  152.8 1.0 slice_add_fusion.1
  153.8 3.6 %collective-permute-start.14 = (f32[128,512]{0,1:T(8,128)S(1)}, f32[128,512]{0,1:T(8,128)}, u32[]{:S(2)}, u32[]{:S(2)}) collective-permute-start(f32[128,512]{0,1:T(8,128)S(1)} %slice_add_fusion.1), channel_id=1, source_target_pairs={{1,0},{2,1},{3,2},{4,3},{5,4},{6,5},{7,6},{8,7},{9,8},{10,9},{11,1... | collective-permute-start | bytes 786440 | tf_op jit(solution)/shard_map/ppermute | solution.py:15
  157.5 1.0 pad_maximum_fusion
  158.5 1.4 collective-permute-done.11
  160.0 0.8 copy.74
  160.8 4.7 %collective-permute-done.14 = f32[128,512]{0,1:T(8,128)} collective-permute-done((f32[128,512]{0,1:T(8,128)S(1)}, f32[128,512]{0,1:T(8,128)}, u32[]{:S(2)}, u32[]{:S(2)}) %collective-permute-start.14) | collective-permute-done | bytes 262176 | tf_op jit(solution)/shard_map/ppermute | solution.py:15
  165.4 1.0 fusion.44
  166.4 0.8 copy.75
  (66 shorter events, 0.9 us)
Async XLA Ops:
  0.6 33.8 %copy-start.1 = (bf16[128,4096]{1,0:T(8,128)(2,1)S(1)}, bf16[128,4096]{1,0:T(8,128)(2,1)}, u32[]{:S(2)}) copy-start(bf16[128,4096]{1,0:T(8,128)(2,1)} %param.8) | copy-start | bytes 3145732
  0.6 34.8 %collective-permute-start.5 = (s32[128]{0:T(128)}, s32[128]{0:T(128)}, u32[]{:S(2)}, u32[]{:S(2)}) collective-permute-start(s32[128]{0:T(128)} %param.9), channel_id=1, source_target_pairs={{0,1},{1,2},{2,3},{3,4},{4,5},{5,6},{6,7},{7,8},{8,9},{9,10},{10,1... | collective-permute-start | bytes 1544 | tf_op jit(solution)/shard_map/ppermute | solution.py:15
  4.8 33.2 %collective-permute-start.4 = (s32[128]{0:T(128)}, s32[128]{0:T(128)}, u32[]{:S(2)}, u32[]{:S(2)}) collective-permute-start(s32[128]{0:T(128)} %param.9), channel_id=1, source_target_pairs={{0,2},{1,3},{2,4},{3,5},{4,6},{5,7},{6,8},{7,9},{8,10},{9,11},{10,... | collective-permute-start | bytes 1544 | tf_op jit(solution)/shard_map/ppermute | solution.py:15
  10.6 31.1 %collective-permute-start.3 = (s32[128]{0:T(128)}, s32[128]{0:T(128)}, u32[]{:S(2)}, u32[]{:S(2)}) collective-permute-start(s32[128]{0:T(128)} %param.9), channel_id=1, source_target_pairs={{0,3},{1,4},{2,5},{3,6},{4,7},{5,8},{6,9},{7,10},{8,11},{9,12},{10... | collective-permute-start | bytes 1544 | tf_op jit(solution)/shard_map/ppermute | solution.py:15
  20.0 48.3 %collective-permute-start.1 = (bf16[128,512]{1,0:T(8,128)(2,1)}, bf16[128,512]{1,0:T(8,128)(2,1)}, u32[]{:S(2)}, u32[]{:S(2)}) collective-permute-start(bf16[128,512]{1,0:T(8,128)(2,1)} %param.6), channel_id=1, source_target_pairs={{0,2},{1,3},{2,4},{3,5},{4,6},{5,7},{6,8},{7,9},{8,10},{9,11},{10,... | collective-permute-start | bytes 393224 | tf_op jit(solution)/shard_map/ppermute | solution.py:15
  24.9 42.3 %collective-permute-start = (bf16[128,512]{1,0:T(8,128)(2,1)}, bf16[128,512]{1,0:T(8,128)(2,1)}, u32[]{:S(2)}, u32[]{:S(2)}) collective-permute-start(bf16[128,512]{1,0:T(8,128)(2,1)} %param.6), channel_id=1, source_target_pairs={{0,3},{1,4},{2,5},{3,6},{4,7},{5,8},{6,9},{7,10},{8,11},{9,12},{10... | collective-permute-start | bytes 393224 | tf_op jit(solution)/shard_map/ppermute | solution.py:15
  34.5 3.5 %copy-start.14 = (bf16[128,512]{1,0:T(8,128)(2,1)S(1)}, bf16[128,512]{1,0:T(8,128)(2,1)}, u32[]{:S(2)}) copy-start(bf16[128,512]{1,0:T(8,128)(2,1)} %param.7) | copy-start | bytes 393220
  34.5 10.1 %copy-start.18 = (s32[128]{0:T(128)S(1)}, s32[128]{0:T(128)}, u32[]{:S(2)}) copy-start(s32[128]{0:T(128)} %param.9) | copy-start | bytes 1540
  34.6 0.9 copy-start.15
  34.6 10.7 %copy-start.19 = (pred[512]{0:T(512)(128)(4,1)S(1)}, pred[512]{0:T(512)(128)(4,1)}, u32[]{:S(2)}) copy-start(pred[512]{0:T(512)(128)(4,1)} %broadcast_compare_fusion) | copy-start | bytes 1540
  35.5 33.8 %collective-permute-start.2 = (bf16[128,512]{1,0:T(8,128)(2,1)S(1)}, bf16[128,512]{1,0:T(8,128)(2,1)S(1)}, u32[]{:S(2)}, u32[]{:S(2)}) collective-permute-start(bf16[128,512]{1,0:T(8,128)(2,1)S(1)} %copy-done.15), channel_id=1, source_target_pairs={{0,1},{1,2},{2,3},{3,4},{4,5},{5,6},{6,7},{7,8},{8,9},{9,10},{10,1... | collective-permute-start | bytes 393224 | tf_op jit(solution)/shard_map/ppermute | solution.py:15
  38.0 18.0 %collective-permute-start.7 = (bf16[128,512]{1,0:T(8,128)(2,1)S(1)}, bf16[128,512]{1,0:T(8,128)(2,1)S(1)}, u32[]{:S(2)}, u32[]{:S(2)}) collective-permute-start(bf16[128,512]{1,0:T(8,128)(2,1)S(1)} %copy-done.14), channel_id=1, source_target_pairs={{0,2},{1,3},{2,4},{3,5},{4,6},{5,7},{6,8},{7,9},{8,10},{9,11},{10,... | collective-permute-start | bytes 393224 | tf_op jit(solution)/shard_map/ppermute | solution.py:15
  41.7 12.4 %collective-permute-start.6 = (bf16[128,512]{1,0:T(8,128)(2,1)S(1)}, bf16[128,512]{1,0:T(8,128)(2,1)S(1)}, u32[]{:S(2)}, u32[]{:S(2)}) collective-permute-start(bf16[128,512]{1,0:T(8,128)(2,1)S(1)} %copy-done.14), channel_id=1, source_target_pairs={{0,3},{1,4},{2,5},{3,6},{4,7},{5,8},{6,9},{7,10},{8,11},{9,12},{10... | collective-permute-start | bytes 393224 | tf_op jit(solution)/shard_map/ppermute | solution.py:15
  54.1 13.1 %collective-permute-start.8 = (bf16[128,512]{1,0:T(8,128)(2,1)S(1)}, bf16[128,512]{1,0:T(8,128)(2,1)S(1)}, u32[]{:S(2)}, u32[]{:S(2)}) collective-permute-start(bf16[128,512]{1,0:T(8,128)(2,1)S(1)} %copy-done.14), channel_id=1, source_target_pairs={{0,1},{1,2},{2,3},{3,4},{4,5},{5,6},{6,7},{7,8},{8,9},{9,10},{10,1... | collective-permute-start | bytes 393224 | tf_op jit(solution)/shard_map/ppermute | solution.py:15
  67.2 2.9 %copy-start.2 = (bf16[512,512]{1,0:T(8,128)(2,1)}, bf16[512,512]{1,0:T(8,128)(2,1)S(1)}, u32[]{:S(2)}) copy-start(bf16[512,512]{1,0:T(8,128)(2,1)S(1)} %constant_dynamic-update-slice_fusion.4) | copy-start | bytes 1572868
  69.3 0.8 copy-start.17
  70.5 3.1 %copy-start.16 = (pred[128,512]{0,1:T(8,128)(4,1)S(1)}, pred[128,512]{0,1:T(8,128)(4,1)}, u32[]{:S(2)}) copy-start(pred[128,512]{0,1:T(8,128)(4,1)} %compare_and_fusion) | copy-start | bytes 196612
  80.1 3.8 %copy-start.3 = (bf16[512,512]{1,0:T(8,128)(2,1)S(1)}, bf16[512,512]{1,0:T(8,128)(2,1)}, u32[]{:S(2)}) copy-start(bf16[512,512]{1,0:T(8,128)(2,1)} %copy-done.2) | copy-start | bytes 1572868
  97.8 2.2 %copy-start.5 = (bf16[128,1024]{0,1:T(8,128)(2,1)S(1)}, bf16[128,1024]{0,1:T(8,128)(2,1)}, u32[]{:S(2)}) copy-start(bf16[128,1024]{0,1:T(8,128)(2,1)} %copy.108) | copy-start | bytes 786436
  100.0 16.1 %copy-start = (f32[512,128,8]{1,0,2:T(8,128)}, f32[512,128,8]{1,0,2:T(8,128)S(1)}, u32[]{:S(2)}) copy-start(f32[512,128,8]{1,0,2:T(8,128)S(1)} %fusion.57) | copy-start | bytes 6291460
  100.0 3.3 %copy-start.6 = (bf16[128,1024]{0,1:T(8,128)(2,1)S(1)}, bf16[128,1024]{0,1:T(8,128)(2,1)}, u32[]{:S(2)}) copy-start(bf16[128,1024]{0,1:T(8,128)(2,1)} %copy.108) | copy-start | bytes 786436
  103.3 2.1 %copy-start.4 = (bf16[128,1024]{0,1:T(8,128)(2,1)S(1)}, bf16[128,1024]{0,1:T(8,128)(2,1)}, u32[]{:S(2)}) copy-start(bf16[128,1024]{0,1:T(8,128)(2,1)} %copy.104) | copy-start | bytes 786436
  116.1 4.0 %copy-start.11 = (f32[512,128]{0,1:T(8,128)S(1)}, f32[512,128]{0,1:T(8,128)}, u32[]{:S(2)}) copy-start(f32[512,128]{0,1:T(8,128)} %convolution_bitcast_fusion.4) | copy-start | bytes 786436
  116.1 4.0 %copy-start.12 = (f32[512,128]{0,1:T(8,128)S(1)}, f32[512,128]{0,1:T(8,128)}, u32[]{:S(2)}) copy-start(f32[512,128]{0,1:T(8,128)} %convolution_bitcast_fusion.6) | copy-start | bytes 786436
  120.1 5.6 %copy-start.9 = (f32[512,128]{0,1:T(8,128)S(1)}, f32[512,128]{0,1:T(8,128)}, u32[]{:S(2)}) copy-start(f32[512,128]{0,1:T(8,128)} %convolution_bitcast_fusion) | copy-start | bytes 786436
  120.1 5.6 %copy-start.10 = (f32[512,128]{0,1:T(8,128)S(1)}, f32[512,128]{0,1:T(8,128)}, u32[]{:S(2)}) copy-start(f32[512,128]{0,1:T(8,128)} %convolution_bitcast_fusion.2) | copy-start | bytes 786436
  120.1 5.6 %copy-start.13 = (f32[512,128]{0,1:T(8,128)S(1)}, f32[512,128]{0,1:T(8,128)}, u32[]{:S(2)}) copy-start(f32[512,128]{0,1:T(8,128)} %convolution_bitcast_fusion.3) | copy-start | bytes 786436
  121.3 11.5 %collective-permute-start.9 = (f32[128,512]{0,1:T(8,128)S(1)}, f32[128,512]{0,1:T(8,128)S(1)}, u32[]{:S(2)}, u32[]{:S(2)}) collective-permute-start(f32[128,512]{0,1:T(8,128)S(1)} %slice.104), channel_id=1, source_target_pairs={{1,0},{2,1},{3,2},{4,3},{5,4},{6,5},{7,6},{8,7},{9,8},{10,9},{11,1... | collective-permute-start | bytes 786440 | tf_op jit(solution)/shard_map/ppermute | solution.py:15
  126.6 11.7 %collective-permute-start.12 = (f32[128,512]{0,1:T(8,128)}, f32[128,512]{0,1:T(8,128)S(1)}, u32[]{:S(2)}, u32[]{:S(2)}) collective-permute-start(f32[128,512]{0,1:T(8,128)} %slice.108), channel_id=1, source_target_pairs={{1,0},{2,1},{3,2},{4,3},{5,4},{6,5},{7,6},{8,7},{9,8},{10,9},{11,1... | collective-permute-start | bytes 786440 | tf_op jit(solution)/shard_map/ppermute | solution.py:15
  132.8 15.8 %collective-permute-start.10 = (f32[128,512]{0,1:T(8,128)S(1)}, f32[128,512]{0,1:T(8,128)}, u32[]{:S(2)}, u32[]{:S(2)}) collective-permute-start(f32[128,512]{0,1:T(8,128)S(1)} %slice_add_fusion.5), channel_id=1, source_target_pairs={{1,0},{2,1},{3,2},{4,3},{5,4},{6,5},{7,6},{8,7},{9,8},{10,9},{11,1... | collective-permute-start | bytes 786440 | tf_op jit(solution)/shard_map/ppermute | solution.py:15
  139.0 8.0 %copy-start.7 = (bf16[128,8,128]{2,0,1:T(8,128)(2,1)S(1)}, bf16[128,8,128]{2,0,1:T(8,128)(2,1)}, u32[]{:S(2)}) copy-start(bf16[128,8,128]{2,0,1:T(8,128)(2,1)} %convolution_convert_fusion) | copy-start | bytes 786436
  139.0 8.2 %copy-start.8 = (bf16[128,8,128]{2,0,1:T(8,128)(2,1)S(1)}, bf16[128,8,128]{2,0,1:T(8,128)(2,1)}, u32[]{:S(2)}) copy-start(bf16[128,8,128]{2,0,1:T(8,128)(2,1)} %convolution_convert_fusion.2) | copy-start | bytes 786436
  139.0 13.8 %collective-permute-start.13 = (f32[128,512]{0,1:T(8,128)}, f32[128,512]{0,1:T(8,128)}, u32[]{:S(2)}, u32[]{:S(2)}) collective-permute-start(f32[128,512]{0,1:T(8,128)} %slice_add_fusion.2), channel_id=1, source_target_pairs={{1,0},{2,1},{3,2},{4,3},{5,4},{6,5},{7,6},{8,7},{9,8},{10,9},{11,1... | collective-permute-start | bytes 786440 | tf_op jit(solution)/shard_map/ppermute | solution.py:15
  149.6 10.3 %collective-permute-start.11 = (f32[128,512]{0,1:T(8,128)S(1)}, f32[128,512]{0,1:T(8,128)S(1)}, u32[]{:S(2)}, u32[]{:S(2)}) collective-permute-start(f32[128,512]{0,1:T(8,128)S(1)} %slice_add_fusion.4), channel_id=1, source_target_pairs={{1,0},{2,1},{3,2},{4,3},{5,4},{6,5},{7,6},{8,7},{9,8},{10,9},{11,1... | collective-permute-start | bytes 786440 | tf_op jit(solution)/shard_map/ppermute | solution.py:15
  153.8 11.6 %collective-permute-start.14 = (f32[128,512]{0,1:T(8,128)S(1)}, f32[128,512]{0,1:T(8,128)}, u32[]{:S(2)}, u32[]{:S(2)}) collective-permute-start(f32[128,512]{0,1:T(8,128)S(1)} %slice_add_fusion.1), channel_id=1, source_target_pairs={{1,0},{2,1},{3,2},{4,3},{5,4},{6,5},{7,6},{8,7},{9,8},{10,9},{11,1... | collective-permute-start | bytes 786440 | tf_op jit(solution)/shard_map/ppermute | solution.py:15
where the time goes:
time: 168 us; the launch traced here: 167 us
  starting transfers between devices  61.9 us (37%)
  matrix products  59.1 us (35%)
  waiting for transfers between devices  25.2 us (15%)
  local copies, waits for them, and re-layouts  11.5 us (7%)
  other arithmetic  8.23 us (5%)
    ppermute x15, starting transfers between devices, from_behind(): return lax.ppermute(block, axis, route)  61.9 us
    ppermute x15, waiting for transfers between devices, from_behind(): return lax.ppermute(block, axis, route)  25.2 us
    dot_general x4, matrix products, band_grads(): jnp.einsum('rtk,kd->trd', score_grad, k_head, preferred_element_type=jnp....  16.8 us
    dot_general x4, matrix products, band_grads(): jnp.einsum('rtk,trd->kd', score_grad, q_head, preferred_element_type=jnp....  16.4 us
    sub x4, matrix products, band_grads(): weights = jnp.exp(scores - row_max)  12.4 us
    dot_general x4, matrix products, band_grads(): jnp.einsum('rtk,trd->kd', probs_low, o_grad, preferred_element_type=jnp.f...  10.5 us
    unnamed x56, local copies, waits for them, and re-layouts  7.85 us
  transfers between devices with their start and end apart: 15, of which 4 were waited for; matrix products, arithmetic and copies ran while one was open for 15% of the time, Pallas kernels for 0%

commit v1 on v0

--- a/solution.py
+++ b/solution.py
@@ -73,40 +73,37 @@
 
 def body(query_rows, key_rows, value_matrix, out_grad, segments):
     tok_rows = query_rows.shape[0]
+    kv_width = key_rows.shape[1]
     position = lax.axis_index(("ctx", "fsdp"))
     query_first = position * tok_rows
     window = SPAN * tok_rows
-    nearby = [(key_rows, value_matrix, segments)]
+    pair = jnp.concatenate([key_rows, value_matrix], 1)
+    nearby = [(pair, segments)]
     for hop_back in range(1, SPAN + 1):
-        nearby.insert(0, from_behind((key_rows, value_matrix, segments), ("ctx", "fsdp"), hop_back))
-    key_win = jnp.concatenate([member[0] for member in nearby], 0)
-    value_win = jnp.concatenate([member[1] for member in nearby], 0)
-    seg_win = jnp.concatenate([member[2] for member in nearby], 0)
+        nearby.insert(0, from_behind(nearby[0], ("ctx", "fsdp"), 1))
+    pair_win = jnp.concatenate([member[0] for member in nearby], 0)
+    seg_win = jnp.concatenate([member[1] for member in nearby], 0)
     dq_part, dk_part, dv_part = band_grads(
         query_rows,
         out_grad,
-        key_win,
-        value_win,
+        pair_win[:, :kv_width],
+        pair_win[:, kv_width:],
         segments,
         seg_win,
         query_first,
         query_first - window,
         window,
     )
-    carried = (dk_part[:tok_rows], dv_part[:tok_rows])
+    grad_part = jnp.concatenate([dk_part, dv_part], 1)
+    carried = grad_part[:tok_rows]
     for relay_step in range(1, SPAN + 1):
-        received = from_behind((carried[0], carried[1]), ("ctx", "fsdp"), -1)
+        received = from_behind(carried.astype(jnp.bfloat16), ("ctx", "fsdp"), -1)
         lower = relay_step * tok_rows
-        carried = (
-            received[0] + dk_part[lower : lower + tok_rows],
-            received[1] + dv_part[lower : lower + tok_rows],
-        )
-    key_own = carried[0]
-    value_own = carried[1]
+        carried = received.astype(jnp.float32) + grad_part[lower : lower + tok_rows]
     return (
         dq_part.astype(jnp.bfloat16),
-        key_own.astype(jnp.bfloat16),
-        value_own.astype(jnp.bfloat16),
+        carried[:, :kv_width].astype(jnp.bfloat16),
+        carried[:, kv_width:].astype(jnp.bfloat16),
     )
 
 

time: 168 us -> 152 us (0.905)
  the two profiles are of different devices: /device:TPU:33 before, /device:TPU:56 now
where the time goes in v1:
time: 152 us; the launch traced here: 150 us
  matrix products  66.7 us (44%)
  waiting for transfers between devices  34.7 us (23%)
  starting transfers between devices  23.4 us (15%)
  local copies, waits for them, and re-layouts  16.4 us (11%)
  other arithmetic  7.62 us (5%)
    ppermute x9, waiting for transfers between devices, from_behind(): return lax.ppermute(block, axis, route)  34.7 us
    ppermute x9, starting transfers between devices, from_behind(): return lax.ppermute(block, axis, route)  23.4 us
    dot_general x4, matrix products, band_grads(): jnp.einsum('rtk,trd->kd', score_grad, q_head, preferred_element_type=jnp....  18.8 us
    dot_general x4, matrix products, band_grads(): jnp.einsum('rtk,kd->trd', score_grad, k_head, preferred_element_type=jnp....  18.6 us
    sub x4, matrix products, band_grads(): weights = jnp.exp(scores - row_max)  12.2 us
    dot_general x4, matrix products, band_grads(): jnp.einsum('rtk,trd->kd', probs_low, o_grad, preferred_element_type=jnp.f...  11.4 us
    unnamed x27, local copies, waits for them, and re-layouts  7.23 us
    reshape x4, local copies, waits for them, and re-layouts, band_grads(): query_parts.append(jnp.einsum('rtk,kd->trd', score_grad, k_head, preferre...  5.79 us
  transfers between devices with their start and end apart: 9, of which 5 were waited for; matrix products, arithmetic and copies ran while one was open for 23% of the time, Pallas kernels for 0%

profile of v1, /device:TPU:56, one launch (start us, length us, event | category | flops | bytes accessed | tf_op | source)
XLA Modules:
  0.0 149.8 jit_solution(12329312653231944700)
XLA Ops:
  0.6 4.4 %collective-permute-start.3 = (s32[128]{0:T(128)}, s32[128]{0:T(128)S(1)}, u32[]{:S(2)}, u32[]{:S(2)}) collective-permute-start(s32[128]{0:T(128)} %param.9), channel_id=1, source_target_pairs={{0,1},{1,2},{2,3},{3,4},{4,5},{5,6},{6,7},{7,8},{8,9},{9,10},{10,1... | collective-permute-start | bytes 1544 | tf_op jit(solution)/shard_map/ppermute | solution.py:15
  5.1 0.9 constant_dynamic-update-slice_fusion.1
  6.0 0.9 constant_dynamic-update-slice_fusion
  6.9 0.0 copy-start.4
  6.9 4.3 %collective-permute-start = (bf16[128,1024]{1,0:T(8,128)(2,1)S(1)}, bf16[128,1024]{1,0:T(8,128)(2,1)}, u32[]{:S(2)}, u32[]{:S(2)}) collective-permute-start(bf16[128,1024]{1,0:T(8,128)(2,1)S(1)} %constant_dynamic-update-slice_fusion), channel_id=1, source_target_pairs={{0,1},{1,2},{2,3},{3,4},{4,5},{5,6},{6,7},{7,8},{8,9},{9,10},{10,1... | collective-permute-start | bytes 786440 | tf_op jit(solution)/shard_map/ppermute | solution.py:15
  11.2 1.3 fusion.95
  12.5 0.1 fusion.96
  12.6 13.1 %collective-permute-done = bf16[128,1024]{1,0:T(8,128)(2,1)} collective-permute-done((bf16[128,1024]{1,0:T(8,128)(2,1)S(1)}, bf16[128,1024]{1,0:T(8,128)(2,1)}, u32[]{:S(2)}, u32[]{:S(2)}) %collective-permute-start) | collective-permute-done | bytes 262176 | tf_op jit(solution)/shard_map/ppermute | solution.py:15
  25.7 1.9 %collective-permute-start.1 = (bf16[128,1024]{1,0:T(8,128)(2,1)}, bf16[128,1024]{1,0:T(8,128)(2,1)S(1)}, u32[]{:S(2)}, u32[]{:S(2)}) collective-permute-start(bf16[128,1024]{1,0:T(8,128)(2,1)} %collective-permute-done), channel_id=1, source_target_pairs={{0,1},{1,2},{2,3},{3,4},{4,5},{5,6},{6,7},{7,8},{8,9},{9,10},{10,1... | collective-permute-start | bytes 786440 | tf_op jit(solution)/shard_map/ppermute | solution.py:15
  27.7 1.9 %collective-permute-start.4 = (s32[128]{0:T(128)S(1)}, s32[128]{0:T(128)S(1)}, u32[]{:S(2)}, u32[]{:S(2)}) collective-permute-start(s32[128]{0:T(128)S(1)} %collective-permute-done.3), channel_id=1, source_target_pairs={{0,1},{1,2},{2,3},{3,4},{4,5},{5,6},{6,7},{7,8},{8,9},{9,10},{10,1... | collective-permute-start | bytes 1544 | tf_op jit(solution)/shard_map/ppermute | solution.py:15
  29.6 0.0 copy-start.7
  29.6 0.9 copy.104
  30.5 0.8 copy.108
  31.3 0.8 copy.106
  32.2 0.8 copy.110
  33.0 4.9 %collective-permute-done.4 = s32[128]{0:T(128)S(1)} collective-permute-done((s32[128]{0:T(128)S(1)}, s32[128]{0:T(128)S(1)}, u32[]{:S(2)}, u32[]{:S(2)}) %collective-permute-start.4) | collective-permute-done | bytes 544 | tf_op jit(solution)/shard_map/ppermute | solution.py:15
  37.9 1.9 %collective-permute-start.5 = (s32[128]{0:T(128)S(1)}, s32[128]{0:T(128)S(1)}, u32[]{:S(2)}, u32[]{:S(2)}) collective-permute-start(s32[128]{0:T(128)S(1)} %collective-permute-done.4), channel_id=1, source_target_pairs={{0,1},{1,2},{2,3},{3,4},{4,5},{5,6},{6,7},{7,8},{8,9},{9,10},{10,1... | collective-permute-start | bytes 1544 | tf_op jit(solution)/shard_map/ppermute | solution.py:15
  39.8 0.9 copy.105
  40.7 0.2 copy.109
  40.8 0.2 copy.107
  41.0 0.2 copy.111
  41.2 0.0 collective-permute-done.1
  41.2 1.9 %collective-permute-start.2 = (bf16[128,1024]{1,0:T(8,128)(2,1)S(1)}, bf16[128,1024]{1,0:T(8,128)(2,1)S(1)}, u32[]{:S(2)}, u32[]{:S(2)}) collective-permute-start(bf16[128,1024]{1,0:T(8,128)(2,1)S(1)} %collective-permute-done.1), channel_id=1, source_target_pairs={{0,1},{1,2},{2,3},{3,4},{4,5},{5,6},{6,7},{7,8},{8,9},{9,10},{10,1... | collective-permute-start | bytes 786440 | tf_op jit(solution)/shard_map/ppermute | solution.py:15
  43.1 3.8 %collective-permute-done.5 = s32[128]{0:T(128)S(1)} collective-permute-done((s32[128]{0:T(128)S(1)}, s32[128]{0:T(128)S(1)}, u32[]{:S(2)}, u32[]{:S(2)}) %collective-permute-start.5) | collective-permute-done | bytes 544 | tf_op jit(solution)/shard_map/ppermute | solution.py:15
  47.0 0.3 compare_and_fusion
  47.3 5.9 %collective-permute-done.2 = bf16[128,1024]{1,0:T(8,128)(2,1)S(1)} collective-permute-done((bf16[128,1024]{1,0:T(8,128)(2,1)S(1)}, bf16[128,1024]{1,0:T(8,128)(2,1)S(1)}, u32[]{:S(2)}, u32[]{:S(2)}) %collective-permute-start.2) | collective-permute-done | bytes 262176 | tf_op jit(solution)/shard_map/ppermute | solution.py:15
  53.1 1.1 pad_maximum_fusion
  54.2 1.8 %fusion.63 = f32[512,128,8]{1,0,2:T(8,128)} fusion(bf16[128,8,128]{0,2,1:T(8,128)(2,1)S(1)} %bitcast.266, bf16[512,1024]{1,0:T(8,128)(2,1)S(1)} %pad_maximum_fusion), kind=kOutput, calls=%fused_computation.99 | convolution fusion | flops 134217728 | bytes 2490368 | tf_op jit(solution)/shard_map/trd,kd->rtk/dot_general | solution.py:52
  56.1 1.8 %fusion.65 = f32[512,128,8]{1,0,2:T(8,128)} fusion(bf16[128,8,128]{0,2,1:T(8,128)(2,1)S(1)} %bitcast.270, bf16[512,1024]{1,0:T(8,128)(2,1)S(1)} %pad_maximum_fusion), kind=kOutput, calls=%fused_computation.105 | convolution fusion | flops 134217728 | bytes 2490368 | tf_op jit(solution)/shard_map/trd,kd->rtk/dot_general | solution.py:52
  57.8 1.7 %fusion.64 = f32[512,128,8]{1,0,2:T(8,128)} fusion(bf16[128,8,128]{0,2,1:T(8,128)(2,1)S(1)} %bitcast.264, bf16[512,1024]{1,0:T(8,128)(2,1)S(1)} %pad_maximum_fusion), kind=kOutput, calls=%fused_computation.102 | convolution fusion | flops 134217728 | bytes 2490368 | tf_op jit(solution)/shard_map/trd,kd->rtk/dot_general | solution.py:52
  59.5 0.4 fusion.66
  60.0 3.1 %fusion.98 = (f32[8,128]{1,0:T(8,128)S(1)}, f32[8,128,512]{1,2,0:T(8,128)}) fusion(pred[128,512]{0,1:T(8,128)(4,1)S(1)} %compare_and_fusion, bf16[128,8,128]{0,2,1:T(8,128)(2,1)} %bitcast.275, bf16[512,1024]{1,0:T(8,128)(2,1)S(1)} %pad_maximum_fusion), kind=kOutput, calls=%fused_computation.148 | convolution fusion | flops 136315392 | bytes 2560000 | tf_op jit(solution)/shard_map/sub | solution.py:50
  63.0 3.0 %fusion.100 = (f32[8,128]{1,0:T(8,128)S(1)}, f32[8,128,512]{1,2,0:T(8,128)}) fusion(pred[128,512]{0,1:T(8,128)(4,1)S(1)} %compare_and_fusion, bf16[128,8,128]{0,2,1:T(8,128)(2,1)} %bitcast.281, bf16[512,1024]{1,0:T(8,128)(2,1)S(1)} %pad_maximum_fusion), kind=kOutput, calls=%fused_computation.150 | convolution fusion | flops 136315392 | bytes 2560000 | tf_op jit(solution)/shard_map/sub | solution.py:50
  66.1 3.0 %fusion.99 = (f32[8,128]{1,0:T(8,128)S(1)}, f32[8,128,512]{1,2,0:T(8,128)}) fusion(pred[128,512]{0,1:T(8,128)(4,1)S(1)} %compare_and_fusion, bf16[128,8,128]{0,2,1:T(8,128)(2,1)} %bitcast.272, bf16[512,1024]{1,0:T(8,128)(2,1)S(1)} %pad_maximum_fusion), kind=kOutput, calls=%fused_computation.149 | convolution fusion | flops 136315392 | bytes 2560000 | tf_op jit(solution)/shard_map/sub | solution.py:50
  69.1 3.1 %fusion.101 = (f32[8,128]{1,0:T(8,128)S(1)}, f32[8,128,512]{1,2,0:T(8,128)}) fusion(pred[128,512]{0,1:T(8,128)(4,1)S(1)} %compare_and_fusion, bf16[128,8,128]{0,2,1:T(8,128)(2,1)} %bitcast.278, bf16[512,1024]{1,0:T(8,128)(2,1)S(1)} %pad_maximum_fusion), kind=kOutput, calls=%fused_computation.151 | convolution fusion | flops 136315392 | bytes 2560000 | tf_op jit(solution)/shard_map/sub | solution.py:50
  72.2 3.7 %fusion.31 = f32[512,1024]{0,1:T(8,128)} fusion(bf16[128,8,128]{0,2,1:T(8,128)(2,1)} %bitcast.279, f32[512,128,8]{1,0,2:T(8,128)S(1)} %fusion.66, f32[8,128,512]{1,2,0:T(8,128)} %get-tuple-element.26, f32[8,128]{1,0:T(8,128)S(1)} %get-tuple-element.25), kind=kOutput, calls=%fused_computation.59 | convolution fusion | flops 137889280 | bytes 8921088 | tf_op jit(solution)/shard_map/rtk,trd->kd/dot_general | solution.py:62
  75.9 5.1 %fusion.30 = f32[512,1024]{0,1:T(8,128)} fusion(f32[512,1024]{0,1:T(8,128)} %fusion.31, bf16[128,8,128]{0,2,1:T(8,128)(2,1)} %bitcast.282, f32[512,128,8]{1,0,2:T(8,128)} %fusion.65, f32[8,128,512]{1,2,0:T(8,128)} %get-tuple-element.24, f32[8,128]{1,0:T(8,128)S(1)} %get-tuple-element.23), kind=kOutput, calls=%fused_computation.57 | convolution fusion | flops 137889280 | bytes 8921088 | tf_op jit(solution)/shard_map/rtk,trd->kd/dot_general | solution.py:62
  81.0 5.1 %fusion.29 = f32[512,1024]{0,1:T(8,128)} fusion(f32[512,1024]{0,1:T(8,128)} %fusion.30, bf16[128,8,128]{0,2,1:T(8,128)(2,1)} %bitcast.273, f32[512,128,8]{1,0,2:T(8,128)} %fusion.64, f32[8,128,512]{1,2,0:T(8,128)} %get-tuple-element.22, f32[8,128]{1,0:T(8,128)S(1)} %get-tuple-element.21), kind=kOutput, calls=%fused_computation.55 | convolution fusion | flops 137889280 | bytes 8921088 | tf_op jit(solution)/shard_map/rtk,trd->kd/dot_general | solution.py:62
  86.0 4.9 %fusion.28 = f32[512,1024]{0,1:T(8,128)} fusion(f32[512,1024]{0,1:T(8,128)} %fusion.29, bf16[128,8,128]{0,2,1:T(8,128)(2,1)} %bitcast.276, f32[512,128,8]{1,0,2:T(8,128)} %fusion.63, f32[8,128,512]{1,2,0:T(8,128)} %get-tuple-element.20, f32[8,128]{1,0:T(8,128)S(1)} %get-tuple-element.19), kind=kOutput, calls=%fused_computation.53 | convolution fusion | flops 137889280 | bytes 8921088 | tf_op jit(solution)/shard_map/rtk,trd->kd/dot_general | solution.py:62
  91.0 2.9 %fusion.27 = f32[512,1024]{0,1:T(8,128)} fusion(f32[512,1024]{0,1:T(8,128)} %fusion.28, bf16[128,8,128]{0,2,1:T(8,128)(2,1)} %bitcast.268, f32[8,128]{1,0:T(8,128)S(1)} %get-tuple-element.25, pred[128,512]{0,1:T(8,128)(4,1)S(1)} %compare_and_fusion, bf16[128,8,128]{0,2,1:T(8,128)(2,1)} %bitcast.280, bf16[512,1024]{1,0:T(8,128)(2,1)S(1)} %pad_maximum_fusion), kind=kOutput, calls=%fused_computation.51 | convolution fusion | flops 271058432 | bytes 987136 | tf_op jit(solution)/shard_map/rtk,trd->kd/dot_general | solution.py:65
  93.8 2.9 %fusion.26 = f32[512,1024]{0,1:T(8,128)} fusion(f32[512,1024]{0,1:T(8,128)} %fusion.27, bf16[128,8,128]{0,2,1:T(8,128)(2,1)} %bitcast.271, f32[8,128]{1,0:T(8,128)S(1)} %get-tuple-element.23, pred[128,512]{0,1:T(8,128)(4,1)S(1)} %compare_and_fusion, bf16[128,8,128]{0,2,1:T(8,128)(2,1)} %bitcast.283, bf16[512,1024]{1,0:T(8,128)(2,1)S(1)} %pad_maximum_fusion), kind=kOutput, calls=%fused_computation.49 | convolution fusion | flops 271058432 | bytes 987136 | tf_op jit(solution)/shard_map/rtk,trd->kd/dot_general | solution.py:65
  96.7 2.8 %fusion.25 = f32[512,1024]{0,1:T(8,128)} fusion(f32[512,1024]{0,1:T(8,128)} %fusion.26, bf16[128,8,128]{0,2,1:T(8,128)(2,1)S(1)} %bitcast.265, f32[8,128]{1,0:T(8,128)S(1)} %get-tuple-element.21, pred[128,512]{0,1:T(8,128)(4,1)S(1)} %compare_and_fusion, bf16[128,8,128]{0,2,1:T(8,128)(2,1)} %bitcast.274, bf16[512,1024]{1,0:T(8,128)(2,1)S(1)} %pad_maximum_fusion), kind=kOutput, calls=%fused_computation.47 | convolution fusion | flops 271058432 | bytes 987136 | tf_op jit(solution)/shard_map/rtk,trd->kd/dot_general | solution.py:65
  99.5 2.9 %fusion.24 = f32[512,1024]{0,1:T(8,128)} fusion(f32[512,1024]{0,1:T(8,128)} %fusion.25, bf16[128,8,128]{0,2,1:T(8,128)(2,1)} %bitcast.267, f32[8,128]{1,0:T(8,128)S(1)} %get-tuple-element.19, pred[128,512]{0,1:T(8,128)(4,1)S(1)} %compare_and_fusion, bf16[128,8,128]{0,2,1:T(8,128)(2,1)} %bitcast.277, bf16[512,1024]{1,0:T(8,128)(2,1)S(1)} %pad_maximum_fusion), kind=kOutput, calls=%fused_computation.45 | convolution fusion | flops 271058432 | bytes 987136 | tf_op jit(solution)/shard_map/rtk,trd->kd/dot_general | solution.py:65
  102.4 1.1 slice.177
  103.5 3.3 %collective-permute-start.6 = (bf16[128,1024]{0,1:T(8,128)(2,1)S(1)}, bf16[128,1024]{0,1:T(8,128)(2,1)}, u32[]{:S(2)}, u32[]{:S(2)}) collective-permute-start(bf16[128,1024]{0,1:T(8,128)(2,1)S(1)} %slice.177), channel_id=1, source_target_pairs={{1,0},{2,1},{3,2},{4,3},{5,4},{6,5},{7,6},{8,7},{9,8},{10,9},{11,1... | collective-permute-start | bytes 786440 | tf_op jit(solution)/shard_map/ppermute | solution.py:15
  106.7 4.9 %convolution_convert_fusion = bf16[128,8,128]{2,0,1:T(8,128)(2,1)} fusion(f32[512,128,8]{1,0,2:T(8,128)} %fusion.63, bf16[512,1024]{1,0:T(8,128)(2,1)S(1)} %pad_maximum_fusion, f32[8,128,512]{1,2,0:T(8,128)} %get-tuple-element.20, f32[8,128]{1,0:T(8,128)S(1)} %get-tuple-element.19), kind=kOutput, calls=%fused_computation.40 | convolution fusion | flops 138020352 | bytes 8790016 | tf_op jit(solution)/shard_map/rtk,kd->trd/dot_general | solution.py:57
  111.7 4.9 %convolution_convert_fusion.2 = bf16[128,8,128]{2,0,1:T(8,128)(2,1)} fusion(f32[512,128,8]{1,0,2:T(8,128)} %fusion.65, bf16[512,1024]{1,0:T(8,128)(2,1)S(1)} %pad_maximum_fusion, f32[8,128,512]{1,2,0:T(8,128)} %get-tuple-element.24, f32[8,128]{1,0:T(8,128)S(1)} %get-tuple-element.23), kind=kOutput, calls=%fused_computation.42 | convolution fusion | flops 138020352 | bytes 8790016 | tf_op jit(solution)/shard_map/rtk,kd->trd/dot_general | solution.py:57
  116.6 0.0 collective-permute-done.6
  116.6 1.9 %fusion.54 = bf16[128,1024]{0,1:T(8,128)(2,1)} fusion(f32[512,1024]{0,1:T(8,128)} %fusion.24, bf16[128,1024]{0,1:T(8,128)(2,1)} %collective-permute-done.6), kind=kLoop, calls=%fused_computation.91 | loop fusion | flops 393216 | bytes 1048576 | tf_op jit(solution)/shard_map/convert_element_type | solution.py:100
  118.5 1.9 %collective-permute-start.7 = (bf16[128,1024]{0,1:T(8,128)(2,1)}, bf16[128,1024]{0,1:T(8,128)(2,1)}, u32[]{:S(2)}, u32[]{:S(2)}) collective-permute-start(bf16[128,1024]{0,1:T(8,128)(2,1)} %fusion.54), channel_id=1, source_target_pairs={{1,0},{2,1},{3,2},{4,3},{5,4},{6,5},{7,6},{8,7},{9,8},{10,9},{11,1... | collective-permute-start | bytes 786440 | tf_op jit(solution)/shard_map/ppermute | solution.py:15
  120.4 5.0 %convolution_convert_fusion.1 = bf16[128,8,128]{2,0,1:T(8,128)(2,1)} fusion(f32[512,128,8]{1,0,2:T(8,128)} %fusion.64, bf16[512,1024]{1,0:T(8,128)(2,1)S(1)} %pad_maximum_fusion, f32[8,128,512]{1,2,0:T(8,128)} %get-tuple-element.22, f32[8,128]{1,0:T(8,128)S(1)} %get-tuple-element.21), kind=kOutput, calls=%fused_computation.41 | convolution fusion | flops 138020352 | bytes 8790016 | tf_op jit(solution)/shard_map/rtk,kd->trd/dot_general | solution.py:57
  125.4 1.1 copy.65
  126.5 1.8 %copy.63 = bf16[128,1024]{1,0:T(8,128)(2,1)} copy(bf16[128,1024]{0,1:T(8,128)(2,1)} %bitcast.285) | data formatting | bytes 524288 | tf_op jit(solution)/shard_map/reshape | solution.py:59
  128.3 1.8 %copy.64 = bf16[128,1024]{1,0:T(8,128)(2,1)} copy(bf16[128,1024]{0,1:T(8,128)(2,1)} %bitcast.286) | data formatting | bytes 524288 | tf_op jit(solution)/shard_map/reshape | solution.py:59
  130.1 3.7 %convolution_convert_fusion.3 = bf16[128,8,128]{2,0,1:T(8,128)(2,1)} fusion(f32[512,128,8]{1,0,2:T(8,128)S(1)} %fusion.66, bf16[512,1024]{1,0:T(8,128)(2,1)S(1)} %pad_maximum_fusion, f32[8,128,512]{1,2,0:T(8,128)} %get-tuple-element.26, f32[8,128]{1,0:T(8,128)S(1)} %get-tuple-element.25), kind=kOutput, calls=%fused_computation.43 | convolution fusion | flops 138020352 | bytes 8790016 | tf_op jit(solution)/shard_map/rtk,kd->trd/dot_general | solution.py:57
  133.8 1.1 copy.62
  134.9 0.0 collective-permute-done.7
  134.9 1.2 fusion.53
  136.1 1.9 %collective-permute-start.8 = (bf16[128,1024]{0,1:T(8,128)(2,1)S(1)}, bf16[128,1024]{0,1:T(8,128)(2,1)S(1)}, u32[]{:S(2)}, u32[]{:S(2)}) collective-permute-start(bf16[128,1024]{0,1:T(8,128)(2,1)S(1)} %fusion.53), channel_id=1, source_target_pairs={{1,0},{2,1},{3,2},{4,3},{5,4},{6,5},{7,6},{8,7},{9,8},{10,9},{11,1... | collective-permute-start | bytes 786440 | tf_op jit(solution)/shard_map/ppermute | solution.py:15
  138.0 2.1 %pad_maximum_fusion.1 = bf16[128,4096]{1,0:T(8,128)(2,1)} fusion(bf16[128,1024]{1,0:T(8,128)(2,1)S(1)} %copy.65, bf16[128,1024]{1,0:T(8,128)(2,1)} %copy.64, bf16[128,1024]{1,0:T(8,128)(2,1)} %copy.63, bf16[128,1024]{1,0:T(8,128)(2,1)S(1)} %copy.62), kind=kLoop, calls=%fused_computation.61 | loop fusion | flops 4194304 | bytes 2097152 | tf_op jit(solution)/shard_map/concatenate | solution.py:68
  140.1 7.1 %collective-permute-done.8 = bf16[128,1024]{0,1:T(8,128)(2,1)S(1)} collective-permute-done((bf16[128,1024]{0,1:T(8,128)(2,1)S(1)}, bf16[128,1024]{0,1:T(8,128)(2,1)S(1)}, u32[]{:S(2)}, u32[]{:S(2)}) %collective-permute-start.8) | collective-permute-done | bytes 262176 | tf_op jit(solution)/shard_map/ppermute | solution.py:15
  147.2 1.1 fusion.52
  148.3 0.8 copy.75
  149.1 0.8 copy.74
  (20 shorter events, 0.1 us)
Async XLA Ops:
  0.6 11.9 %copy-start.3 = (bf16[128,4096]{1,0:T(8,128)(2,1)S(1)}, bf16[128,4096]{1,0:T(8,128)(2,1)}, u32[]{:S(2)}) copy-start(bf16[128,4096]{1,0:T(8,128)(2,1)} %param.8) | copy-start | bytes 3145732
  0.6 27.0 %collective-permute-start.3 = (s32[128]{0:T(128)}, s32[128]{0:T(128)S(1)}, u32[]{:S(2)}, u32[]{:S(2)}) collective-permute-start(s32[128]{0:T(128)} %param.9), channel_id=1, source_target_pairs={{0,1},{1,2},{2,3},{3,4},{4,5},{5,6},{6,7},{7,8},{8,9},{9,10},{10,1... | collective-permute-start | bytes 1544 | tf_op jit(solution)/shard_map/ppermute | solution.py:15
  6.9 5.7 %copy-start.4 = (bf16[128,1024]{1,0:T(8,128)(2,1)}, bf16[128,1024]{1,0:T(8,128)(2,1)S(1)}, u32[]{:S(2)}) copy-start(bf16[128,1024]{1,0:T(8,128)(2,1)S(1)} %constant_dynamic-update-slice_fusion) | copy-start | bytes 786436
  6.9 18.8 %collective-permute-start = (bf16[128,1024]{1,0:T(8,128)(2,1)S(1)}, bf16[128,1024]{1,0:T(8,128)(2,1)}, u32[]{:S(2)}, u32[]{:S(2)}) collective-permute-start(bf16[128,1024]{1,0:T(8,128)(2,1)S(1)} %constant_dynamic-update-slice_fusion), channel_id=1, source_target_pairs={{0,1},{1,2},{2,3},{3,4},{4,5},{5,6},{6,7},{7,8},{8,9},{9,10},{10,1... | collective-permute-start | bytes 786440 | tf_op jit(solution)/shard_map/ppermute | solution.py:15
  25.7 15.5 %collective-permute-start.1 = (bf16[128,1024]{1,0:T(8,128)(2,1)}, bf16[128,1024]{1,0:T(8,128)(2,1)S(1)}, u32[]{:S(2)}, u32[]{:S(2)}) collective-permute-start(bf16[128,1024]{1,0:T(8,128)(2,1)} %collective-permute-done), channel_id=1, source_target_pairs={{0,1},{1,2},{2,3},{3,4},{4,5},{5,6},{6,7},{7,8},{8,9},{9,10},{10,1... | collective-permute-start | bytes 786440 | tf_op jit(solution)/shard_map/ppermute | solution.py:15
  27.7 10.2 %collective-permute-start.4 = (s32[128]{0:T(128)S(1)}, s32[128]{0:T(128)S(1)}, u32[]{:S(2)}, u32[]{:S(2)}) collective-permute-start(s32[128]{0:T(128)S(1)} %collective-permute-done.3), channel_id=1, source_target_pairs={{0,1},{1,2},{2,3},{3,4},{4,5},{5,6},{6,7},{7,8},{8,9},{9,10},{10,1... | collective-permute-start | bytes 1544 | tf_op jit(solution)/shard_map/ppermute | solution.py:15
  29.6 17.3 %copy-start.7 = (s32[128]{0:T(128)S(1)}, s32[128]{0:T(128)}, u32[]{:S(2)}) copy-start(s32[128]{0:T(128)} %param.9) | copy-start | bytes 1540
  30.5 22.7 %copy-start.5 = (bf16[128,1024]{1,0:T(8,128)(2,1)S(1)}, bf16[128,1024]{1,0:T(8,128)(2,1)}, u32[]{:S(2)}) copy-start(bf16[128,1024]{1,0:T(8,128)(2,1)} %copy-done.4) | copy-start | bytes 786436
  37.9 9.1 %collective-permute-start.5 = (s32[128]{0:T(128)S(1)}, s32[128]{0:T(128)S(1)}, u32[]{:S(2)}, u32[]{:S(2)}) collective-permute-start(s32[128]{0:T(128)S(1)} %collective-permute-done.4), channel_id=1, source_target_pairs={{0,1},{1,2},{2,3},{3,4},{4,5},{5,6},{6,7},{7,8},{8,9},{9,10},{10,1... | collective-permute-start | bytes 1544 | tf_op jit(solution)/shard_map/ppermute | solution.py:15
  41.0 15.1 %copy-start.2 = (bf16[128,1024]{0,1:T(8,128)(2,1)}, bf16[128,1024]{0,1:T(8,128)(2,1)S(1)}, u32[]{:S(2)}) copy-start(bf16[128,1024]{0,1:T(8,128)(2,1)S(1)} %copy.107) | copy-start | bytes 786436
  41.2 14.9 %copy-start = (bf16[128,1024]{0,1:T(8,128)(2,1)}, bf16[128,1024]{0,1:T(8,128)(2,1)S(1)}, u32[]{:S(2)}) copy-start(bf16[128,1024]{0,1:T(8,128)(2,1)S(1)} %copy.111) | copy-start | bytes 786436
  41.2 6.0 %copy-start.6 = (bf16[128,1024]{1,0:T(8,128)(2,1)}, bf16[128,1024]{1,0:T(8,128)(2,1)S(1)}, u32[]{:S(2)}) copy-start(bf16[128,1024]{1,0:T(8,128)(2,1)S(1)} %collective-permute-done.1) | copy-start | bytes 786436
  41.2 11.9 %collective-permute-start.2 = (bf16[128,1024]{1,0:T(8,128)(2,1)S(1)}, bf16[128,1024]{1,0:T(8,128)(2,1)S(1)}, u32[]{:S(2)}, u32[]{:S(2)}) collective-permute-start(bf16[128,1024]{1,0:T(8,128)(2,1)S(1)} %collective-permute-done.1), channel_id=1, source_target_pairs={{0,1},{1,2},{2,3},{3,4},{4,5},{5,6},{6,7},{7,8},{8,9},{9,10},{10,1... | collective-permute-start | bytes 786440 | tf_op jit(solution)/shard_map/ppermute | solution.py:15
  56.1 3.5 %copy-start.1 = (bf16[128,1024]{0,1:T(8,128)(2,1)S(1)}, bf16[128,1024]{0,1:T(8,128)(2,1)}, u32[]{:S(2)}) copy-start(bf16[128,1024]{0,1:T(8,128)(2,1)} %copy.105) | copy-start | bytes 786436
  103.5 13.2 %collective-permute-start.6 = (bf16[128,1024]{0,1:T(8,128)(2,1)S(1)}, bf16[128,1024]{0,1:T(8,128)(2,1)}, u32[]{:S(2)}, u32[]{:S(2)}) collective-permute-start(bf16[128,1024]{0,1:T(8,128)(2,1)S(1)} %slice.177), channel_id=1, source_target_pairs={{1,0},{2,1},{3,2},{4,3},{5,4},{6,5},{7,6},{8,7},{9,8},{10,9},{11,1... | collective-permute-start | bytes 786440 | tf_op jit(solution)/shard_map/ppermute | solution.py:15
  118.5 16.4 %collective-permute-start.7 = (bf16[128,1024]{0,1:T(8,128)(2,1)}, bf16[128,1024]{0,1:T(8,128)(2,1)}, u32[]{:S(2)}, u32[]{:S(2)}) collective-permute-start(bf16[128,1024]{0,1:T(8,128)(2,1)} %fusion.54), channel_id=1, source_target_pairs={{1,0},{2,1},{3,2},{4,3},{5,4},{6,5},{7,6},{8,7},{9,8},{10,9},{11,1... | collective-permute-start | bytes 786440 | tf_op jit(solution)/shard_map/ppermute | solution.py:15
  136.1 11.1 %collective-permute-start.8 = (bf16[128,1024]{0,1:T(8,128)(2,1)S(1)}, bf16[128,1024]{0,1:T(8,128)(2,1)S(1)}, u32[]{:S(2)}, u32[]{:S(2)}) collective-permute-start(bf16[128,1024]{0,1:T(8,128)(2,1)S(1)} %fusion.53), channel_id=1, source_target_pairs={{1,0},{2,1},{3,2},{4,3},{5,4},{6,5},{7,6},{8,7},{9,8},{10,9},{11,1... | collective-permute-start | bytes 786440 | tf_op jit(solution)/shard_map/ppermute | solution.py:15

commit v2 on v1

v2 whole, which is shorter than its diff:
```python
import math

import jax
import jax.numpy as jnp
from jax import lax
from jax.experimental import pallas as pl
from jax.sharding import PartitionSpec as P

HEAD_WIDTH = 128
SPAN = 3


def from_behind(block, axis, distance):
    devices = range(lax.axis_size(axis))
    route = [(i - distance, i) for i in devices if i - distance in devices]
    return lax.ppermute(block, axis, route)


def band_kernel(seg_q_ref, seg_k_ref, query_ref, grad_ref, pair_ref, dq_ref, dpair_ref):
    tok_rows = query_ref.shape[0]
    key_count = pair_ref.shape[0]
    heads_per_group = query_ref.shape[1] // HEAD_WIDTH
    inv_root = 1.0 / math.sqrt(HEAD_WIDTH)
    row = lax.broadcasted_iota(jnp.int32, (tok_rows, key_count), 0)
    col = lax.broadcasted_iota(jnp.int32, (tok_rows, key_count), 1)
    window = key_count - tok_rows
    allowed = (col > row) & (col <= row + window) & (seg_k_ref[...] == seg_q_ref[...])
    k_head = pair_ref[:, :HEAD_WIDTH]
    v_head = pair_ref[:, HEAD_WIDTH:]
    key_acc = jnp.zeros((key_count, HEAD_WIDTH), jnp.float32)
    value_acc = jnp.zeros((key_count, HEAD_WIDTH), jnp.float32)
    for head in range(heads_per_group):
        cols = slice(head * HEAD_WIDTH, (head + 1) * HEAD_WIDTH)
        q_head = query_ref[:, cols]
        o_grad = grad_ref[:, cols]
        scores = lax.dot_general(
            q_head, k_head, (((1,), (1,)), ((), ())), preferred_element_type=jnp.float32
        )
        scores = jnp.where(allowed, scores * inv_root, -1e30)
        row_max = jnp.max(scores, axis=1, keepdims=True)
        weights = jnp.exp(scores - row_max)
        probs = weights * (1.0 / jnp.sum(weights, axis=1, keepdims=True))
        prob_grad = lax.dot_general(
            o_grad, v_head, (((1,), (1,)), ((), ())), preferred_element_type=jnp.float32
        )
        row_delta = jnp.sum(probs * prob_grad, axis=1, keepdims=True)
        score_grad = (probs * (prob_grad - row_delta) * inv_root).astype(jnp.bfloat16)
        probs_low = probs.astype(jnp.bfloat16)
        dq_ref[:, cols] = jnp.dot(
            score_grad, k_head, preferred_element_type=jnp.float32
        ).astype(jnp.bfloat16)
        key_acc = key_acc + lax.dot_general(
            score_grad, q_head, (((0,), (0,)), ((), ())), preferred_element_type=jnp.float32
        )
        value_acc = value_acc + lax.dot_general(
            probs_low, o_grad, (((0,), (0,)), ((), ())), preferred_element_type=jnp.float32
        )
    dpair_ref[:, :HEAD_WIDTH] = key_acc
    dpair_ref[:, HEAD_WIDTH:] = value_acc


def band_grads(query_blk, grad_blk, pair_win, query_seg, key_seg):
    tok_rows, q_width = query_blk.shape
    key_count, pair_width = pair_win.shape
    kv_heads = pair_width // (2 * HEAD_WIDTH)
    group_width = q_width // kv_heads
    return pl.pallas_call(
        band_kernel,
        grid=(kv_heads,),
        in_specs=[
            pl.BlockSpec((tok_rows, 1), lambda g: (0, 0)),
            pl.BlockSpec((1, key_count), lambda g: (0, 0)),
            pl.BlockSpec((tok_rows, group_width), lambda g: (0, g)),
            pl.BlockSpec((tok_rows, group_width), lambda g: (0, g)),
            pl.BlockSpec((key_count, 2 * HEAD_WIDTH), lambda g: (0, g)),
        ],
        out_specs=[
            pl.BlockSpec((tok_rows, group_width), lambda g: (0, g)),
            pl.BlockSpec((key_count, 2 * HEAD_WIDTH), lambda g: (0, g)),
        ],
        out_shape=[
            jax.ShapeDtypeStruct((tok_rows, q_width), jnp.bfloat16),
            jax.ShapeDtypeStruct((key_count, pair_width), jnp.float32),
        ],
    )(query_seg.reshape(tok_rows, 1), key_seg.reshape(1, key_count), query_blk, grad_blk, pair_win)


def interleave(first, second):
    rows, width = first.shape
    heads = width // HEAD_WIDTH
    return jnp.stack(
        [first.reshape(rows, heads, HEAD_WIDTH), second.reshape(rows, heads, HEAD_WIDTH)], 2
    ).reshape(rows, 2 * width)


def body(query_rows, key_rows, value_matrix, out_grad, segments):
    tok_rows = query_rows.shape[0]
    kv_width = key_rows.shape[1]
    position = lax.axis_index(("ctx", "fsdp"))
    query_first = position * tok_rows
    window = SPAN * tok_rows
    pair = interleave(key_rows, value_matrix)
    nearby = [(pair, segments)]
    for hop_back in range(1, SPAN + 1):
        nearby.insert(0, from_behind(nearby[0], ("ctx", "fsdp"), 1))
    pair_win = jnp.concatenate([member[0] for member in nearby], 0)
    seg_win = jnp.concatenate([member[1] for member in nearby], 0)
    key_pos = query_first - window + jnp.arange(window + tok_rows, dtype=jnp.int32)
    seg_win = jnp.where(key_pos >= 0, seg_win, -1)
    dq_part, grad_part = band_grads(query_rows, out_grad, pair_win, segments, seg_win)
    carried = grad_part[:tok_rows]
    for relay_step in range(1, SPAN + 1):
        received = from_behind(carried.astype(jnp.bfloat16), ("ctx", "fsdp"), -1)
        lower = relay_step * tok_rows
        carried = received.astype(jnp.float32) + grad_part[lower : lower + tok_rows]
    carried = carried.reshape(tok_rows, kv_width // HEAD_WIDTH, 2, HEAD_WIDTH)
    return (
        dq_part,
        carried[:, :, 0].reshape(tok_rows, kv_width).astype(jnp.bfloat16),
        carried[:, :, 1].reshape(tok_rows, kv_width).astype(jnp.bfloat16),
    )


def solution(mesh):
    return jax.shard_map(
        body,
        mesh=mesh,
        in_specs=(
            P(("ctx", "fsdp"), None),
            P(("ctx", "fsdp"), None),
            P(("ctx", "fsdp"), None),
            P(("ctx", "fsdp"), None),
            P(("ctx", "fsdp")),
        ),
        out_specs=(P(("ctx", "fsdp"), None), P(("ctx", "fsdp"), None), P(("ctx", "fsdp"), None)),
        check_vma=False,
    )
```

time: 152 us -> 132 us (0.87)
  the two profiles are of different devices: /device:TPU:56 before, /device:TPU:32 now
where the time goes in v2:
time: 132 us
  waiting for transfers between devices  67.7 us (51%)
  starting transfers between devices  30.5 us (23%)
  Pallas kernels  20 us (15%)
  local copies, waits for them, and re-layouts  7 us (5%)
  other arithmetic  5.56 us (4%)
    ppermute x9, waiting for transfers between devices, from_behind(): return lax.ppermute(block, axis, route)  67.7 us
    ppermute x9, starting transfers between devices, from_behind(): return lax.ppermute(block, axis, route)  30.5 us
    pallas_call x1, Pallas kernels, band_grads(): pl.pallas_call(band_kernel, grid=(kv_heads,), in_specs=[pl.BlockSpec((tok...  20 us
  transfers between devices with their start and end apart: 9, of which 8 were waited for; matrix products, arithmetic and copies ran while one was open for 1% of the time, Pallas kernels for 0%

profile of v2, /device:TPU:32, one launch (start us, length us, event | category | flops | bytes accessed | tf_op | source)
XLA Modules:
  0.0 131.6 jit_solution(11742919694651490630)
XLA Ops:
  0.6 0.0 copy-start
  0.6 1.3 stack_reshape.8
  2.0 1.3 stack_reshape.9
  3.3 0.6 pad_maximum_fusion.1
  3.9 0.2 reshape.84
  4.1 4.3 %collective-permute-start.3 = (bf16[128,1024]{1,0:T(8,128)(2,1)S(1)}, bf16[128,1024]{1,0:T(8,128)(2,1)S(1)}, u32[]{:S(2)}, u32[]{:S(2)}) collective-permute-start(bf16[128,1024]{1,0:T(8,128)(2,1)S(1)} %reshape.84), channel_id=1, source_target_pairs={{0,1},{1,2},{2,3},{3,4},{4,5},{5,6},{6,7},{7,8},{8,9},{9,10},{10,1... | collective-permute-start | bytes 786440 | tf_op jit(solution)/shard_map/ppermute | solution.py:16
  8.3 15.9 %collective-permute-done.3 = bf16[128,1024]{1,0:T(8,128)(2,1)S(1)} collective-permute-done((bf16[128,1024]{1,0:T(8,128)(2,1)S(1)}, bf16[128,1024]{1,0:T(8,128)(2,1)S(1)}, u32[]{:S(2)}, u32[]{:S(2)}) %collective-permute-start.3) | collective-permute-done | bytes 262176 | tf_op jit(solution)/shard_map/ppermute | solution.py:16
  24.2 1.9 %collective-permute-start.4 = (bf16[128,1024]{1,0:T(8,128)(2,1)S(1)}, bf16[128,1024]{1,0:T(8,128)(2,1)S(1)}, u32[]{:S(2)}, u32[]{:S(2)}) collective-permute-start(bf16[128,1024]{1,0:T(8,128)(2,1)S(1)} %collective-permute-done.3), channel_id=1, source_target_pairs={{0,1},{1,2},{2,3},{3,4},{4,5},{5,6},{6,7},{7,8},{8,9},{9,10},{10,1... | collective-permute-start | bytes 786440 | tf_op jit(solution)/shard_map/ppermute | solution.py:16
  26.1 11.2 %collective-permute-done.4 = bf16[128,1024]{1,0:T(8,128)(2,1)S(1)} collective-permute-done((bf16[128,1024]{1,0:T(8,128)(2,1)S(1)}, bf16[128,1024]{1,0:T(8,128)(2,1)S(1)}, u32[]{:S(2)}, u32[]{:S(2)}) %collective-permute-start.4) | collective-permute-done | bytes 262176 | tf_op jit(solution)/shard_map/ppermute | solution.py:16
  37.3 1.9 %collective-permute-start.5 = (bf16[128,1024]{1,0:T(8,128)(2,1)S(1)}, bf16[128,1024]{1,0:T(8,128)(2,1)S(1)}, u32[]{:S(2)}, u32[]{:S(2)}) collective-permute-start(bf16[128,1024]{1,0:T(8,128)(2,1)S(1)} %collective-permute-done.4), channel_id=1, source_target_pairs={{0,1},{1,2},{2,3},{3,4},{4,5},{5,6},{6,7},{7,8},{8,9},{9,10},{10,1... | collective-permute-start | bytes 786440 | tf_op jit(solution)/shard_map/ppermute | solution.py:16
  39.2 0.0 copy-done
  39.2 1.9 %collective-permute-start = (s32[128]{0:T(128)S(1)}, s32[128]{0:T(128)S(1)}, u32[]{:S(2)}, u32[]{:S(2)}) collective-permute-start(s32[128]{0:T(128)S(1)} %copy-done), channel_id=1, source_target_pairs={{0,1},{1,2},{2,3},{3,4},{4,5},{5,6},{6,7},{7,8},{8,9},{9,10},{10,1... | collective-permute-start | bytes 1544 | tf_op jit(solution)/shard_map/ppermute | solution.py:16
  41.2 9.3 %collective-permute-done = s32[128]{0:T(128)S(1)} collective-permute-done((s32[128]{0:T(128)S(1)}, s32[128]{0:T(128)S(1)}, u32[]{:S(2)}, u32[]{:S(2)}) %collective-permute-start) | collective-permute-done | bytes 544 | tf_op jit(solution)/shard_map/ppermute | solution.py:16
  50.5 1.9 %collective-permute-start.1 = (s32[128]{0:T(128)S(1)}, s32[128]{0:T(128)S(1)}, u32[]{:S(2)}, u32[]{:S(2)}) collective-permute-start(s32[128]{0:T(128)S(1)} %collective-permute-done), channel_id=1, source_target_pairs={{0,1},{1,2},{2,3},{3,4},{4,5},{5,6},{6,7},{7,8},{8,9},{9,10},{10,1... | collective-permute-start | bytes 1544 | tf_op jit(solution)/shard_map/ppermute | solution.py:16
  52.4 8.3 %collective-permute-done.1 = s32[128]{0:T(128)S(1)} collective-permute-done((s32[128]{0:T(128)S(1)}, s32[128]{0:T(128)S(1)}, u32[]{:S(2)}, u32[]{:S(2)}) %collective-permute-start.1) | collective-permute-done | bytes 544 | tf_op jit(solution)/shard_map/ppermute | solution.py:16
  60.8 1.9 %collective-permute-start.2 = (s32[128]{0:T(128)S(1)}, s32[128]{0:T(128)S(1)}, u32[]{:S(2)}, u32[]{:S(2)}) collective-permute-start(s32[128]{0:T(128)S(1)} %collective-permute-done.1), channel_id=1, source_target_pairs={{0,1},{1,2},{2,3},{3,4},{4,5},{5,6},{6,7},{7,8},{8,9},{9,10},{10,1... | collective-permute-start | bytes 1544 | tf_op jit(solution)/shard_map/ppermute | solution.py:16
  62.7 0.7 copy.13.seg_q_ref
  63.4 7.6 %collective-permute-done.2 = s32[128]{0:T(128)S(1)} collective-permute-done((s32[128]{0:T(128)S(1)}, s32[128]{0:T(128)S(1)}, u32[]{:S(2)}, u32[]{:S(2)}) %collective-permute-start.2) | collective-permute-done | bytes 544 | tf_op jit(solution)/shard_map/ppermute | solution.py:16
  71.0 0.6 compare_select_fusion.seg_k_ref
  71.6 0.0 collective-permute-done.5
  71.6 1.1 pad_maximum_fusion.pair_ref
  72.7 20.0 %shard_map.76 = (bf16[128,4096]{1,0:T(8,128)(2,1)}, f32[512,1024]{1,0:T(8,128)}) custom-call(s32[128,1]{1,0:T(8,128)} %copy.13.seg_q_ref, s32[1,512]{1,0:T(1,128)} %compare_select_fusion.seg_k_ref, bf16[128,4096]{1,0:T(8,128)(2,1)} %query_ref.1, bf16[128,4096]{1,0:T(8,128)(2,1)} %grad_ref.1, bf16[512,1024]{1,0:T(8,128)(2,1)} %pad_maximum_fusion.pair_ref), custom_call_target="tpu_custom_call" | custom-call | tf_op jit(solution)/shard_map/pallas_call | solution.py:67
  92.7 1.1 slice.34
  93.8 1.9 %collective-permute-start.6 = (bf16[128,1024]{1,0:T(8,128)(2,1)S(1)}, bf16[128,1024]{1,0:T(8,128)(2,1)S(1)}, u32[]{:S(2)}, u32[]{:S(2)}) collective-permute-start(bf16[128,1024]{1,0:T(8,128)(2,1)S(1)} %slice.34), channel_id=1, source_target_pairs={{1,0},{2,1},{3,2},{4,3},{5,4},{6,5},{7,6},{8,7},{9,8},{10,9},{11,1... | collective-permute-start | bytes 786440 | tf_op jit(solution)/shard_map/ppermute | solution.py:16
  95.7 7.6 %collective-permute-done.6 = bf16[128,1024]{1,0:T(8,128)(2,1)S(1)} collective-permute-done((bf16[128,1024]{1,0:T(8,128)(2,1)S(1)}, bf16[128,1024]{1,0:T(8,128)(2,1)S(1)}, u32[]{:S(2)}, u32[]{:S(2)}) %collective-permute-start.6) | collective-permute-done | bytes 262176 | tf_op jit(solution)/shard_map/ppermute | solution.py:16
  103.3 1.1 add_convert_fusion.2
  104.4 5.5 %collective-permute-start.7 = (bf16[128,1024]{1,0:T(8,128)(2,1)S(1)}, bf16[128,1024]{1,0:T(8,128)(2,1)S(1)}, u32[]{:S(2)}, u32[]{:S(2)}) collective-permute-start(bf16[128,1024]{1,0:T(8,128)(2,1)S(1)} %add_convert_fusion.2), channel_id=1, source_target_pairs={{1,0},{2,1},{3,2},{4,3},{5,4},{6,5},{7,6},{8,7},{9,8},{10,9},{11,1... | collective-permute-start | bytes 786440 | tf_op jit(solution)/shard_map/ppermute | solution.py:16
  110.0 3.9 %collective-permute-done.7 = bf16[128,1024]{1,0:T(8,128)(2,1)S(1)} collective-permute-done((bf16[128,1024]{1,0:T(8,128)(2,1)S(1)}, bf16[128,1024]{1,0:T(8,128)(2,1)S(1)}, u32[]{:S(2)}, u32[]{:S(2)}) %collective-permute-start.7) | collective-permute-done | bytes 262176 | tf_op jit(solution)/shard_map/ppermute | solution.py:16
  113.8 1.1 add_convert_fusion.1
  114.9 9.2 %collective-permute-start.8 = (bf16[128,1024]{1,0:T(8,128)(2,1)S(1)}, bf16[128,1024]{1,0:T(8,128)(2,1)S(1)}, u32[]{:S(2)}, u32[]{:S(2)}) collective-permute-start(bf16[128,1024]{1,0:T(8,128)(2,1)S(1)} %add_convert_fusion.1), channel_id=1, source_target_pairs={{1,0},{2,1},{3,2},{4,3},{5,4},{6,5},{7,6},{8,7},{9,8},{10,9},{11,1... | collective-permute-start | bytes 786440 | tf_op jit(solution)/shard_map/ppermute | solution.py:16
  124.2 3.9 %collective-permute-done.8 = bf16[128,1024]{1,0:T(8,128)(2,1)S(1)} collective-permute-done((bf16[128,1024]{1,0:T(8,128)(2,1)S(1)}, bf16[128,1024]{1,0:T(8,128)(2,1)S(1)}, u32[]{:S(2)}, u32[]{:S(2)}) %collective-permute-start.8) | collective-permute-done | bytes 262176 | tf_op jit(solution)/shard_map/ppermute | solution.py:16
  128.1 1.1 add_convert_fusion
  129.2 0.2 reshape.86
  129.3 0.4 fusion
  129.7 0.2 copy.19
  129.9 0.8 copy.17
  130.6 0.2 copy.18
  130.8 0.8 copy.16
Async XLA Ops:
  0.6 38.6 %copy-start = (s32[128]{0:T(128)S(1)}, s32[128]{0:T(128)}, u32[]{:S(2)}) copy-start(s32[128]{0:T(128)} %param.9) | copy-start | bytes 1540
  4.1 20.2 %collective-permute-start.3 = (bf16[128,1024]{1,0:T(8,128)(2,1)S(1)}, bf16[128,1024]{1,0:T(8,128)(2,1)S(1)}, u32[]{:S(2)}, u32[]{:S(2)}) collective-permute-start(bf16[128,1024]{1,0:T(8,128)(2,1)S(1)} %reshape.84), channel_id=1, source_target_pairs={{0,1},{1,2},{2,3},{3,4},{4,5},{5,6},{6,7},{7,8},{8,9},{9,10},{10,1... | collective-permute-start | bytes 786440 | tf_op jit(solution)/shard_map/ppermute | solution.py:16
  24.2 13.1 %collective-permute-start.4 = (bf16[128,1024]{1,0:T(8,128)(2,1)S(1)}, bf16[128,1024]{1,0:T(8,128)(2,1)S(1)}, u32[]{:S(2)}, u32[]{:S(2)}) collective-permute-start(bf16[128,1024]{1,0:T(8,128)(2,1)S(1)} %collective-permute-done.3), channel_id=1, source_target_pairs={{0,1},{1,2},{2,3},{3,4},{4,5},{5,6},{6,7},{7,8},{8,9},{9,10},{10,1... | collective-permute-start | bytes 786440 | tf_op jit(solution)/shard_map/ppermute | solution.py:16
  37.3 34.3 %collective-permute-start.5 = (bf16[128,1024]{1,0:T(8,128)(2,1)S(1)}, bf16[128,1024]{1,0:T(8,128)(2,1)S(1)}, u32[]{:S(2)}, u32[]{:S(2)}) collective-permute-start(bf16[128,1024]{1,0:T(8,128)(2,1)S(1)} %collective-permute-done.4), channel_id=1, source_target_pairs={{0,1},{1,2},{2,3},{3,4},{4,5},{5,6},{6,7},{7,8},{8,9},{9,10},{10,1... | collective-permute-start | bytes 786440 | tf_op jit(solution)/shard_map/ppermute | solution.py:16
  39.2 11.2 %collective-permute-start = (s32[128]{0:T(128)S(1)}, s32[128]{0:T(128)S(1)}, u32[]{:S(2)}, u32[]{:S(2)}) collective-permute-start(s32[128]{0:T(128)S(1)} %copy-done), channel_id=1, source_target_pairs={{0,1},{1,2},{2,3},{3,4},{4,5},{5,6},{6,7},{7,8},{8,9},{9,10},{10,1... | collective-permute-start | bytes 1544 | tf_op jit(solution)/shard_map/ppermute | solution.py:16
  50.5 10.3 %collective-permute-start.1 = (s32[128]{0:T(128)S(1)}, s32[128]{0:T(128)S(1)}, u32[]{:S(2)}, u32[]{:S(2)}) collective-permute-start(s32[128]{0:T(128)S(1)} %collective-permute-done), channel_id=1, source_target_pairs={{0,1},{1,2},{2,3},{3,4},{4,5},{5,6},{6,7},{7,8},{8,9},{9,10},{10,1... | collective-permute-start | bytes 1544 | tf_op jit(solution)/shard_map/ppermute | solution.py:16
  60.8 10.3 %collective-permute-start.2 = (s32[128]{0:T(128)S(1)}, s32[128]{0:T(128)S(1)}, u32[]{:S(2)}, u32[]{:S(2)}) collective-permute-start(s32[128]{0:T(128)S(1)} %collective-permute-done.1), channel_id=1, source_target_pairs={{0,1},{1,2},{2,3},{3,4},{4,5},{5,6},{6,7},{7,8},{8,9},{9,10},{10,1... | collective-permute-start | bytes 1544 | tf_op jit(solution)/shard_map/ppermute | solution.py:16
  93.8 9.5 %collective-permute-start.6 = (bf16[128,1024]{1,0:T(8,128)(2,1)S(1)}, bf16[128,1024]{1,0:T(8,128)(2,1)S(1)}, u32[]{:S(2)}, u32[]{:S(2)}) collective-permute-start(bf16[128,1024]{1,0:T(8,128)(2,1)S(1)} %slice.34), channel_id=1, source_target_pairs={{1,0},{2,1},{3,2},{4,3},{5,4},{6,5},{7,6},{8,7},{9,8},{10,9},{11,1... | collective-permute-start | bytes 786440 | tf_op jit(solution)/shard_map/ppermute | solution.py:16
  104.4 9.4 %collective-permute-start.7 = (bf16[128,1024]{1,0:T(8,128)(2,1)S(1)}, bf16[128,1024]{1,0:T(8,128)(2,1)S(1)}, u32[]{:S(2)}, u32[]{:S(2)}) collective-permute-start(bf16[128,1024]{1,0:T(8,128)(2,1)S(1)} %add_convert_fusion.2), channel_id=1, source_target_pairs={{1,0},{2,1},{3,2},{4,3},{5,4},{6,5},{7,6},{8,7},{9,8},{10,9},{11,1... | collective-permute-start | bytes 786440 | tf_op jit(solution)/shard_map/ppermute | solution.py:16
  114.9 13.1 %collective-permute-start.8 = (bf16[128,1024]{1,0:T(8,128)(2,1)S(1)}, bf16[128,1024]{1,0:T(8,128)(2,1)S(1)}, u32[]{:S(2)}, u32[]{:S(2)}) collective-permute-start(bf16[128,1024]{1,0:T(8,128)(2,1)S(1)} %add_convert_fusion.1), channel_id=1, source_target_pairs={{1,0},{2,1},{3,2},{4,3},{5,4},{6,5},{7,6},{8,7},{9,8},{10,9},{11,1... | collective-permute-start | bytes 786440 | tf_op jit(solution)/shard_map/ppermute | solution.py:16

commit v3 on v2

v3 whole, which is shorter than its diff:
```python
import math

import jax
import jax.numpy as jnp
from jax import lax
from jax.experimental import pallas as pl
from jax.sharding import PartitionSpec as P

HEAD_WIDTH = 128
SPAN = 3


def from_behind(block, axis, distance):
    devices = range(lax.axis_size(axis))
    route = [(i - distance, i) for i in devices if i - distance in devices]
    return lax.ppermute(block, axis, route)


def band_kernel(seg_q_ref, seg_k_ref, query_ref, grad_ref, *refs):
    key_refs = refs[0:8:2]
    value_refs = refs[1:8:2]
    dq_ref, send_ref, middle_ref, own_ref = refs[8:]
    tok_rows = query_ref.shape[0]
    key_count = tok_rows * len(key_refs)
    heads_per_group = query_ref.shape[1] // HEAD_WIDTH
    inv_root = 1.0 / math.sqrt(HEAD_WIDTH)
    row = lax.broadcasted_iota(jnp.int32, (tok_rows, key_count), 0)
    col = lax.broadcasted_iota(jnp.int32, (tok_rows, key_count), 1)
    window = key_count - tok_rows
    allowed = (col > row) & (col <= row + window) & (seg_k_ref[...] == seg_q_ref[...])
    k_head = jnp.concatenate([ref[...] for ref in key_refs], 0)
    v_head = jnp.concatenate([ref[...] for ref in value_refs], 0)
    key_acc = jnp.zeros((key_count, HEAD_WIDTH), jnp.float32)
    value_acc = jnp.zeros((key_count, HEAD_WIDTH), jnp.float32)
    for head in range(heads_per_group):
        cols = slice(head * HEAD_WIDTH, (head + 1) * HEAD_WIDTH)
        q_head = query_ref[:, cols]
        o_grad = grad_ref[:, cols]
        scores = lax.dot_general(
            q_head, k_head, (((1,), (1,)), ((), ())), preferred_element_type=jnp.float32
        )
        scores = jnp.where(allowed, scores * inv_root, -1e30)
        row_max = jnp.max(scores, axis=1, keepdims=True)
        weights = jnp.exp(scores - row_max)
        probs = weights * (1.0 / jnp.sum(weights, axis=1, keepdims=True))
        prob_grad = lax.dot_general(
            o_grad, v_head, (((1,), (1,)), ((), ())), preferred_element_type=jnp.float32
        )
        row_delta = jnp.sum(probs * prob_grad, axis=1, keepdims=True)
        score_grad = (probs * (prob_grad - row_delta) * inv_root).astype(jnp.bfloat16)
        probs_low = probs.astype(jnp.bfloat16)
        dq_ref[:, cols] = jnp.dot(
            score_grad, k_head, preferred_element_type=jnp.float32
        ).astype(jnp.bfloat16)
        key_acc = key_acc + lax.dot_general(
            score_grad, q_head, (((0,), (0,)), ((), ())), preferred_element_type=jnp.float32
        )
        value_acc = value_acc + lax.dot_general(
            probs_low, o_grad, (((0,), (0,)), ((), ())), preferred_element_type=jnp.float32
        )

    def rows(block):
        return slice(block * tok_rows, (block + 1) * tok_rows)

    w = HEAD_WIDTH
    send_ref[:, 0:w] = key_acc[rows(0)].astype(jnp.bfloat16)
    send_ref[:, w : 2 * w] = value_acc[rows(0)].astype(jnp.bfloat16)
    send_ref[:, 2 * w : 3 * w] = key_acc[rows(2)].astype(jnp.bfloat16)
    send_ref[:, 3 * w : 4 * w] = value_acc[rows(2)].astype(jnp.bfloat16)
    middle_ref[:, 0:w] = key_acc[rows(1)]
    middle_ref[:, w : 2 * w] = value_acc[rows(1)]
    own_ref[:, 0:w] = key_acc[rows(3)]
    own_ref[:, w : 2 * w] = value_acc[rows(3)]


def band_grads(query_blk, grad_blk, blocks, query_seg, key_seg):
    tok_rows, q_width = query_blk.shape
    kv_heads = (blocks[0].shape[1] - HEAD_WIDTH) // (2 * HEAD_WIDTH)
    group_width = q_width // kv_heads
    kv_specs = []
    kv_args = []
    for blk in blocks:
        kv_specs.append(pl.BlockSpec((tok_rows, HEAD_WIDTH), lambda g: (0, g)))
        kv_specs.append(pl.BlockSpec((tok_rows, HEAD_WIDTH), lambda g, n=kv_heads: (0, n + g)))
        kv_args += [blk, blk]
    return pl.pallas_call(
        band_kernel,
        grid=(kv_heads,),
        in_specs=[
            pl.BlockSpec((tok_rows, 1), lambda g: (0, 0)),
            pl.BlockSpec((1, key_seg.shape[0]), lambda g: (0, 0)),
            pl.BlockSpec((tok_rows, group_width), lambda g: (0, g)),
            pl.BlockSpec((tok_rows, group_width), lambda g: (0, g)),
        ]
        + kv_specs,
        out_specs=[
            pl.BlockSpec((tok_rows, group_width), lambda g: (0, g)),
            pl.BlockSpec((tok_rows, 4 * HEAD_WIDTH), lambda g: (0, g)),
            pl.BlockSpec((tok_rows, 2 * HEAD_WIDTH), lambda g: (0, g)),
            pl.BlockSpec((tok_rows, 2 * HEAD_WIDTH), lambda g: (0, g)),
        ],
        out_shape=[
            jax.ShapeDtypeStruct((tok_rows, q_width), jnp.bfloat16),
            jax.ShapeDtypeStruct((tok_rows, 4 * HEAD_WIDTH * kv_heads), jnp.bfloat16),
            jax.ShapeDtypeStruct((tok_rows, 2 * HEAD_WIDTH * kv_heads), jnp.float32),
            jax.ShapeDtypeStruct((tok_rows, 2 * HEAD_WIDTH * kv_heads), jnp.float32),
        ],
    )(query_seg.reshape(tok_rows, 1), key_seg.reshape(1, -1), query_blk, grad_blk, *kv_args)


def body(query_rows, key_rows, value_matrix, out_grad, segments):
    tok_rows = query_rows.shape[0]
    kv_width = key_rows.shape[1]
    kv_heads = kv_width // HEAD_WIDTH
    axes = ("ctx", "fsdp")
    position = lax.axis_index(axes)
    query_first = position * tok_rows
    window = SPAN * tok_rows
    seg_cols = jnp.broadcast_to(segments.astype(jnp.bfloat16)[:, None], (tok_rows, HEAD_WIDTH))
    own = jnp.concatenate([key_rows, value_matrix, seg_cols], 1)
    back_one = from_behind(own, axes, 1)
    back_two = from_behind(own, axes, 2)
    back_three = from_behind(back_two, axes, 1)
    blocks = [back_three, back_two, back_one, own]
    seg_win = jnp.concatenate([blk[:, 2 * kv_width] for blk in blocks], 0).astype(jnp.int32)
    key_pos = query_first - window + jnp.arange(window + tok_rows, dtype=jnp.int32)
    seg_win = jnp.where(key_pos >= 0, seg_win, -1)
    dq_part, send, middle, own_part = band_grads(query_rows, out_grad, blocks, segments, seg_win)
    received = from_behind(send, axes, -1).reshape(tok_rows, kv_heads, 2, 2 * HEAD_WIDTH)
    middle = middle.reshape(tok_rows, kv_heads, 2 * HEAD_WIDTH)
    forward = (middle + received[:, :, 0].astype(jnp.float32)).astype(jnp.bfloat16)
    gathered = from_behind(forward, axes, -2)
    total = (
        own_part.reshape(tok_rows, kv_heads, 2 * HEAD_WIDTH)
        + received[:, :, 1].astype(jnp.float32)
        + gathered.astype(jnp.float32)
    ).reshape(tok_rows, kv_heads, 2, HEAD_WIDTH)
    return (
        dq_part,
        total[:, :, 0].reshape(tok_rows, kv_width).astype(jnp.bfloat16),
        total[:, :, 1].reshape(tok_rows, kv_width).astype(jnp.bfloat16),
    )


def solution(mesh):
    return jax.shard_map(
        body,
        mesh=mesh,
        in_specs=(
            P(("ctx", "fsdp"), None),
            P(("ctx", "fsdp"), None),
            P(("ctx", "fsdp"), None),
            P(("ctx", "fsdp"), None),
            P(("ctx", "fsdp")),
        ),
        out_specs=(P(("ctx", "fsdp"), None), P(("ctx", "fsdp"), None), P(("ctx", "fsdp"), None)),
        check_vma=False,
    )
```

time: 132 us -> 96.4 us (0.73)
  the two profiles are of different devices: /device:TPU:32 before, /device:TPU:56 now
where the time goes in v3:
time: 96.4 us; the launch traced here: 96.1 us
  starting transfers between devices  33.2 us (34%)
  waiting for transfers between devices  32.5 us (34%)
  Pallas kernels  20.1 us (21%)
  local copies, waits for them, and re-layouts  6.73 us (7%)
  other arithmetic  2.71 us (3%)
    ppermute x5, starting transfers between devices, from_behind(): return lax.ppermute(block, axis, route)  33.2 us
    ppermute x5, waiting for transfers between devices, from_behind(): return lax.ppermute(block, axis, route)  32.5 us
    pallas_call x1, Pallas kernels, band_grads(): pl.pallas_call(band_kernel, grid=(kv_heads,), in_specs=[pl.BlockSpec((tok...  20.1 us
  transfers between devices with their start and end apart: 5, of which 4 were waited for; matrix products, arithmetic and copies ran while one was open for 3% of the time, Pallas kernels for 0%

profile of v3, /device:TPU:56, one launch (start us, length us, event | category | flops | bytes accessed | tf_op | source)
XLA Modules:
  0.0 96.1 jit_solution(6207134246272920445)
XLA Ops:
  0.6 0.7 fusion.4
  1.3 0.1 broadcast_in_dim.10
  1.4 1.0 %pad_maximum_fusion.refs_6_.refs_7_ = bf16[128,1152]{1,0:T(8,128)(2,1)S(1)} fusion(bf16[128,128]{1,0:T(8,128)(2,1)S(1)} %broadcast_in_dim.10, bf16[128,512]{1,0:T(8,128)(2,1)} %param.7, bf16[128,512]{1,0:T(8,128)(2,1)} %param.6), kind=kLoop, calls=%fused_computation.5 | loop fusion | flops 884736 | bytes 589824 | tf_op jit(solution)/shard_map/concatenate | solution.py:120
  2.4 0.0 copy-start
  2.4 6.1 %collective-permute-start = (bf16[128,1152]{1,0:T(8,128)(2,1)S(1)}, bf16[128,1152]{1,0:T(8,128)(2,1)S(1)}, u32[]{:S(2)}, u32[]{:S(2)}) collective-permute-start(bf16[128,1152]{1,0:T(8,128)(2,1)S(1)} %pad_maximum_fusion.refs_6_.refs_7_), channel_id=1, source_target_pairs={{0,2},{1,3},{2,4},{3,5},{4,6},{5,7},{6,8},{7,9},{8,10},{9,11},{10,... | collective-permute-start | bytes 884744 | tf_op jit(solution)/shard_map/ppermute | solution.py:16
  8.5 4.3 %collective-permute-start.2 = (bf16[128,1152]{1,0:T(8,128)(2,1)S(1)}, bf16[128,1152]{1,0:T(8,128)(2,1)S(1)}, u32[]{:S(2)}, u32[]{:S(2)}) collective-permute-start(bf16[128,1152]{1,0:T(8,128)(2,1)S(1)} %pad_maximum_fusion.refs_6_.refs_7_), channel_id=1, source_target_pairs={{0,1},{1,2},{2,3},{3,4},{4,5},{5,6},{6,7},{7,8},{8,9},{9,10},{10,1... | collective-permute-start | bytes 884744 | tf_op jit(solution)/shard_map/ppermute | solution.py:16
  12.8 11.2 %collective-permute-done.refs_2_.refs_3_ = bf16[128,1152]{1,0:T(8,128)(2,1)S(1)} collective-permute-done((bf16[128,1152]{1,0:T(8,128)(2,1)S(1)}, bf16[128,1152]{1,0:T(8,128)(2,1)S(1)}, u32[]{:S(2)}, u32[]{:S(2)}) %collective-permute-start) | collective-permute-done | bytes 294944 | tf_op jit(solution)/shard_map/ppermute | solution.py:16
  23.9 0.0 copy-start.1
  23.9 6.5 %collective-permute-start.1 = (bf16[128,1152]{1,0:T(8,128)(2,1)S(1)}, bf16[128,1152]{1,0:T(8,128)(2,1)S(1)}, u32[]{:S(2)}, u32[]{:S(2)}) collective-permute-start(bf16[128,1152]{1,0:T(8,128)(2,1)S(1)} %collective-permute-done.refs_2_.refs_3_), channel_id=1, source_target_pairs={{0,1},{1,2},{2,3},{3,4},{4,5},{5,6},{6,7},{7,8},{8,9},{9,10},{10,1... | collective-permute-start | bytes 884744 | tf_op jit(solution)/shard_map/ppermute | solution.py:16
  30.4 0.0 copy-start.5
  30.4 0.6 copy-done.5
  31.1 0.7 copy.13.seg_q_ref
  31.8 0.1 slice_reduce_fusion.3
  31.9 0.0 collective-permute-done.2.refs_4_.refs_5_
  31.9 0.0 copy-start.2
  32.0 0.1 slice_reduce_fusion.2
  32.1 9.7 %collective-permute-done.1.refs_0_.refs_1_ = bf16[128,1152]{1,0:T(8,128)(2,1)S(1)} collective-permute-done((bf16[128,1152]{1,0:T(8,128)(2,1)S(1)}, bf16[128,1152]{1,0:T(8,128)(2,1)S(1)}, u32[]{:S(2)}, u32[]{:S(2)}) %collective-permute-start.1) | collective-permute-done | bytes 294944 | tf_op jit(solution)/shard_map/ppermute | solution.py:16
  41.8 0.0 copy-start.3
  41.8 0.1 slice_reduce_fusion.4
  41.9 0.6 compare_select_fusion.seg_k_ref
  42.5 0.0 copy-done
  42.5 0.0 copy-done.1
  42.5 0.0 copy-done.2
  42.5 0.0 copy-done.3
  42.5 20.1 %shard_map.76 = (bf16[128,4096]{1,0:T(8,128)(2,1)}, bf16[128,2048]{1,0:T(8,128)(2,1)}, f32[128,1024]{1,0:T(8,128)}, f32[128,1024]{1,0:T(8,128)}) custom-call(s32[128,1]{1,0:T(8,128)} %copy.13.seg_q_ref, s32[1,512]{1,0:T(1,128)} %compare_select_fusion.seg_k_ref, bf16[128,4096]{1,0:T(8,128)(2,1)} %query_ref.1, bf16[128,4096]{1,0:T(8,128)(2,1)} %grad_ref.1, ...), custom_call_target="tpu_custom_call" | custom-call | tf_op jit(solution)/shard_map/pallas_call | solution.py:86
  62.7 5.5 %collective-permute-start.3 = (bf16[128,2048]{1,0:T(8,128)(2,1)}, bf16[128,2048]{1,0:T(8,128)(2,1)S(1)}, u32[]{:S(2)}, u32[]{:S(2)}) collective-permute-start(bf16[128,2048]{1,0:T(8,128)(2,1)} %get-tuple-element.9), channel_id=1, source_target_pairs={{1,0},{2,1},{3,2},{4,3},{5,4},{6,5},{7,6},{8,7},{9,8},{10,9},{11,1... | collective-permute-start | bytes 1572872 | tf_op jit(solution)/shard_map/ppermute | solution.py:16
  68.2 1.3 %reshape.104 = f32[128,4,256]{2,1,0:T(4,128)S(1)} reshape(f32[128,1024]{1,0:T(8,128)} %get-tuple-element.10) | data formatting | bytes 1048576 | tf_op jit(solution)/shard_map/reshape | solution.py:130
  69.4 5.7 %collective-permute-done.3 = bf16[128,2048]{1,0:T(8,128)(2,1)S(1)} collective-permute-done((bf16[128,2048]{1,0:T(8,128)(2,1)}, bf16[128,2048]{1,0:T(8,128)(2,1)S(1)}, u32[]{:S(2)}, u32[]{:S(2)}) %collective-permute-start.3) | collective-permute-done | bytes 524320 | tf_op jit(solution)/shard_map/ppermute | solution.py:16
  75.1 0.4 reshape.103
  75.5 0.7 fusion.3
  76.3 0.0 copy-start.4
  76.3 0.2 fusion
  76.5 10.9 %collective-permute-start.4 = (bf16[128,4,256]{2,1,0:T(4,128)(2,1)S(1)}, bf16[128,4,256]{2,1,0:T(4,128)(2,1)S(1)}, u32[]{:S(2)}, u32[]{:S(2)}) collective-permute-start(bf16[128,4,256]{2,1,0:T(4,128)(2,1)S(1)} %fusion), channel_id=1, source_target_pairs={{2,0},{3,1},{4,2},{5,3},{6,4},{7,5},{8,6},{9,7},{10,8},{11,9},{12,... | collective-permute-start | bytes 786440 | tf_op jit(solution)/shard_map/ppermute | solution.py:16
  87.4 0.0 copy-done.4
  87.4 0.2 reshape.102
  87.7 5.9 %collective-permute-done.4 = bf16[128,4,256]{2,1,0:T(4,128)(2,1)S(1)} collective-permute-done((bf16[128,4,256]{2,1,0:T(4,128)(2,1)S(1)}, bf16[128,4,256]{2,1,0:T(4,128)(2,1)S(1)}, u32[]{:S(2)}, u32[]{:S(2)}) %collective-permute-start.4) | collective-permute-done | bytes 262176 | tf_op jit(solution)/shard_map/ppermute | solution.py:16
  93.6 0.2 fusion.2
  93.8 0.1 reshape.108
  93.9 1.5 %slice_reduce_fusion = (bf16[128,4,128]{2,1,0:T(4,128)(2,1)S(1)}, bf16[128,4,128]{2,1,0:T(4,128)(2,1)S(1)}) fusion(bf16[128,4,2,128]{3,2,1,0:T(2,128)(2,1)S(1)} %reshape.108), kind=kLoop, calls=%fused_computation.6 | loop fusion | bytes 524288 | tf_op jit(solution)/shard_map/slice | solution.py:141
  95.4 0.7 copy_bitcast_fusion.2
Async XLA Ops:
  2.4 40.1 %copy-start = (bf16[128,1152]{1,0:T(8,128)(2,1)}, bf16[128,1152]{1,0:T(8,128)(2,1)S(1)}, u32[]{:S(2)}) copy-start(bf16[128,1152]{1,0:T(8,128)(2,1)S(1)} %pad_maximum_fusion.refs_6_.refs_7_) | copy-start | bytes 884740
  2.4 21.5 %collective-permute-start = (bf16[128,1152]{1,0:T(8,128)(2,1)S(1)}, bf16[128,1152]{1,0:T(8,128)(2,1)S(1)}, u32[]{:S(2)}, u32[]{:S(2)}) collective-permute-start(bf16[128,1152]{1,0:T(8,128)(2,1)S(1)} %pad_maximum_fusion.refs_6_.refs_7_), channel_id=1, source_target_pairs={{0,2},{1,3},{2,4},{3,5},{4,6},{5,7},{6,8},{7,9},{8,10},{9,11},{10,... | collective-permute-start | bytes 884744 | tf_op jit(solution)/shard_map/ppermute | solution.py:16
  8.5 23.5 %collective-permute-start.2 = (bf16[128,1152]{1,0:T(8,128)(2,1)S(1)}, bf16[128,1152]{1,0:T(8,128)(2,1)S(1)}, u32[]{:S(2)}, u32[]{:S(2)}) collective-permute-start(bf16[128,1152]{1,0:T(8,128)(2,1)S(1)} %pad_maximum_fusion.refs_6_.refs_7_), channel_id=1, source_target_pairs={{0,1},{1,2},{2,3},{3,4},{4,5},{5,6},{6,7},{7,8},{8,9},{9,10},{10,1... | collective-permute-start | bytes 884744 | tf_op jit(solution)/shard_map/ppermute | solution.py:16
  23.9 18.6 %copy-start.1 = (bf16[128,1152]{1,0:T(8,128)(2,1)}, bf16[128,1152]{1,0:T(8,128)(2,1)S(1)}, u32[]{:S(2)}) copy-start(bf16[128,1152]{1,0:T(8,128)(2,1)S(1)} %collective-permute-done.refs_2_.refs_3_) | copy-start | bytes 884740
  23.9 17.9 %collective-permute-start.1 = (bf16[128,1152]{1,0:T(8,128)(2,1)S(1)}, bf16[128,1152]{1,0:T(8,128)(2,1)S(1)}, u32[]{:S(2)}, u32[]{:S(2)}) collective-permute-start(bf16[128,1152]{1,0:T(8,128)(2,1)S(1)} %collective-permute-done.refs_2_.refs_3_), channel_id=1, source_target_pairs={{0,1},{1,2},{2,3},{3,4},{4,5},{5,6},{6,7},{7,8},{8,9},{9,10},{10,1... | collective-permute-start | bytes 884744 | tf_op jit(solution)/shard_map/ppermute | solution.py:16
  30.4 0.7 copy-start.5
  31.9 10.6 %copy-start.2 = (bf16[128,1152]{1,0:T(8,128)(2,1)}, bf16[128,1152]{1,0:T(8,128)(2,1)S(1)}, u32[]{:S(2)}) copy-start(bf16[128,1152]{1,0:T(8,128)(2,1)S(1)} %collective-permute-done.2.refs_4_.refs_5_) | copy-start | bytes 884740
  41.8 0.7 copy-start.3
  62.7 12.5 %collective-permute-start.3 = (bf16[128,2048]{1,0:T(8,128)(2,1)}, bf16[128,2048]{1,0:T(8,128)(2,1)S(1)}, u32[]{:S(2)}, u32[]{:S(2)}) collective-permute-start(bf16[128,2048]{1,0:T(8,128)(2,1)} %get-tuple-element.9), channel_id=1, source_target_pairs={{1,0},{2,1},{3,2},{4,3},{5,4},{6,5},{7,6},{8,7},{9,8},{10,9},{11,1... | collective-permute-start | bytes 1572872 | tf_op jit(solution)/shard_map/ppermute | solution.py:16
  76.3 11.1 %copy-start.4 = (f32[128,1024]{1,0:T(8,128)S(1)}, f32[128,1024]{1,0:T(8,128)}, u32[]{:S(2)}) copy-start(f32[128,1024]{1,0:T(8,128)} %get-tuple-element.8) | copy-start | bytes 1572868
  76.5 17.1 %collective-permute-start.4 = (bf16[128,4,256]{2,1,0:T(4,128)(2,1)S(1)}, bf16[128,4,256]{2,1,0:T(4,128)(2,1)S(1)}, u32[]{:S(2)}, u32[]{:S(2)}) collective-permute-start(bf16[128,4,256]{2,1,0:T(4,128)(2,1)S(1)} %fusion), channel_id=1, source_target_pairs={{2,0},{3,1},{4,2},{5,3},{6,4},{7,5},{8,6},{9,7},{10,8},{11,9},{12,... | collective-permute-start | bytes 786440 | tf_op jit(solution)/shard_map/ppermute | solution.py:16

commit v4 on v3

--- a/solution.py
+++ b/solution.py
@@ -8,6 +8,7 @@
 
 HEAD_WIDTH = 128
 SPAN = 3
+GROUP_HEADS = 8
 
 
 def from_behind(block, axis, distance):
@@ -19,7 +20,7 @@
 def band_kernel(seg_q_ref, seg_k_ref, query_ref, grad_ref, *refs):
     key_refs = refs[0:8:2]
     value_refs = refs[1:8:2]
-    dq_ref, send_ref, middle_ref, own_ref = refs[8:]
+    dq_ref, send_ref, middle_ref, own_ref = refs[-4:]
     tok_rows = query_ref.shape[0]
     key_count = tok_rows * len(key_refs)
     heads_per_group = query_ref.shape[1] // HEAD_WIDTH
@@ -73,28 +74,35 @@
     own_ref[:, w : 2 * w] = value_acc[rows(3)]
 
 
-def band_grads(query_blk, grad_blk, blocks, query_seg, key_seg):
-    tok_rows, q_width = query_blk.shape
-    kv_heads = (blocks[0].shape[1] - HEAD_WIDTH) // (2 * HEAD_WIDTH)
-    group_width = q_width // kv_heads
+def band_grads(query_rows, out_grad, blocks, query_seg, key_seg, first_kv, kv_heads, dq_buf):
+    tok_rows, q_width = query_rows.shape
+    group_width = HEAD_WIDTH * GROUP_HEADS
     kv_specs = []
     kv_args = []
     for blk in blocks:
         kv_specs.append(pl.BlockSpec((tok_rows, HEAD_WIDTH), lambda g: (0, g)))
         kv_specs.append(pl.BlockSpec((tok_rows, HEAD_WIDTH), lambda g, n=kv_heads: (0, n + g)))
         kv_args += [blk, blk]
+    extra_specs = []
+    extra_args = []
+    aliases = {}
+    if dq_buf is not None:
+        extra_specs = [pl.BlockSpec(memory_space=pl.ANY)]
+        extra_args = [dq_buf]
+        aliases = {4 + len(kv_args): 0}
     return pl.pallas_call(
         band_kernel,
         grid=(kv_heads,),
         in_specs=[
             pl.BlockSpec((tok_rows, 1), lambda g: (0, 0)),
             pl.BlockSpec((1, key_seg.shape[0]), lambda g: (0, 0)),
-            pl.BlockSpec((tok_rows, group_width), lambda g: (0, g)),
-            pl.BlockSpec((tok_rows, group_width), lambda g: (0, g)),
+            pl.BlockSpec((tok_rows, group_width), lambda g, f=first_kv: (0, f + g)),
+            pl.BlockSpec((tok_rows, group_width), lambda g, f=first_kv: (0, f + g)),
         ]
-        + kv_specs,
+        + kv_specs
+        + extra_specs,
         out_specs=[
-            pl.BlockSpec((tok_rows, group_width), lambda g: (0, g)),
+            pl.BlockSpec((tok_rows, group_width), lambda g, f=first_kv: (0, f + g)),
             pl.BlockSpec((tok_rows, 4 * HEAD_WIDTH), lambda g: (0, g)),
             pl.BlockSpec((tok_rows, 2 * HEAD_WIDTH), lambda g: (0, g)),
             pl.BlockSpec((tok_rows, 2 * HEAD_WIDTH), lambda g: (0, g)),
@@ -105,40 +113,69 @@
             jax.ShapeDtypeStruct((tok_rows, 2 * HEAD_WIDTH * kv_heads), jnp.float32),
             jax.ShapeDtypeStruct((tok_rows, 2 * HEAD_WIDTH * kv_heads), jnp.float32),
         ],
-    )(query_seg.reshape(tok_rows, 1), key_seg.reshape(1, -1), query_blk, grad_blk, *kv_args)
+        input_output_aliases=aliases,
+    )(
+        query_seg.reshape(tok_rows, 1),
+        key_seg.reshape(1, -1),
+        query_rows,
+        out_grad,
+        *kv_args,
+        *extra_args,
+    )
 
 
 def body(query_rows, key_rows, value_matrix, out_grad, segments):
     tok_rows = query_rows.shape[0]
     kv_width = key_rows.shape[1]
     kv_heads = kv_width // HEAD_WIDTH
+    halves = 2
+    half_heads = kv_heads // halves
+    half_width = half_heads * HEAD_WIDTH
     axes = ("ctx", "fsdp")
     position = lax.axis_index(axes)
     query_first = position * tok_rows
     window = SPAN * tok_rows
     seg_cols = jnp.broadcast_to(segments.astype(jnp.bfloat16)[:, None], (tok_rows, HEAD_WIDTH))
-    own = jnp.concatenate([key_rows, value_matrix, seg_cols], 1)
-    back_one = from_behind(own, axes, 1)
-    back_two = from_behind(own, axes, 2)
-    back_three = from_behind(back_two, axes, 1)
-    blocks = [back_three, back_two, back_one, own]
-    seg_win = jnp.concatenate([blk[:, 2 * kv_width] for blk in blocks], 0).astype(jnp.int32)
-    key_pos = query_first - window + jnp.arange(window + tok_rows, dtype=jnp.int32)
-    seg_win = jnp.where(key_pos >= 0, seg_win, -1)
-    dq_part, send, middle, own_part = band_grads(query_rows, out_grad, blocks, segments, seg_win)
-    received = from_behind(send, axes, -1).reshape(tok_rows, kv_heads, 2, 2 * HEAD_WIDTH)
-    middle = middle.reshape(tok_rows, kv_heads, 2 * HEAD_WIDTH)
-    forward = (middle + received[:, :, 0].astype(jnp.float32)).astype(jnp.bfloat16)
-    gathered = from_behind(forward, axes, -2)
-    total = (
-        own_part.reshape(tok_rows, kv_heads, 2 * HEAD_WIDTH)
-        + received[:, :, 1].astype(jnp.float32)
-        + gathered.astype(jnp.float32)
-    ).reshape(tok_rows, kv_heads, 2, HEAD_WIDTH)
+    dq_buf = None
+    previous = None
+    seg_win = None
+    key_parts = []
+    value_parts = []
+    for half in range(halves):
+        cols = slice(half * half_width, (half + 1) * half_width)
+        pieces = [key_rows[:, cols], value_matrix[:, cols]]
+        if half == 0:
+            pieces.append(seg_cols)
+        own = jnp.concatenate(pieces, 1)
+        if previous is not None:
+            own, previous = lax.optimization_barrier((own, previous))
+        back_one = from_behind(own, axes, 1)
+        back_two = from_behind(own, axes, 2)
+        back_three = from_behind(back_two, axes, 1)
+        blocks = [back_three, back_two, back_one, own]
+        previous = blocks
+        if seg_win is None:
+            seg_win = jnp.concatenate([blk[:, 2 * half_width] for blk in blocks], 0)
+            key_pos = query_first - window + jnp.arange(window + tok_rows, dtype=jnp.int32)
+            seg_win = jnp.where(key_pos >= 0, seg_win.astype(jnp.int32), -1)
+        dq_buf, send, middle, own_part = band_grads(
+            query_rows, out_grad, blocks, segments, seg_win, half * half_heads, half_heads, dq_buf
+        )
+        received = from_behind(send, axes, -1).reshape(tok_rows, half_heads, 2, 2 * HEAD_WIDTH)
+        middle = middle.reshape(tok_rows, half_heads, 2 * HEAD_WIDTH)
+        forward = (middle + received[:, :, 0].astype(jnp.float32)).astype(jnp.bfloat16)
+        gathered = from_behind(forward, axes, -2)
+        total = (
+            own_part.reshape(tok_rows, half_heads, 2 * HEAD_WIDTH)
+            + received[:, :, 1].astype(jnp.float32)
+            + gathered.astype(jnp.float32)
+        ).reshape(tok_rows, half_heads, 2, HEAD_WIDTH)
+        key_parts.append(total[:, :, 0].reshape(tok_rows, half_width).astype(jnp.bfloat16))
+        value_parts.append(total[:, :, 1].reshape(tok_rows, half_width).astype(jnp.bfloat16))
     return (
-        dq_part,
-        total[:, :, 0].reshape(tok_rows, kv_width).astype(jnp.bfloat16),
-        total[:, :, 1].reshape(tok_rows, kv_width).astype(jnp.bfloat16),
+        dq_buf,
+        jnp.concatenate(key_parts, 1),
+        jnp.concatenate(value_parts, 1),
     )
 
 

time: 96.4 us -> 112 us (1.16)
  the two profiles are of different devices: /device:TPU:56 before, /device:TPU:96 now
where the time goes in v4:
time: 112 us; the launch traced here: 111 us
  starting transfers between devices  44.9 us (40%)
  waiting for transfers between devices  31.1 us (28%)
  Pallas kernels  22.2 us (20%)
  local copies, waits for them, and re-layouts  8.58 us (8%)
  other arithmetic  3.44 us (3%)
    ppermute x10, starting transfers between devices, from_behind(): return lax.ppermute(block, axis, route)  44.9 us
    ppermute x10, waiting for transfers between devices, from_behind(): return lax.ppermute(block, axis, route)  31.1 us
    pallas_call x2, Pallas kernels, band_grads(): pl.pallas_call(band_kernel, grid=(kv_heads,), in_specs=[pl.BlockSpec((tok...  22.2 us
    unnamed x30, local copies, waits for them, and re-layouts  2.94 us
  transfers between devices with their start and end apart: 10, of which 5 were waited for; matrix products, arithmetic and copies ran while one was open for 3% of the time, Pallas kernels for 10%

profile of v4, /device:TPU:96, one launch (start us, length us, event | category | flops | bytes accessed | tf_op | source)
XLA Modules:
  0.0 111.2 jit_solution(10966744975511737783)
XLA Ops:
  0.6 0.7 fusion.10
  1.3 1.0 fusion.8
  2.2 0.1 broadcast_in_dim.10
  2.4 0.0 copy-start
  2.4 6.1 %collective-permute-start = (bf16[128,640]{1,0:T(8,128)(2,1)S(1)}, bf16[128,640]{1,0:T(8,128)(2,1)S(1)}, u32[]{:S(2)}, u32[]{:S(2)}) collective-permute-start(bf16[128,640]{1,0:T(8,128)(2,1)S(1)} %pad_maximum_fusion.refs_6_.refs_7_), channel_id=1, source_target_pairs={{0,2},{1,3},{2,4},{3,5},{4,6},{5,7},{6,8},{7,9},{8,10},{9,11},{10,... | collective-permute-start | bytes 491528 | tf_op jit(solution)/shard_map/ppermute | solution.py:17
  8.5 5.5 %collective-permute-start.2 = (bf16[128,640]{1,0:T(8,128)(2,1)S(1)}, bf16[128,640]{1,0:T(8,128)(2,1)S(1)}, u32[]{:S(2)}, u32[]{:S(2)}) collective-permute-start(bf16[128,640]{1,0:T(8,128)(2,1)S(1)} %pad_maximum_fusion.refs_6_.refs_7_), channel_id=1, source_target_pairs={{0,1},{1,2},{2,3},{3,4},{4,5},{5,6},{6,7},{7,8},{8,9},{9,10},{10,1... | collective-permute-start | bytes 491528 | tf_op jit(solution)/shard_map/ppermute | solution.py:17
  14.0 0.0 copy-start.12
  14.0 0.6 copy-done.12
  14.6 0.7 copy.20.seg_q_ref
  15.4 6.9 %collective-permute-done.refs_2_.refs_3_ = bf16[128,640]{1,0:T(8,128)(2,1)S(1)} collective-permute-done((bf16[128,640]{1,0:T(8,128)(2,1)S(1)}, bf16[128,640]{1,0:T(8,128)(2,1)S(1)}, u32[]{:S(2)}, u32[]{:S(2)}) %collective-permute-start) | collective-permute-done | bytes 163872 | tf_op jit(solution)/shard_map/ppermute | solution.py:17
  22.3 1.9 %collective-permute-start.1 = (bf16[128,640]{1,0:T(8,128)(2,1)S(1)}, bf16[128,640]{1,0:T(8,128)(2,1)S(1)}, u32[]{:S(2)}, u32[]{:S(2)}) collective-permute-start(bf16[128,640]{1,0:T(8,128)(2,1)S(1)} %collective-permute-done.refs_2_.refs_3_), channel_id=1, source_target_pairs={{0,1},{1,2},{2,3},{3,4},{4,5},{5,6},{6,7},{7,8},{8,9},{9,10},{10,1... | collective-permute-start | bytes 491528 | tf_op jit(solution)/shard_map/ppermute | solution.py:17
  24.2 0.1 slice_reduce_fusion.5
  24.3 0.0 collective-permute-done.2.refs_4_.refs_5_
  24.3 0.0 copy-start.3
  24.4 0.1 slice_reduce_fusion.4
  24.5 5.0 %collective-permute-done.1.refs_0_.refs_1_ = bf16[128,640]{1,0:T(8,128)(2,1)S(1)} collective-permute-done((bf16[128,640]{1,0:T(8,128)(2,1)S(1)}, bf16[128,640]{1,0:T(8,128)(2,1)S(1)}, u32[]{:S(2)}, u32[]{:S(2)}) %collective-permute-start.1) | collective-permute-done | bytes 163872 | tf_op jit(solution)/shard_map/ppermute | solution.py:17
  29.5 0.1 slice_reduce_fusion.6
  29.6 0.6 compare_select_fusion.seg_k_ref
  30.2 0.0 copy-done
  30.2 0.0 copy-done.2
  30.2 0.0 copy-done.3
  30.2 0.0 copy-done.4
  30.2 11.1 %shard_map.76 = (bf16[128,4096]{1,0:T(8,128)(2,1)}, bf16[128,1024]{1,0:T(8,128)(2,1)}, f32[128,512]{1,0:T(8,128)}, f32[128,512]{1,0:T(8,128)}) custom-call(s32[128,1]{1,0:T(8,128)} %copy.20.seg_q_ref, s32[1,512]{1,0:T(1,128)} %compare_select_fusion.seg_k_ref, bf16[128,4096]{1,0:T(8,128)(2,1)} %query_ref.3, bf16[128,4096]{1,0:T(8,128)(2,1)} %grad_ref.3, ...), custom_call_target="tpu_custom_call" | custom-call | tf_op jit(solution)/shard_map/pallas_call | solution.py:93
  41.3 0.0 copy-start.9
  41.3 6.1 %collective-permute-start.6 = (bf16[128,1024]{1,0:T(8,128)(2,1)}, bf16[128,1024]{1,0:T(8,128)(2,1)S(1)}, u32[]{:S(2)}, u32[]{:S(2)}) collective-permute-start(bf16[128,1024]{1,0:T(8,128)(2,1)} %get-tuple-element.16), channel_id=1, source_target_pairs={{1,0},{2,1},{3,2},{4,3},{5,4},{6,5},{7,6},{8,7},{9,8},{10,9},{11,1... | collective-permute-start | bytes 786440 | tf_op jit(solution)/shard_map/ppermute | solution.py:17
  47.4 0.0 copy-start.1
  47.4 1.9 %collective-permute-start.3 = (bf16[128,512]{1,0:T(8,128)(2,1)S(1)}, bf16[128,512]{1,0:T(8,128)(2,1)S(1)}, u32[]{:S(2)}, u32[]{:S(2)}) collective-permute-start(bf16[128,512]{1,0:T(8,128)(2,1)S(1)} %pad_maximum_fusion.1.refs_6_.refs_7_), channel_id=1, source_target_pairs={{0,2},{1,3},{2,4},{3,5},{4,6},{5,7},{6,8},{7,9},{8,10},{9,11},{10,... | collective-permute-start | bytes 393224 | tf_op jit(solution)/shard_map/ppermute | solution.py:17
  49.3 1.9 %collective-permute-start.5 = (bf16[128,512]{1,0:T(8,128)(2,1)S(1)}, bf16[128,512]{1,0:T(8,128)(2,1)S(1)}, u32[]{:S(2)}, u32[]{:S(2)}) collective-permute-start(bf16[128,512]{1,0:T(8,128)(2,1)S(1)} %pad_maximum_fusion.1.refs_6_.refs_7_), channel_id=1, source_target_pairs={{0,1},{1,2},{2,3},{3,4},{4,5},{5,6},{6,7},{7,8},{8,9},{9,10},{10,1... | collective-permute-start | bytes 393224 | tf_op jit(solution)/shard_map/ppermute | solution.py:17
  51.3 0.0 copy-done.9
  51.3 0.2 reshape.124
  51.5 8.6 %collective-permute-done.3.refs_2_.refs_3_ = bf16[128,512]{1,0:T(8,128)(2,1)S(1)} collective-permute-done((bf16[128,512]{1,0:T(8,128)(2,1)S(1)}, bf16[128,512]{1,0:T(8,128)(2,1)S(1)}, u32[]{:S(2)}, u32[]{:S(2)}) %collective-permute-start.3) | collective-permute-done | bytes 131104 | tf_op jit(solution)/shard_map/ppermute | solution.py:17
  60.0 1.9 %collective-permute-start.4 = (bf16[128,512]{1,0:T(8,128)(2,1)S(1)}, bf16[128,512]{1,0:T(8,128)(2,1)S(1)}, u32[]{:S(2)}, u32[]{:S(2)}) collective-permute-start(bf16[128,512]{1,0:T(8,128)(2,1)S(1)} %collective-permute-done.3.refs_2_.refs_3_), channel_id=1, source_target_pairs={{0,1},{1,2},{2,3},{3,4},{4,5},{5,6},{6,7},{7,8},{8,9},{9,10},{10,1... | collective-permute-start | bytes 393224 | tf_op jit(solution)/shard_map/ppermute | solution.py:17
  62.0 0.0 collective-permute-done.6
  62.0 0.2 reshape.123
  62.2 0.4 fusion.6
  62.5 0.2 fusion.3
  62.7 13.1 %collective-permute-start.7 = (bf16[128,2,256]{2,1,0:T(2,128)(2,1)S(1)}, bf16[128,2,256]{2,1,0:T(2,128)(2,1)S(1)}, u32[]{:S(2)}, u32[]{:S(2)}) collective-permute-start(bf16[128,2,256]{2,1,0:T(2,128)(2,1)S(1)} %fusion.3), channel_id=1, source_target_pairs={{2,0},{3,1},{4,2},{5,3},{6,4},{7,5},{8,6},{9,7},{10,8},{11,9},{12,... | collective-permute-start | bytes 393224 | tf_op jit(solution)/shard_map/ppermute | solution.py:17
  75.8 0.0 collective-permute-done.5.refs_4_.refs_5_
  75.9 0.0 collective-permute-done.4.refs_0_.refs_1_
  75.9 0.0 copy-start.7
  75.9 0.6 copy-done.6
  76.5 0.0 copy-done.7
  76.5 11.1 %shard_map.77 = (bf16[128,4096]{1,0:T(8,128)(2,1)}, bf16[128,1024]{1,0:T(8,128)(2,1)}, f32[128,512]{1,0:T(8,128)}, f32[128,512]{1,0:T(8,128)}) custom-call(s32[128,1]{1,0:T(8,128)} %copy.20.seg_q_ref, s32[1,512]{1,0:T(1,128)} %compare_select_fusion.seg_k_ref, bf16[128,4096]{1,0:T(8,128)(2,1)} %query_ref.3, ...), custom_call_target="tpu_custom_call", output_to_operand_aliasing={{0}: (12, {})} | custom-call | tf_op jit(solution)/shard_map/pallas_call | solution.py:93
  87.6 2.4 %collective-permute-start.8 = (bf16[128,1024]{1,0:T(8,128)(2,1)}, bf16[128,1024]{1,0:T(8,128)(2,1)S(1)}, u32[]{:S(2)}, u32[]{:S(2)}) collective-permute-start(bf16[128,1024]{1,0:T(8,128)(2,1)} %get-tuple-element.19), channel_id=1, source_target_pairs={{1,0},{2,1},{3,2},{4,3},{5,4},{6,5},{7,6},{8,7},{9,8},{10,9},{11,1... | collective-permute-start | bytes 786440 | tf_op jit(solution)/shard_map/ppermute | solution.py:17
  90.0 0.2 reshape.122
  90.2 0.8 copy-done.11
  91.0 0.2 reshape.128
  91.1 0.8 copy-done.10
  91.9 0.2 reshape.126
  92.1 0.0 collective-permute-done.7
  92.1 0.2 fusion.5
  92.3 0.1 reshape.132
  92.4 6.4 %collective-permute-done.8 = bf16[128,1024]{1,0:T(8,128)(2,1)S(1)} collective-permute-done((bf16[128,1024]{1,0:T(8,128)(2,1)}, bf16[128,1024]{1,0:T(8,128)(2,1)S(1)}, u32[]{:S(2)}, u32[]{:S(2)}) %collective-permute-start.8) | collective-permute-done | bytes 262176 | tf_op jit(solution)/shard_map/ppermute | solution.py:17
  98.8 0.2 reshape.127
  99.0 0.4 fusion.7
  99.4 0.2 fusion
  99.5 4.1 %collective-permute-start.9 = (bf16[128,2,256]{2,1,0:T(2,128)(2,1)S(1)}, bf16[128,2,256]{2,1,0:T(2,128)(2,1)S(1)}, u32[]{:S(2)}, u32[]{:S(2)}) collective-permute-start(bf16[128,2,256]{2,1,0:T(2,128)(2,1)S(1)} %fusion), channel_id=1, source_target_pairs={{2,0},{3,1},{4,2},{5,3},{6,4},{7,5},{8,6},{9,7},{10,8},{11,9},{12,... | collective-permute-start | bytes 393224 | tf_op jit(solution)/shard_map/ppermute | solution.py:17
  103.6 0.8 slice_reduce_fusion.1
  104.5 4.2 %collective-permute-done.9 = bf16[128,2,256]{2,1,0:T(2,128)(2,1)S(1)} collective-permute-done((bf16[128,2,256]{2,1,0:T(2,128)(2,1)S(1)}, bf16[128,2,256]{2,1,0:T(2,128)(2,1)S(1)}, u32[]{:S(2)}, u32[]{:S(2)}) %collective-permute-start.9) | collective-permute-done | bytes 131104 | tf_op jit(solution)/shard_map/ppermute | solution.py:17
  108.7 0.2 fusion.2
  108.9 0.1 reshape.135
  109.0 0.8 slice_reduce_fusion
  109.9 0.7 pad_maximum_fusion.3
  110.6 0.7 pad_maximum_fusion.2
  (16 shorter events, 0.1 us)
Async XLA Ops:
  2.4 27.9 %copy-start = (bf16[128,640]{1,0:T(8,128)(2,1)}, bf16[128,640]{1,0:T(8,128)(2,1)S(1)}, u32[]{:S(2)}) copy-start(bf16[128,640]{1,0:T(8,128)(2,1)S(1)} %pad_maximum_fusion.refs_6_.refs_7_) | copy-start | bytes 491524
  2.4 19.9 %collective-permute-start = (bf16[128,640]{1,0:T(8,128)(2,1)S(1)}, bf16[128,640]{1,0:T(8,128)(2,1)S(1)}, u32[]{:S(2)}, u32[]{:S(2)}) collective-permute-start(bf16[128,640]{1,0:T(8,128)(2,1)S(1)} %pad_maximum_fusion.refs_6_.refs_7_), channel_id=1, source_target_pairs={{0,2},{1,3},{2,4},{3,5},{4,6},{5,7},{6,8},{7,9},{8,10},{9,11},{10,... | collective-permute-start | bytes 491528 | tf_op jit(solution)/shard_map/ppermute | solution.py:17
  8.5 15.9 %collective-permute-start.2 = (bf16[128,640]{1,0:T(8,128)(2,1)S(1)}, bf16[128,640]{1,0:T(8,128)(2,1)S(1)}, u32[]{:S(2)}, u32[]{:S(2)}) collective-permute-start(bf16[128,640]{1,0:T(8,128)(2,1)S(1)} %pad_maximum_fusion.refs_6_.refs_7_), channel_id=1, source_target_pairs={{0,1},{1,2},{2,3},{3,4},{4,5},{5,6},{6,7},{7,8},{8,9},{9,10},{10,1... | collective-permute-start | bytes 491528 | tf_op jit(solution)/shard_map/ppermute | solution.py:17
  14.0 0.7 copy-start.12
  22.3 7.9 %copy-start.2 = (bf16[128,640]{1,0:T(8,128)(2,1)}, bf16[128,640]{1,0:T(8,128)(2,1)S(1)}, u32[]{:S(2)}) copy-start(bf16[128,640]{1,0:T(8,128)(2,1)S(1)} %collective-permute-done.refs_2_.refs_3_) | copy-start | bytes 491524
  22.3 7.2 %collective-permute-start.1 = (bf16[128,640]{1,0:T(8,128)(2,1)S(1)}, bf16[128,640]{1,0:T(8,128)(2,1)S(1)}, u32[]{:S(2)}, u32[]{:S(2)}) collective-permute-start(bf16[128,640]{1,0:T(8,128)(2,1)S(1)} %collective-permute-done.refs_2_.refs_3_), channel_id=1, source_target_pairs={{0,1},{1,2},{2,3},{3,4},{4,5},{5,6},{6,7},{7,8},{8,9},{9,10},{10,1... | collective-permute-start | bytes 491528 | tf_op jit(solution)/shard_map/ppermute | solution.py:17
  24.3 5.9 %copy-start.3 = (bf16[128,640]{1,0:T(8,128)(2,1)}, bf16[128,640]{1,0:T(8,128)(2,1)S(1)}, u32[]{:S(2)}) copy-start(bf16[128,640]{1,0:T(8,128)(2,1)S(1)} %collective-permute-done.2.refs_4_.refs_5_) | copy-start | bytes 491524
  29.5 0.7 copy-start.4
  41.3 10.0 %copy-start.9 = (f32[128,512]{1,0:T(8,128)S(1)}, f32[128,512]{1,0:T(8,128)}, u32[]{:S(2)}) copy-start(f32[128,512]{1,0:T(8,128)} %get-tuple-element.17) | copy-start | bytes 786436
  41.3 20.6 %collective-permute-start.6 = (bf16[128,1024]{1,0:T(8,128)(2,1)}, bf16[128,1024]{1,0:T(8,128)(2,1)S(1)}, u32[]{:S(2)}, u32[]{:S(2)}) collective-permute-start(bf16[128,1024]{1,0:T(8,128)(2,1)} %get-tuple-element.16), channel_id=1, source_target_pairs={{1,0},{2,1},{3,2},{4,3},{5,4},{6,5},{7,6},{8,7},{9,8},{10,9},{11,1... | collective-permute-start | bytes 786440 | tf_op jit(solution)/shard_map/ppermute | solution.py:17
  47.4 4.1 %copy-start.1 = (bf16[128,512]{1,0:T(8,128)(2,1)}, bf16[128,512]{1,0:T(8,128)(2,1)S(1)}, u32[]{:S(2)}) copy-start(bf16[128,512]{1,0:T(8,128)(2,1)S(1)} %pad_maximum_fusion.1.refs_6_.refs_7_) | copy-start | bytes 393220
  47.4 12.6 %collective-permute-start.3 = (bf16[128,512]{1,0:T(8,128)(2,1)S(1)}, bf16[128,512]{1,0:T(8,128)(2,1)S(1)}, u32[]{:S(2)}, u32[]{:S(2)}) collective-permute-start(bf16[128,512]{1,0:T(8,128)(2,1)S(1)} %pad_maximum_fusion.1.refs_6_.refs_7_), channel_id=1, source_target_pairs={{0,2},{1,3},{2,4},{3,5},{4,6},{5,7},{6,8},{7,9},{8,10},{9,11},{10,... | collective-permute-start | bytes 393224 | tf_op jit(solution)/shard_map/ppermute | solution.py:17
  49.3 26.5 %collective-permute-start.5 = (bf16[128,512]{1,0:T(8,128)(2,1)S(1)}, bf16[128,512]{1,0:T(8,128)(2,1)S(1)}, u32[]{:S(2)}, u32[]{:S(2)}) collective-permute-start(bf16[128,512]{1,0:T(8,128)(2,1)S(1)} %pad_maximum_fusion.1.refs_6_.refs_7_), channel_id=1, source_target_pairs={{0,1},{1,2},{2,3},{3,4},{4,5},{5,6},{6,7},{7,8},{8,9},{9,10},{10,1... | collective-permute-start | bytes 393224 | tf_op jit(solution)/shard_map/ppermute | solution.py:17
  60.0 2.1 %copy-start.5 = (bf16[128,512]{1,0:T(8,128)(2,1)}, bf16[128,512]{1,0:T(8,128)(2,1)S(1)}, u32[]{:S(2)}) copy-start(bf16[128,512]{1,0:T(8,128)(2,1)S(1)} %collective-permute-done.3.refs_2_.refs_3_) | copy-start | bytes 393220
  60.0 15.8 %collective-permute-start.4 = (bf16[128,512]{1,0:T(8,128)(2,1)S(1)}, bf16[128,512]{1,0:T(8,128)(2,1)S(1)}, u32[]{:S(2)}, u32[]{:S(2)}) collective-permute-start(bf16[128,512]{1,0:T(8,128)(2,1)S(1)} %collective-permute-done.3.refs_2_.refs_3_), channel_id=1, source_target_pairs={{0,1},{1,2},{2,3},{3,4},{4,5},{5,6},{6,7},{7,8},{8,9},{9,10},{10,1... | collective-permute-start | bytes 393224 | tf_op jit(solution)/shard_map/ppermute | solution.py:17
  62.7 29.4 %collective-permute-start.7 = (bf16[128,2,256]{2,1,0:T(2,128)(2,1)S(1)}, bf16[128,2,256]{2,1,0:T(2,128)(2,1)S(1)}, u32[]{:S(2)}, u32[]{:S(2)}) collective-permute-start(bf16[128,2,256]{2,1,0:T(2,128)(2,1)S(1)} %fusion.3), channel_id=1, source_target_pairs={{2,0},{3,1},{4,2},{5,3},{6,4},{7,5},{8,6},{9,7},{10,8},{11,9},{12,... | collective-permute-start | bytes 393224 | tf_op jit(solution)/shard_map/ppermute | solution.py:17
  75.8 0.7 copy-start.6
  75.9 0.7 copy-start.7
  76.5 13.5 %copy-start.8 = (f32[128,512]{1,0:T(8,128)S(1)}, f32[128,512]{1,0:T(8,128)}, u32[]{:S(2)}) copy-start(f32[128,512]{1,0:T(8,128)} %get-tuple-element.15) | copy-start | bytes 786436
  87.6 11.2 %collective-permute-start.8 = (bf16[128,1024]{1,0:T(8,128)(2,1)}, bf16[128,1024]{1,0:T(8,128)(2,1)S(1)}, u32[]{:S(2)}, u32[]{:S(2)}) collective-permute-start(bf16[128,1024]{1,0:T(8,128)(2,1)} %get-tuple-element.19), channel_id=1, source_target_pairs={{1,0},{2,1},{3,2},{4,3},{5,4},{6,5},{7,6},{8,7},{9,8},{10,9},{11,1... | collective-permute-start | bytes 786440 | tf_op jit(solution)/shard_map/ppermute | solution.py:17
  90.0 1.0 copy-start.11
  91.0 0.9 copy-start.10
  99.5 9.2 %collective-permute-start.9 = (bf16[128,2,256]{2,1,0:T(2,128)(2,1)S(1)}, bf16[128,2,256]{2,1,0:T(2,128)(2,1)S(1)}, u32[]{:S(2)}, u32[]{:S(2)}) collective-permute-start(bf16[128,2,256]{2,1,0:T(2,128)(2,1)S(1)} %fusion), channel_id=1, source_target_pairs={{2,0},{3,1},{4,2},{5,3},{6,4},{7,5},{8,6},{9,7},{10,8},{11,9},{12,... | collective-permute-start | bytes 393224 | tf_op jit(solution)/shard_map/ppermute | solution.py:17

commit v5 on v3

v5 whole, which is shorter than its diff:
```python
import math

import jax
import jax.numpy as jnp
from jax import lax
from jax.experimental import pallas as pl
from jax.sharding import PartitionSpec as P

HEAD_WIDTH = 128
SPAN = 3


def from_behind(block, axis, distance):
    devices = range(lax.axis_size(axis))
    route = [(i - distance, i) for i in devices if i - distance in devices]
    return lax.ppermute(block, axis, route)


def band_kernel(query_ref, grad_ref, *refs):
    key_refs = refs[0:12:3]
    value_refs = refs[1:12:3]
    seg_refs = refs[2:12:3]
    dq_ref, send_ref, middle_ref, own_ref = refs[12:]
    tok_rows = query_ref.shape[0]
    key_count = tok_rows * len(key_refs)
    heads_per_group = query_ref.shape[1] // HEAD_WIDTH
    inv_root = 1.0 / math.sqrt(HEAD_WIDTH)
    window = key_count - tok_rows
    position = lax.axis_index(("ctx", "fsdp"))
    seg_q = seg_refs[-1][:, 0:1].astype(jnp.float32)
    seg_k = jnp.concatenate(
        [jnp.transpose(ref[...].astype(jnp.float32))[0:1] for ref in seg_refs], 1
    )
    row = lax.broadcasted_iota(jnp.int32, (tok_rows, key_count), 0)
    col = lax.broadcasted_iota(jnp.int32, (tok_rows, key_count), 1)
    allowed = (col > row) & (col <= row + window) & (col >= window - position * tok_rows)
    allowed = allowed & (seg_k == seg_q)
    k_head = jnp.concatenate([ref[...] for ref in key_refs], 0)
    v_head = jnp.concatenate([ref[...] for ref in value_refs], 0)
    key_acc = jnp.zeros((key_count, HEAD_WIDTH), jnp.float32)
    value_acc = jnp.zeros((key_count, HEAD_WIDTH), jnp.float32)
    for head in range(heads_per_group):
        cols = slice(head * HEAD_WIDTH, (head + 1) * HEAD_WIDTH)
        q_head = query_ref[:, cols]
        o_grad = grad_ref[:, cols]
        scores = lax.dot_general(
            q_head, k_head, (((1,), (1,)), ((), ())), preferred_element_type=jnp.float32
        )
        scores = jnp.where(allowed, scores * inv_root, -1e30)
        row_max = jnp.max(scores, axis=1, keepdims=True)
        weights = jnp.exp(scores - row_max)
        probs = weights * (1.0 / jnp.sum(weights, axis=1, keepdims=True))
        prob_grad = lax.dot_general(
            o_grad, v_head, (((1,), (1,)), ((), ())), preferred_element_type=jnp.float32
        )
        row_delta = jnp.sum(probs * prob_grad, axis=1, keepdims=True)
        score_grad = (probs * (prob_grad - row_delta) * inv_root).astype(jnp.bfloat16)
        probs_low = probs.astype(jnp.bfloat16)
        dq_ref[:, cols] = jnp.dot(
            score_grad, k_head, preferred_element_type=jnp.float32
        ).astype(jnp.bfloat16)
        key_acc = key_acc + lax.dot_general(
            score_grad, q_head, (((0,), (0,)), ((), ())), preferred_element_type=jnp.float32
        )
        value_acc = value_acc + lax.dot_general(
            probs_low, o_grad, (((0,), (0,)), ((), ())), preferred_element_type=jnp.float32
        )

    def rows(block):
        return slice(block * tok_rows, (block + 1) * tok_rows)

    for slot, block in enumerate((0, 2)):
        send_ref[slot, 0] = key_acc[rows(block)].astype(jnp.bfloat16)
        send_ref[slot, 1] = value_acc[rows(block)].astype(jnp.bfloat16)
    middle_ref[0] = key_acc[rows(1)]
    middle_ref[1] = value_acc[rows(1)]
    own_ref[0] = key_acc[rows(3)]
    own_ref[1] = value_acc[rows(3)]


def band_grads(query_blk, grad_blk, blocks, kv_heads):
    tok_rows, q_width = query_blk.shape
    kv_width = kv_heads * HEAD_WIDTH
    group_width = q_width // kv_heads
    kv_specs = []
    kv_args = []
    for blk in blocks:
        kv_specs.append(pl.BlockSpec((tok_rows, HEAD_WIDTH), lambda g: (0, g)))
        kv_specs.append(pl.BlockSpec((tok_rows, HEAD_WIDTH), lambda g, n=kv_heads: (0, n + g)))
        kv_specs.append(pl.BlockSpec((tok_rows, HEAD_WIDTH), lambda g, n=kv_heads: (0, 2 * n)))
        kv_args += [blk, blk, blk]
    return pl.pallas_call(
        band_kernel,
        grid=(kv_heads,),
        in_specs=[
            pl.BlockSpec((tok_rows, group_width), lambda g: (0, g)),
            pl.BlockSpec((tok_rows, group_width), lambda g: (0, g)),
        ]
        + kv_specs,
        out_specs=[
            pl.BlockSpec((tok_rows, group_width), lambda g: (0, g)),
            pl.BlockSpec((2, 2, tok_rows, HEAD_WIDTH), lambda g: (0, 0, 0, g)),
            pl.BlockSpec((2, tok_rows, HEAD_WIDTH), lambda g: (0, 0, g)),
            pl.BlockSpec((2, tok_rows, HEAD_WIDTH), lambda g: (0, 0, g)),
        ],
        out_shape=[
            jax.ShapeDtypeStruct((tok_rows, q_width), jnp.bfloat16),
            jax.ShapeDtypeStruct((2, 2, tok_rows, kv_width), jnp.bfloat16),
            jax.ShapeDtypeStruct((2, tok_rows, kv_width), jnp.float32),
            jax.ShapeDtypeStruct((2, tok_rows, kv_width), jnp.float32),
        ],
    )(query_blk, grad_blk, *kv_args)


def body(query_rows, key_rows, value_matrix, out_grad, segments):
    tok_rows = query_rows.shape[0]
    kv_width = key_rows.shape[1]
    kv_heads = kv_width // HEAD_WIDTH
    axes = ("ctx", "fsdp")
    seg_cols = jnp.broadcast_to(segments.astype(jnp.bfloat16)[:, None], (tok_rows, HEAD_WIDTH))
    own = jnp.concatenate([key_rows, value_matrix, seg_cols], 1)
    back_one = from_behind(own, axes, 1)
    back_two = from_behind(own, axes, 2)
    back_three = from_behind(back_two, axes, 1)
    blocks = [back_three, back_two, back_one, own]
    dq_part, send, middle, own_part = band_grads(query_rows, out_grad, blocks, kv_heads)
    received = from_behind(send, axes, -1)
    forward = (middle + received[0].astype(jnp.float32)).astype(jnp.bfloat16)
    gathered = from_behind(forward, axes, -2)
    total = own_part + received[1].astype(jnp.float32) + gathered.astype(jnp.float32)
    return (
        dq_part,
        total[0].astype(jnp.bfloat16),
        total[1].astype(jnp.bfloat16),
    )


def solution(mesh):
    return jax.shard_map(
        body,
        mesh=mesh,
        in_specs=(
            P(("ctx", "fsdp"), None),
            P(("ctx", "fsdp"), None),
            P(("ctx", "fsdp"), None),
            P(("ctx", "fsdp"), None),
            P(("ctx", "fsdp")),
        ),
        out_specs=(P(("ctx", "fsdp"), None), P(("ctx", "fsdp"), None), P(("ctx", "fsdp"), None)),
        check_vma=False,
    )
```

time: 96.4 us -> 94.5 us (0.980)
  local copies, waits for them, and re-layouts: 6.73 us -> 1.53 us
  waiting for transfers between devices: 32.5 us -> 35.7 us
    ppermute x5, waiting for transfers between devices: 32.5 us -> 35.7 us  [from_behind(): return lax.ppermute(block, axis, route)]
    reshape x4 -> x0, local copies, waits for them, and re-layouts: 2.64 us -> none  [the longest x1 1.28 us: body(): middle = middle.reshape(tok_rows, kv_heads, 2 * HEAD_WIDTH)]
    slice x5 -> x0, local copies, waits for them, and re-layouts: 2.51 us -> none  [the longest x1 1.47 us: body(): total[:, :, 1].reshape(tok_rows, kv_width).astype(jnp.bfloat16)]
  transfers between devices with their start and end apart: 5 -> 5, of which waited for: 4 -> 4; matrix products, arithmetic and copies ran while one was open for 3% -> 0% of each run, Pallas kernels for 0% -> 0%
where the time goes in v5:
time: 94.5 us; the launch traced here: 94.2 us
  waiting for transfers between devices  35.7 us (38%)
  starting transfers between devices  33.2 us (35%)
  Pallas kernels  20.2 us (21%)
  other arithmetic  2.94 us (3%)
  local copies, waits for them, and re-layouts  1.53 us (2%)
    ppermute x5, waiting for transfers between devices, from_behind(): return lax.ppermute(block, axis, route)  35.7 us
    ppermute x5, starting transfers between devices, from_behind(): return lax.ppermute(block, axis, route)  33.2 us
    pallas_call x1, Pallas kernels, band_grads(): pl.pallas_call(band_kernel, grid=(kv_heads,), in_specs=[pl.BlockSpec((tok...  20.2 us
  transfers between devices with their start and end apart: 5, of which 4 were waited for; matrix products, arithmetic and copies ran while one was open for 0% of the time, Pallas kernels for 0%

profile of v5, /device:TPU:56, one launch (start us, length us, event | category | flops | bytes accessed | tf_op | source)
XLA Modules:
  0.0 94.2 jit_solution(4124117863892154052)
XLA Ops:
  0.6 0.7 convert_element_type.29
  1.3 0.1 broadcast_in_dim.2
  1.4 1.0 %pad_maximum_fusion.refs_9_.refs_10_.refs_11_ = bf16[128,1152]{1,0:T(8,128)(2,1)S(1)} fusion(bf16[128,128]{1,0:T(8,128)(2,1)S(1)} %broadcast_in_dim.2, bf16[128,512]{1,0:T(8,128)(2,1)} %param.7, bf16[128,512]{1,0:T(8,128)(2,1)} %param.6), kind=kLoop, calls=%fused_computation.5 | loop fusion | flops 884736 | bytes 589824 | tf_op jit(solution)/shard_map/concatenate | solution.py:121
  2.4 0.0 copy-start
  2.4 6.1 %collective-permute-start = (bf16[128,1152]{1,0:T(8,128)(2,1)S(1)}, bf16[128,1152]{1,0:T(8,128)(2,1)S(1)}, u32[]{:S(2)}, u32[]{:S(2)}) collective-permute-start(bf16[128,1152]{1,0:T(8,128)(2,1)S(1)} %pad_maximum_fusion.refs_9_.refs_10_.refs_11_), channel_id=1, source_target_pairs={{0,2},{1,3},{2,4},{3,5},{4,6},{5,7},{6,8},{7,9},{8,10},{9,11},{10,... | collective-permute-start | bytes 884744 | tf_op jit(solution)/shard_map/ppermute | solution.py:16
  8.5 4.3 %collective-permute-start.2 = (bf16[128,1152]{1,0:T(8,128)(2,1)S(1)}, bf16[128,1152]{1,0:T(8,128)(2,1)S(1)}, u32[]{:S(2)}, u32[]{:S(2)}) collective-permute-start(bf16[128,1152]{1,0:T(8,128)(2,1)S(1)} %pad_maximum_fusion.refs_9_.refs_10_.refs_11_), channel_id=1, source_target_pairs={{0,1},{1,2},{2,3},{3,4},{4,5},{5,6},{6,7},{7,8},{8,9},{9,10},{10,1... | collective-permute-start | bytes 884744 | tf_op jit(solution)/shard_map/ppermute | solution.py:16
  12.8 11.2 %collective-permute-done.refs_3_.refs_4_.refs_5_ = bf16[128,1152]{1,0:T(8,128)(2,1)S(1)} collective-permute-done((bf16[128,1152]{1,0:T(8,128)(2,1)S(1)}, bf16[128,1152]{1,0:T(8,128)(2,1)S(1)}, u32[]{:S(2)}, u32[]{:S(2)}) %collective-permute-start) | collective-permute-done | bytes 294944 | tf_op jit(solution)/shard_map/ppermute | solution.py:16
  23.9 0.0 copy-start.1
  23.9 6.5 %collective-permute-start.1 = (bf16[128,1152]{1,0:T(8,128)(2,1)S(1)}, bf16[128,1152]{1,0:T(8,128)(2,1)S(1)}, u32[]{:S(2)}, u32[]{:S(2)}) collective-permute-start(bf16[128,1152]{1,0:T(8,128)(2,1)S(1)} %collective-permute-done.refs_3_.refs_4_.refs_5_), channel_id=1, source_target_pairs={{0,1},{1,2},{2,3},{3,4},{4,5},{5,6},{6,7},{7,8},{8,9},{9,10},{10,1... | collective-permute-start | bytes 884744 | tf_op jit(solution)/shard_map/ppermute | solution.py:16
  30.4 0.0 collective-permute-done.2.refs_6_.refs_7_.refs_8_
  30.4 0.0 copy-start.2
  30.4 11.4 %collective-permute-done.1.refs_0_.refs_1_.refs_2_ = bf16[128,1152]{1,0:T(8,128)(2,1)S(1)} collective-permute-done((bf16[128,1152]{1,0:T(8,128)(2,1)S(1)}, bf16[128,1152]{1,0:T(8,128)(2,1)S(1)}, u32[]{:S(2)}, u32[]{:S(2)}) %collective-permute-start.1) | collective-permute-done | bytes 294944 | tf_op jit(solution)/shard_map/ppermute | solution.py:16
  41.8 0.0 copy-done
  41.8 0.0 copy-done.1
  41.8 0.0 copy-done.2
  41.8 0.0 copy-start.3
  41.8 0.7 copy-done.3
  42.5 20.2 %shard_map.76 = (bf16[128,4096]{1,0:T(8,128)(2,1)}, bf16[2,2,128,512]{3,2,1,0:T(8,128)(2,1)}, f32[2,128,512]{2,1,0:T(8,128)}, f32[2,128,512]{2,1,0:T(8,128)}) custom-call(bf16[128,4096]{1,0:T(8,128)(2,1)} %query_ref.1, bf16[128,4096]{1,0:T(8,128)(2,1)} %grad_ref.1, bf16[128,1152]{1,0:T(8,128)(2,1)} %copy-done.3, bf16[128,1152]{1,0:T(8,128)(2,1)} %copy-done.3, ...), custom_call_target="tpu_custom_call" | custom-call | tf_op jit(solution)/shard_map/pallas_call | solution.py:92
  62.7 5.5 %collective-permute-start.3 = (bf16[2,2,128,512]{3,2,1,0:T(8,128)(2,1)}, bf16[2,2,128,512]{3,2,1,0:T(8,128)(2,1)S(1)}, u32[]{:S(2)}, u32[]{:S(2)}) collective-permute-start(bf16[2,2,128,512]{3,2,1,0:T(8,128)(2,1)} %get-tuple-element.9), channel_id=1, source_target_pairs={{1,0},{2,1},{3,2},{4,3},{5,4},{6,5},{7,6},{8,7},{9,8},{10,9},{11,1... | collective-permute-start | bytes 1572872 | tf_op jit(solution)/shard_map/ppermute | solution.py:16
  68.2 7.0 %collective-permute-done.3 = bf16[2,2,128,512]{3,2,1,0:T(8,128)(2,1)S(1)} collective-permute-done((bf16[2,2,128,512]{3,2,1,0:T(8,128)(2,1)}, bf16[2,2,128,512]{3,2,1,0:T(8,128)(2,1)S(1)}, u32[]{:S(2)}, u32[]{:S(2)}) %collective-permute-start.3) | collective-permute-done | bytes 524320 | tf_op jit(solution)/shard_map/ppermute | solution.py:16
  75.2 0.0 copy-start.4
  75.2 1.2 %fusion = bf16[2,128,512]{2,1,0:T(8,128)(2,1)S(1)} fusion(f32[2,128,512]{2,1,0:T(8,128)} %get-tuple-element.10, bf16[2,2,128,512]{3,2,1,0:T(8,128)(2,1)S(1)} %collective-permute-done.3), kind=kLoop, calls=%fused_computation.1 | loop fusion | flops 393216 | bytes 1048576 | tf_op jit(solution)/shard_map/convert_element_type | solution.py:128
  76.4 10.9 %collective-permute-start.4 = (bf16[2,128,512]{2,1,0:T(8,128)(2,1)S(1)}, bf16[2,128,512]{2,1,0:T(8,128)(2,1)S(1)}, u32[]{:S(2)}, u32[]{:S(2)}) collective-permute-start(bf16[2,128,512]{2,1,0:T(8,128)(2,1)S(1)} %fusion), channel_id=1, source_target_pairs={{2,0},{3,1},{4,2},{5,3},{6,4},{7,5},{8,6},{9,7},{10,8},{11,9},{12,... | collective-permute-start | bytes 786440 | tf_op jit(solution)/shard_map/ppermute | solution.py:16
  87.3 6.1 %collective-permute-done.4 = bf16[2,128,512]{2,1,0:T(8,128)(2,1)S(1)} collective-permute-done((bf16[2,128,512]{2,1,0:T(8,128)(2,1)S(1)}, bf16[2,128,512]{2,1,0:T(8,128)(2,1)S(1)}, u32[]{:S(2)}, u32[]{:S(2)}) %collective-permute-start.4) | collective-permute-done | bytes 262176 | tf_op jit(solution)/shard_map/ppermute | solution.py:16
  93.4 0.0 copy-done.4
  93.4 0.1 fusion.2
  93.5 0.7 slice_bitcast_fusion.2
Async XLA Ops:
  2.4 39.4 %copy-start = (bf16[128,1152]{1,0:T(8,128)(2,1)}, bf16[128,1152]{1,0:T(8,128)(2,1)S(1)}, u32[]{:S(2)}) copy-start(bf16[128,1152]{1,0:T(8,128)(2,1)S(1)} %pad_maximum_fusion.refs_9_.refs_10_.refs_11_) | copy-start | bytes 884740
  2.4 21.5 %collective-permute-start = (bf16[128,1152]{1,0:T(8,128)(2,1)S(1)}, bf16[128,1152]{1,0:T(8,128)(2,1)S(1)}, u32[]{:S(2)}, u32[]{:S(2)}) collective-permute-start(bf16[128,1152]{1,0:T(8,128)(2,1)S(1)} %pad_maximum_fusion.refs_9_.refs_10_.refs_11_), channel_id=1, source_target_pairs={{0,2},{1,3},{2,4},{3,5},{4,6},{5,7},{6,8},{7,9},{8,10},{9,11},{10,... | collective-permute-start | bytes 884744 | tf_op jit(solution)/shard_map/ppermute | solution.py:16
  8.5 21.9 %collective-permute-start.2 = (bf16[128,1152]{1,0:T(8,128)(2,1)S(1)}, bf16[128,1152]{1,0:T(8,128)(2,1)S(1)}, u32[]{:S(2)}, u32[]{:S(2)}) collective-permute-start(bf16[128,1152]{1,0:T(8,128)(2,1)S(1)} %pad_maximum_fusion.refs_9_.refs_10_.refs_11_), channel_id=1, source_target_pairs={{0,1},{1,2},{2,3},{3,4},{4,5},{5,6},{6,7},{7,8},{8,9},{9,10},{10,1... | collective-permute-start | bytes 884744 | tf_op jit(solution)/shard_map/ppermute | solution.py:16
  23.9 17.9 %copy-start.1 = (bf16[128,1152]{1,0:T(8,128)(2,1)}, bf16[128,1152]{1,0:T(8,128)(2,1)S(1)}, u32[]{:S(2)}) copy-start(bf16[128,1152]{1,0:T(8,128)(2,1)S(1)} %collective-permute-done.refs_3_.refs_4_.refs_5_) | copy-start | bytes 884740
  23.9 17.9 %collective-permute-start.1 = (bf16[128,1152]{1,0:T(8,128)(2,1)S(1)}, bf16[128,1152]{1,0:T(8,128)(2,1)S(1)}, u32[]{:S(2)}, u32[]{:S(2)}) collective-permute-start(bf16[128,1152]{1,0:T(8,128)(2,1)S(1)} %collective-permute-done.refs_3_.refs_4_.refs_5_), channel_id=1, source_target_pairs={{0,1},{1,2},{2,3},{3,4},{4,5},{5,6},{6,7},{7,8},{8,9},{9,10},{10,1... | collective-permute-start | bytes 884744 | tf_op jit(solution)/shard_map/ppermute | solution.py:16
  30.4 11.4 %copy-start.2 = (bf16[128,1152]{1,0:T(8,128)(2,1)}, bf16[128,1152]{1,0:T(8,128)(2,1)S(1)}, u32[]{:S(2)}) copy-start(bf16[128,1152]{1,0:T(8,128)(2,1)S(1)} %collective-permute-done.2.refs_6_.refs_7_.refs_8_) | copy-start | bytes 884740
  41.8 0.7 copy-start.3
  62.7 12.5 %collective-permute-start.3 = (bf16[2,2,128,512]{3,2,1,0:T(8,128)(2,1)}, bf16[2,2,128,512]{3,2,1,0:T(8,128)(2,1)S(1)}, u32[]{:S(2)}, u32[]{:S(2)}) collective-permute-start(bf16[2,2,128,512]{3,2,1,0:T(8,128)(2,1)} %get-tuple-element.9), channel_id=1, source_target_pairs={{1,0},{2,1},{3,2},{4,3},{5,4},{6,5},{7,6},{8,7},{9,8},{10,9},{11,1... | collective-permute-start | bytes 1572872 | tf_op jit(solution)/shard_map/ppermute | solution.py:16
  75.2 18.2 %copy-start.4 = (f32[2,128,512]{2,1,0:T(8,128)S(1)}, f32[2,128,512]{2,1,0:T(8,128)}, u32[]{:S(2)}) copy-start(f32[2,128,512]{2,1,0:T(8,128)} %get-tuple-element.8) | copy-start | bytes 1572868
  76.4 17.1 %collective-permute-start.4 = (bf16[2,128,512]{2,1,0:T(8,128)(2,1)S(1)}, bf16[2,128,512]{2,1,0:T(8,128)(2,1)S(1)}, u32[]{:S(2)}, u32[]{:S(2)}) collective-permute-start(bf16[2,128,512]{2,1,0:T(8,128)(2,1)S(1)} %fusion), channel_id=1, source_target_pairs={{2,0},{3,1},{4,2},{5,3},{6,4},{7,5},{8,6},{9,7},{10,8},{11,9},{12,... | collective-permute-start | bytes 786440 | tf_op jit(solution)/shard_map/ppermute | solution.py:16

commit v6 on v5

--- a/solution.py
+++ b/solution.py
@@ -39,20 +39,28 @@
     v_head = jnp.concatenate([ref[...] for ref in value_refs], 0)
     key_acc = jnp.zeros((key_count, HEAD_WIDTH), jnp.float32)
     value_acc = jnp.zeros((key_count, HEAD_WIDTH), jnp.float32)
-    for head in range(heads_per_group):
+    def head_scores(head):
         cols = slice(head * HEAD_WIDTH, (head + 1) * HEAD_WIDTH)
         q_head = query_ref[:, cols]
         o_grad = grad_ref[:, cols]
         scores = lax.dot_general(
             q_head, k_head, (((1,), (1,)), ((), ())), preferred_element_type=jnp.float32
         )
+        prob_grad = lax.dot_general(
+            o_grad, v_head, (((1,), (1,)), ((), ())), preferred_element_type=jnp.float32
+        )
+        return q_head, o_grad, scores, prob_grad
+
+    pending = head_scores(0)
+    for head in range(heads_per_group):
+        cols = slice(head * HEAD_WIDTH, (head + 1) * HEAD_WIDTH)
+        q_head, o_grad, scores, prob_grad = pending
+        if head + 1 < heads_per_group:
+            pending = head_scores(head + 1)
         scores = jnp.where(allowed, scores * inv_root, -1e30)
         row_max = jnp.max(scores, axis=1, keepdims=True)
         weights = jnp.exp(scores - row_max)
         probs = weights * (1.0 / jnp.sum(weights, axis=1, keepdims=True))
-        prob_grad = lax.dot_general(
-            o_grad, v_head, (((1,), (1,)), ((), ())), preferred_element_type=jnp.float32
-        )
         row_delta = jnp.sum(probs * prob_grad, axis=1, keepdims=True)
         score_grad = (probs * (prob_grad - row_delta) * inv_root).astype(jnp.bfloat16)
         probs_low = probs.astype(jnp.bfloat16)

time: 94.5 us -> 88.6 us (0.938)
  Pallas kernels: 20.2 us -> 14.2 us
    pallas_call x1, Pallas kernels: 20.2 us -> 14.2 us  [band_grads(): pl.pallas_call(band_kernel, grid=(kv_heads,), in_specs=[pl.BlockSpec((tok...]
where the time goes in v6:
time: 88.6 us; the launch traced here: 88.2 us
  waiting for transfers between devices  35.7 us (40%)
  starting transfers between devices  33.2 us (37%)
  Pallas kernels  14.2 us (16%)
  other arithmetic  2.94 us (3%)
  local copies, waits for them, and re-layouts  1.53 us (2%)
    ppermute x5, waiting for transfers between devices, from_behind(): return lax.ppermute(block, axis, route)  35.7 us
    ppermute x5, starting transfers between devices, from_behind(): return lax.ppermute(block, axis, route)  33.2 us
    pallas_call x1, Pallas kernels, band_grads(): pl.pallas_call(band_kernel, grid=(kv_heads,), in_specs=[pl.BlockSpec((tok...  14.2 us
  transfers between devices with their start and end apart: 5, of which 4 were waited for; matrix products, arithmetic and copies ran while one was open for 0% of the time, Pallas kernels for 0%

profile of v6, /device:TPU:56, one launch (start us, length us, event | category | flops | bytes accessed | tf_op | source)
XLA Modules:
  0.0 88.2 jit_solution(3276510518807116108)
XLA Ops:
  0.6 0.7 convert_element_type.29
  1.3 0.1 broadcast_in_dim.2
  1.4 1.0 %pad_maximum_fusion.refs_9_.refs_10_.refs_11_ = bf16[128,1152]{1,0:T(8,128)(2,1)S(1)} fusion(bf16[128,128]{1,0:T(8,128)(2,1)S(1)} %broadcast_in_dim.2, bf16[128,512]{1,0:T(8,128)(2,1)} %param.7, bf16[128,512]{1,0:T(8,128)(2,1)} %param.6), kind=kLoop, calls=%fused_computation.5 | loop fusion | flops 884736 | bytes 589824 | tf_op jit(solution)/shard_map/concatenate | solution.py:129
  2.4 0.0 copy-start
  2.4 6.1 %collective-permute-start = (bf16[128,1152]{1,0:T(8,128)(2,1)S(1)}, bf16[128,1152]{1,0:T(8,128)(2,1)S(1)}, u32[]{:S(2)}, u32[]{:S(2)}) collective-permute-start(bf16[128,1152]{1,0:T(8,128)(2,1)S(1)} %pad_maximum_fusion.refs_9_.refs_10_.refs_11_), channel_id=1, source_target_pairs={{0,2},{1,3},{2,4},{3,5},{4,6},{5,7},{6,8},{7,9},{8,10},{9,11},{10,... | collective-permute-start | bytes 884744 | tf_op jit(solution)/shard_map/ppermute | solution.py:16
  8.5 4.3 %collective-permute-start.2 = (bf16[128,1152]{1,0:T(8,128)(2,1)S(1)}, bf16[128,1152]{1,0:T(8,128)(2,1)S(1)}, u32[]{:S(2)}, u32[]{:S(2)}) collective-permute-start(bf16[128,1152]{1,0:T(8,128)(2,1)S(1)} %pad_maximum_fusion.refs_9_.refs_10_.refs_11_), channel_id=1, source_target_pairs={{0,1},{1,2},{2,3},{3,4},{4,5},{5,6},{6,7},{7,8},{8,9},{9,10},{10,1... | collective-permute-start | bytes 884744 | tf_op jit(solution)/shard_map/ppermute | solution.py:16
  12.8 11.2 %collective-permute-done.refs_3_.refs_4_.refs_5_ = bf16[128,1152]{1,0:T(8,128)(2,1)S(1)} collective-permute-done((bf16[128,1152]{1,0:T(8,128)(2,1)S(1)}, bf16[128,1152]{1,0:T(8,128)(2,1)S(1)}, u32[]{:S(2)}, u32[]{:S(2)}) %collective-permute-start) | collective-permute-done | bytes 294944 | tf_op jit(solution)/shard_map/ppermute | solution.py:16
  23.9 0.0 copy-start.1
  23.9 6.5 %collective-permute-start.1 = (bf16[128,1152]{1,0:T(8,128)(2,1)S(1)}, bf16[128,1152]{1,0:T(8,128)(2,1)S(1)}, u32[]{:S(2)}, u32[]{:S(2)}) collective-permute-start(bf16[128,1152]{1,0:T(8,128)(2,1)S(1)} %collective-permute-done.refs_3_.refs_4_.refs_5_), channel_id=1, source_target_pairs={{0,1},{1,2},{2,3},{3,4},{4,5},{5,6},{6,7},{7,8},{8,9},{9,10},{10,1... | collective-permute-start | bytes 884744 | tf_op jit(solution)/shard_map/ppermute | solution.py:16
  30.4 0.0 collective-permute-done.2.refs_6_.refs_7_.refs_8_
  30.4 0.0 copy-start.2
  30.4 11.4 %collective-permute-done.1.refs_0_.refs_1_.refs_2_ = bf16[128,1152]{1,0:T(8,128)(2,1)S(1)} collective-permute-done((bf16[128,1152]{1,0:T(8,128)(2,1)S(1)}, bf16[128,1152]{1,0:T(8,128)(2,1)S(1)}, u32[]{:S(2)}, u32[]{:S(2)}) %collective-permute-start.1) | collective-permute-done | bytes 294944 | tf_op jit(solution)/shard_map/ppermute | solution.py:16
  41.8 0.0 copy-done
  41.8 0.0 copy-done.1
  41.8 0.0 copy-done.2
  41.8 0.0 copy-start.3
  41.8 0.7 copy-done.3
  42.5 14.2 %shard_map.76 = (bf16[128,4096]{1,0:T(8,128)(2,1)}, bf16[2,2,128,512]{3,2,1,0:T(8,128)(2,1)}, f32[2,128,512]{2,1,0:T(8,128)}, f32[2,128,512]{2,1,0:T(8,128)}) custom-call(bf16[128,4096]{1,0:T(8,128)(2,1)} %query_ref.1, bf16[128,4096]{1,0:T(8,128)(2,1)} %grad_ref.1, bf16[128,1152]{1,0:T(8,128)(2,1)} %copy-done.3, bf16[128,1152]{1,0:T(8,128)(2,1)} %copy-done.3, ...), custom_call_target="tpu_custom_call" | custom-call | tf_op jit(solution)/shard_map/pallas_call | solution.py:100
  56.7 5.4 %collective-permute-start.3 = (bf16[2,2,128,512]{3,2,1,0:T(8,128)(2,1)}, bf16[2,2,128,512]{3,2,1,0:T(8,128)(2,1)S(1)}, u32[]{:S(2)}, u32[]{:S(2)}) collective-permute-start(bf16[2,2,128,512]{3,2,1,0:T(8,128)(2,1)} %get-tuple-element.9), channel_id=1, source_target_pairs={{1,0},{2,1},{3,2},{4,3},{5,4},{6,5},{7,6},{8,7},{9,8},{10,9},{11,1... | collective-permute-start | bytes 1572872 | tf_op jit(solution)/shard_map/ppermute | solution.py:16
  62.2 7.0 %collective-permute-done.3 = bf16[2,2,128,512]{3,2,1,0:T(8,128)(2,1)S(1)} collective-permute-done((bf16[2,2,128,512]{3,2,1,0:T(8,128)(2,1)}, bf16[2,2,128,512]{3,2,1,0:T(8,128)(2,1)S(1)}, u32[]{:S(2)}, u32[]{:S(2)}) %collective-permute-start.3) | collective-permute-done | bytes 524320 | tf_op jit(solution)/shard_map/ppermute | solution.py:16
  69.2 0.0 copy-start.4
  69.2 1.2 %fusion = bf16[2,128,512]{2,1,0:T(8,128)(2,1)S(1)} fusion(f32[2,128,512]{2,1,0:T(8,128)} %get-tuple-element.10, bf16[2,2,128,512]{3,2,1,0:T(8,128)(2,1)S(1)} %collective-permute-done.3), kind=kLoop, calls=%fused_computation.1 | loop fusion | flops 393216 | bytes 1048576 | tf_op jit(solution)/shard_map/convert_element_type | solution.py:136
  70.4 10.9 %collective-permute-start.4 = (bf16[2,128,512]{2,1,0:T(8,128)(2,1)S(1)}, bf16[2,128,512]{2,1,0:T(8,128)(2,1)S(1)}, u32[]{:S(2)}, u32[]{:S(2)}) collective-permute-start(bf16[2,128,512]{2,1,0:T(8,128)(2,1)S(1)} %fusion), channel_id=1, source_target_pairs={{2,0},{3,1},{4,2},{5,3},{6,4},{7,5},{8,6},{9,7},{10,8},{11,9},{12,... | collective-permute-start | bytes 786440 | tf_op jit(solution)/shard_map/ppermute | solution.py:16
  81.3 6.2 %collective-permute-done.4 = bf16[2,128,512]{2,1,0:T(8,128)(2,1)S(1)} collective-permute-done((bf16[2,128,512]{2,1,0:T(8,128)(2,1)S(1)}, bf16[2,128,512]{2,1,0:T(8,128)(2,1)S(1)}, u32[]{:S(2)}, u32[]{:S(2)}) %collective-permute-start.4) | collective-permute-done | bytes 262176 | tf_op jit(solution)/shard_map/ppermute | solution.py:16
  87.4 0.0 copy-done.4
  87.4 0.1 fusion.2
  87.5 0.7 slice_bitcast_fusion.2
Async XLA Ops:
  2.4 39.4 %copy-start = (bf16[128,1152]{1,0:T(8,128)(2,1)}, bf16[128,1152]{1,0:T(8,128)(2,1)S(1)}, u32[]{:S(2)}) copy-start(bf16[128,1152]{1,0:T(8,128)(2,1)S(1)} %pad_maximum_fusion.refs_9_.refs_10_.refs_11_) | copy-start | bytes 884740
  2.4 21.5 %collective-permute-start = (bf16[128,1152]{1,0:T(8,128)(2,1)S(1)}, bf16[128,1152]{1,0:T(8,128)(2,1)S(1)}, u32[]{:S(2)}, u32[]{:S(2)}) collective-permute-start(bf16[128,1152]{1,0:T(8,128)(2,1)S(1)} %pad_maximum_fusion.refs_9_.refs_10_.refs_11_), channel_id=1, source_target_pairs={{0,2},{1,3},{2,4},{3,5},{4,6},{5,7},{6,8},{7,9},{8,10},{9,11},{10,... | collective-permute-start | bytes 884744 | tf_op jit(solution)/shard_map/ppermute | solution.py:16
  8.5 21.9 %collective-permute-start.2 = (bf16[128,1152]{1,0:T(8,128)(2,1)S(1)}, bf16[128,1152]{1,0:T(8,128)(2,1)S(1)}, u32[]{:S(2)}, u32[]{:S(2)}) collective-permute-start(bf16[128,1152]{1,0:T(8,128)(2,1)S(1)} %pad_maximum_fusion.refs_9_.refs_10_.refs_11_), channel_id=1, source_target_pairs={{0,1},{1,2},{2,3},{3,4},{4,5},{5,6},{6,7},{7,8},{8,9},{9,10},{10,1... | collective-permute-start | bytes 884744 | tf_op jit(solution)/shard_map/ppermute | solution.py:16
  23.9 17.9 %copy-start.1 = (bf16[128,1152]{1,0:T(8,128)(2,1)}, bf16[128,1152]{1,0:T(8,128)(2,1)S(1)}, u32[]{:S(2)}) copy-start(bf16[128,1152]{1,0:T(8,128)(2,1)S(1)} %collective-permute-done.refs_3_.refs_4_.refs_5_) | copy-start | bytes 884740
  23.9 17.9 %collective-permute-start.1 = (bf16[128,1152]{1,0:T(8,128)(2,1)S(1)}, bf16[128,1152]{1,0:T(8,128)(2,1)S(1)}, u32[]{:S(2)}, u32[]{:S(2)}) collective-permute-start(bf16[128,1152]{1,0:T(8,128)(2,1)S(1)} %collective-permute-done.refs_3_.refs_4_.refs_5_), channel_id=1, source_target_pairs={{0,1},{1,2},{2,3},{3,4},{4,5},{5,6},{6,7},{7,8},{8,9},{9,10},{10,1... | collective-permute-start | bytes 884744 | tf_op jit(solution)/shard_map/ppermute | solution.py:16
  30.4 11.4 %copy-start.2 = (bf16[128,1152]{1,0:T(8,128)(2,1)}, bf16[128,1152]{1,0:T(8,128)(2,1)S(1)}, u32[]{:S(2)}) copy-start(bf16[128,1152]{1,0:T(8,128)(2,1)S(1)} %collective-permute-done.2.refs_6_.refs_7_.refs_8_) | copy-start | bytes 884740
  41.8 0.7 copy-start.3
  56.7 12.4 %collective-permute-start.3 = (bf16[2,2,128,512]{3,2,1,0:T(8,128)(2,1)}, bf16[2,2,128,512]{3,2,1,0:T(8,128)(2,1)S(1)}, u32[]{:S(2)}, u32[]{:S(2)}) collective-permute-start(bf16[2,2,128,512]{3,2,1,0:T(8,128)(2,1)} %get-tuple-element.9), channel_id=1, source_target_pairs={{1,0},{2,1},{3,2},{4,3},{5,4},{6,5},{7,6},{8,7},{9,8},{10,9},{11,1... | collective-permute-start | bytes 1572872 | tf_op jit(solution)/shard_map/ppermute | solution.py:16
  69.2 18.2 %copy-start.4 = (f32[2,128,512]{2,1,0:T(8,128)S(1)}, f32[2,128,512]{2,1,0:T(8,128)}, u32[]{:S(2)}) copy-start(f32[2,128,512]{2,1,0:T(8,128)} %get-tuple-element.8) | copy-start | bytes 1572868
  70.4 17.1 %collective-permute-start.4 = (bf16[2,128,512]{2,1,0:T(8,128)(2,1)S(1)}, bf16[2,128,512]{2,1,0:T(8,128)(2,1)S(1)}, u32[]{:S(2)}, u32[]{:S(2)}) collective-permute-start(bf16[2,128,512]{2,1,0:T(8,128)(2,1)S(1)} %fusion), channel_id=1, source_target_pairs={{2,0},{3,1},{4,2},{5,3},{6,4},{7,5},{8,6},{9,7},{10,8},{11,9},{12,... | collective-permute-start | bytes 786440 | tf_op jit(solution)/shard_map/ppermute | solution.py:16

commit v7 on v6

--- a/solution.py
+++ b/solution.py
@@ -128,7 +128,7 @@
     seg_cols = jnp.broadcast_to(segments.astype(jnp.bfloat16)[:, None], (tok_rows, HEAD_WIDTH))
     own = jnp.concatenate([key_rows, value_matrix, seg_cols], 1)
     back_one = from_behind(own, axes, 1)
-    back_two = from_behind(own, axes, 2)
+    back_two = from_behind(back_one, axes, 1)
     back_three = from_behind(back_two, axes, 1)
     blocks = [back_three, back_two, back_one, own]
     dq_part, send, middle, own_part = band_grads(query_rows, out_grad, blocks, kv_heads)

time: 88.6 us -> 92 us (1.038); the launches traced: 88.2 us -> 90.2 us
  waiting for transfers between devices: 35.7 us -> 58.9 us
  starting transfers between devices: 33.2 us -> 11.9 us
    ppermute x5, waiting for transfers between devices: 35.7 us -> 58.9 us  [from_behind(): return lax.ppermute(block, axis, route)]
    ppermute x5, starting transfers between devices: 33.2 us -> 11.9 us  [from_behind(): return lax.ppermute(block, axis, route)]
  transfers between devices with their start and end apart: 5 -> 5, of which waited for: 4 -> 5; matrix products, arithmetic and copies ran while one was open for 0% -> 0% of each run, Pallas kernels for 0% -> 0%
where the time goes in v7:
time: 92 us; the launch traced here: 90.2 us
  waiting for transfers between devices  58.9 us (64%)
  Pallas kernels  14.2 us (15%)
  starting transfers between devices  11.9 us (13%)
  other arithmetic  2.94 us (3%)
  local copies, waits for them, and re-layouts  1.52 us (2%)
    ppermute x5, waiting for transfers between devices, from_behind(): return lax.ppermute(block, axis, route)  58.9 us
    pallas_call x1, Pallas kernels, band_grads(): pl.pallas_call(band_kernel, grid=(kv_heads,), in_specs=[pl.BlockSpec((tok...  14.2 us
    ppermute x5, starting transfers between devices, from_behind(): return lax.ppermute(block, axis, route)  11.9 us
  transfers between devices with their start and end apart: 5, of which 5 were waited for; matrix products, arithmetic and copies ran while one was open for 0% of the time, Pallas kernels for 0%

profile of v7, /device:TPU:56, one launch (start us, length us, event | category | flops | bytes accessed | tf_op | source)
XLA Modules:
  0.0 90.2 jit_solution(16807131268991669230)
XLA Ops:
  0.6 0.7 convert_element_type.29
  1.3 0.1 broadcast_in_dim.2
  1.4 1.0 %pad_maximum_fusion.refs_9_.refs_10_.refs_11_ = bf16[128,1152]{1,0:T(8,128)(2,1)S(1)} fusion(bf16[128,128]{1,0:T(8,128)(2,1)S(1)} %broadcast_in_dim.2, bf16[128,512]{1,0:T(8,128)(2,1)} %param.7, bf16[128,512]{1,0:T(8,128)(2,1)} %param.6), kind=kLoop, calls=%fused_computation.5 | loop fusion | flops 884736 | bytes 589824 | tf_op jit(solution)/shard_map/concatenate | solution.py:129
  2.4 0.0 copy-start
  2.4 4.3 %collective-permute-start = (bf16[128,1152]{1,0:T(8,128)(2,1)S(1)}, bf16[128,1152]{1,0:T(8,128)(2,1)S(1)}, u32[]{:S(2)}, u32[]{:S(2)}) collective-permute-start(bf16[128,1152]{1,0:T(8,128)(2,1)S(1)} %pad_maximum_fusion.refs_9_.refs_10_.refs_11_), channel_id=1, source_target_pairs={{0,1},{1,2},{2,3},{3,4},{4,5},{5,6},{6,7},{7,8},{8,9},{9,10},{10,1... | collective-permute-start | bytes 884744 | tf_op jit(solution)/shard_map/ppermute | solution.py:16
  6.7 17.1 %collective-permute-done.refs_6_.refs_7_.refs_8_ = bf16[128,1152]{1,0:T(8,128)(2,1)S(1)} collective-permute-done((bf16[128,1152]{1,0:T(8,128)(2,1)S(1)}, bf16[128,1152]{1,0:T(8,128)(2,1)S(1)}, u32[]{:S(2)}, u32[]{:S(2)}) %collective-permute-start) | collective-permute-done | bytes 294944 | tf_op jit(solution)/shard_map/ppermute | solution.py:16
  23.8 0.0 copy-start.1
  23.8 1.9 %collective-permute-start.1 = (bf16[128,1152]{1,0:T(8,128)(2,1)S(1)}, bf16[128,1152]{1,0:T(8,128)(2,1)S(1)}, u32[]{:S(2)}, u32[]{:S(2)}) collective-permute-start(bf16[128,1152]{1,0:T(8,128)(2,1)S(1)} %collective-permute-done.refs_6_.refs_7_.refs_8_), channel_id=1, source_target_pairs={{0,1},{1,2},{2,3},{3,4},{4,5},{5,6},{6,7},{7,8},{8,9},{9,10},{10,1... | collective-permute-start | bytes 884744 | tf_op jit(solution)/shard_map/ppermute | solution.py:16
  25.7 10.3 %collective-permute-done.1.refs_3_.refs_4_.refs_5_ = bf16[128,1152]{1,0:T(8,128)(2,1)S(1)} collective-permute-done((bf16[128,1152]{1,0:T(8,128)(2,1)S(1)}, bf16[128,1152]{1,0:T(8,128)(2,1)S(1)}, u32[]{:S(2)}, u32[]{:S(2)}) %collective-permute-start.1) | collective-permute-done | bytes 294944 | tf_op jit(solution)/shard_map/ppermute | solution.py:16
  36.0 0.0 copy-start.2
  36.0 1.9 %collective-permute-start.2 = (bf16[128,1152]{1,0:T(8,128)(2,1)S(1)}, bf16[128,1152]{1,0:T(8,128)(2,1)S(1)}, u32[]{:S(2)}, u32[]{:S(2)}) collective-permute-start(bf16[128,1152]{1,0:T(8,128)(2,1)S(1)} %collective-permute-done.1.refs_3_.refs_4_.refs_5_), channel_id=1, source_target_pairs={{0,1},{1,2},{2,3},{3,4},{4,5},{5,6},{6,7},{7,8},{8,9},{9,10},{10,1... | collective-permute-start | bytes 884744 | tf_op jit(solution)/shard_map/ppermute | solution.py:16
  38.0 10.3 %collective-permute-done.2.refs_0_.refs_1_.refs_2_ = bf16[128,1152]{1,0:T(8,128)(2,1)S(1)} collective-permute-done((bf16[128,1152]{1,0:T(8,128)(2,1)S(1)}, bf16[128,1152]{1,0:T(8,128)(2,1)S(1)}, u32[]{:S(2)}, u32[]{:S(2)}) %collective-permute-start.2) | collective-permute-done | bytes 294944 | tf_op jit(solution)/shard_map/ppermute | solution.py:16
  48.3 0.0 copy-done
  48.3 0.0 copy-done.1
  48.3 0.0 copy-done.2
  48.3 0.0 copy-start.3
  48.3 0.7 copy-done.3
  49.0 14.2 %shard_map.76 = (bf16[128,4096]{1,0:T(8,128)(2,1)}, bf16[2,2,128,512]{3,2,1,0:T(8,128)(2,1)}, f32[2,128,512]{2,1,0:T(8,128)}, f32[2,128,512]{2,1,0:T(8,128)}) custom-call(bf16[128,4096]{1,0:T(8,128)(2,1)} %query_ref.1, bf16[128,4096]{1,0:T(8,128)(2,1)} %grad_ref.1, bf16[128,1152]{1,0:T(8,128)(2,1)} %copy-done.3, bf16[128,1152]{1,0:T(8,128)(2,1)} %copy-done.3, ...), custom_call_target="tpu_custom_call" | custom-call | tf_op jit(solution)/shard_map/pallas_call | solution.py:100
  63.2 1.9 %collective-permute-start.3 = (bf16[2,2,128,512]{3,2,1,0:T(8,128)(2,1)}, bf16[2,2,128,512]{3,2,1,0:T(8,128)(2,1)S(1)}, u32[]{:S(2)}, u32[]{:S(2)}) collective-permute-start(bf16[2,2,128,512]{3,2,1,0:T(8,128)(2,1)} %get-tuple-element.9), channel_id=1, source_target_pairs={{1,0},{2,1},{3,2},{4,3},{5,4},{6,5},{7,6},{8,7},{9,8},{10,9},{11,1... | collective-permute-start | bytes 1572872 | tf_op jit(solution)/shard_map/ppermute | solution.py:16
  65.1 11.0 %collective-permute-done.3 = bf16[2,2,128,512]{3,2,1,0:T(8,128)(2,1)S(1)} collective-permute-done((bf16[2,2,128,512]{3,2,1,0:T(8,128)(2,1)}, bf16[2,2,128,512]{3,2,1,0:T(8,128)(2,1)S(1)}, u32[]{:S(2)}, u32[]{:S(2)}) %collective-permute-start.3) | collective-permute-done | bytes 524320 | tf_op jit(solution)/shard_map/ppermute | solution.py:16
  76.1 0.0 copy-start.4
  76.1 1.2 %fusion = bf16[2,128,512]{2,1,0:T(8,128)(2,1)S(1)} fusion(f32[2,128,512]{2,1,0:T(8,128)} %get-tuple-element.10, bf16[2,2,128,512]{3,2,1,0:T(8,128)(2,1)S(1)} %collective-permute-done.3), kind=kLoop, calls=%fused_computation.1 | loop fusion | flops 393216 | bytes 1048576 | tf_op jit(solution)/shard_map/convert_element_type | solution.py:136
  77.3 1.9 %collective-permute-start.4 = (bf16[2,128,512]{2,1,0:T(8,128)(2,1)S(1)}, bf16[2,128,512]{2,1,0:T(8,128)(2,1)S(1)}, u32[]{:S(2)}, u32[]{:S(2)}) collective-permute-start(bf16[2,128,512]{2,1,0:T(8,128)(2,1)S(1)} %fusion), channel_id=1, source_target_pairs={{2,0},{3,1},{4,2},{5,3},{6,4},{7,5},{8,6},{9,7},{10,8},{11,9},{12,... | collective-permute-start | bytes 786440 | tf_op jit(solution)/shard_map/ppermute | solution.py:16
  79.3 10.1 %collective-permute-done.4 = bf16[2,128,512]{2,1,0:T(8,128)(2,1)S(1)} collective-permute-done((bf16[2,128,512]{2,1,0:T(8,128)(2,1)S(1)}, bf16[2,128,512]{2,1,0:T(8,128)(2,1)S(1)}, u32[]{:S(2)}, u32[]{:S(2)}) %collective-permute-start.4) | collective-permute-done | bytes 262176 | tf_op jit(solution)/shard_map/ppermute | solution.py:16
  89.4 0.0 copy-done.4
  89.4 0.1 fusion.2
  89.5 0.7 slice_bitcast_fusion.2
Async XLA Ops:
  2.4 45.9 %copy-start = (bf16[128,1152]{1,0:T(8,128)(2,1)}, bf16[128,1152]{1,0:T(8,128)(2,1)S(1)}, u32[]{:S(2)}) copy-start(bf16[128,1152]{1,0:T(8,128)(2,1)S(1)} %pad_maximum_fusion.refs_9_.refs_10_.refs_11_) | copy-start | bytes 884740
  2.4 21.4 %collective-permute-start = (bf16[128,1152]{1,0:T(8,128)(2,1)S(1)}, bf16[128,1152]{1,0:T(8,128)(2,1)S(1)}, u32[]{:S(2)}, u32[]{:S(2)}) collective-permute-start(bf16[128,1152]{1,0:T(8,128)(2,1)S(1)} %pad_maximum_fusion.refs_9_.refs_10_.refs_11_), channel_id=1, source_target_pairs={{0,1},{1,2},{2,3},{3,4},{4,5},{5,6},{6,7},{7,8},{8,9},{9,10},{10,1... | collective-permute-start | bytes 884744 | tf_op jit(solution)/shard_map/ppermute | solution.py:16
  23.8 24.5 %copy-start.1 = (bf16[128,1152]{1,0:T(8,128)(2,1)}, bf16[128,1152]{1,0:T(8,128)(2,1)S(1)}, u32[]{:S(2)}) copy-start(bf16[128,1152]{1,0:T(8,128)(2,1)S(1)} %collective-permute-done.refs_6_.refs_7_.refs_8_) | copy-start | bytes 884740
  23.8 12.2 %collective-permute-start.1 = (bf16[128,1152]{1,0:T(8,128)(2,1)S(1)}, bf16[128,1152]{1,0:T(8,128)(2,1)S(1)}, u32[]{:S(2)}, u32[]{:S(2)}) collective-permute-start(bf16[128,1152]{1,0:T(8,128)(2,1)S(1)} %collective-permute-done.refs_6_.refs_7_.refs_8_), channel_id=1, source_target_pairs={{0,1},{1,2},{2,3},{3,4},{4,5},{5,6},{6,7},{7,8},{8,9},{9,10},{10,1... | collective-permute-start | bytes 884744 | tf_op jit(solution)/shard_map/ppermute | solution.py:16
  36.0 12.3 %copy-start.2 = (bf16[128,1152]{1,0:T(8,128)(2,1)}, bf16[128,1152]{1,0:T(8,128)(2,1)S(1)}, u32[]{:S(2)}) copy-start(bf16[128,1152]{1,0:T(8,128)(2,1)S(1)} %collective-permute-done.1.refs_3_.refs_4_.refs_5_) | copy-start | bytes 884740
  36.0 12.2 %collective-permute-start.2 = (bf16[128,1152]{1,0:T(8,128)(2,1)S(1)}, bf16[128,1152]{1,0:T(8,128)(2,1)S(1)}, u32[]{:S(2)}, u32[]{:S(2)}) collective-permute-start(bf16[128,1152]{1,0:T(8,128)(2,1)S(1)} %collective-permute-done.1.refs_3_.refs_4_.refs_5_), channel_id=1, source_target_pairs={{0,1},{1,2},{2,3},{3,4},{4,5},{5,6},{6,7},{7,8},{8,9},{9,10},{10,1... | collective-permute-start | bytes 884744 | tf_op jit(solution)/shard_map/ppermute | solution.py:16
  48.3 0.7 copy-start.3
  63.2 12.9 %collective-permute-start.3 = (bf16[2,2,128,512]{3,2,1,0:T(8,128)(2,1)}, bf16[2,2,128,512]{3,2,1,0:T(8,128)(2,1)S(1)}, u32[]{:S(2)}, u32[]{:S(2)}) collective-permute-start(bf16[2,2,128,512]{3,2,1,0:T(8,128)(2,1)} %get-tuple-element.9), channel_id=1, source_target_pairs={{1,0},{2,1},{3,2},{4,3},{5,4},{6,5},{7,6},{8,7},{9,8},{10,9},{11,1... | collective-permute-start | bytes 1572872 | tf_op jit(solution)/shard_map/ppermute | solution.py:16
  76.1 13.2 %copy-start.4 = (f32[2,128,512]{2,1,0:T(8,128)S(1)}, f32[2,128,512]{2,1,0:T(8,128)}, u32[]{:S(2)}) copy-start(f32[2,128,512]{2,1,0:T(8,128)} %get-tuple-element.8) | copy-start | bytes 1572868
  77.3 12.0 %collective-permute-start.4 = (bf16[2,128,512]{2,1,0:T(8,128)(2,1)S(1)}, bf16[2,128,512]{2,1,0:T(8,128)(2,1)S(1)}, u32[]{:S(2)}, u32[]{:S(2)}) collective-permute-start(bf16[2,128,512]{2,1,0:T(8,128)(2,1)S(1)} %fusion), channel_id=1, source_target_pairs={{2,0},{3,1},{4,2},{5,3},{6,4},{7,5},{8,6},{9,7},{10,8},{11,9},{12,... | collective-permute-start | bytes 786440 | tf_op jit(solution)/shard_map/ppermute | solution.py:16

commit v8 on v6

--- a/solution.py
+++ b/solution.py
@@ -8,6 +8,7 @@
 
 HEAD_WIDTH = 128
 SPAN = 3
+GROUP_HEADS = 8
 
 
 def from_behind(block, axis, distance):
@@ -20,7 +21,7 @@
     key_refs = refs[0:12:3]
     value_refs = refs[1:12:3]
     seg_refs = refs[2:12:3]
-    dq_ref, send_ref, middle_ref, own_ref = refs[12:]
+    dq_ref, send_ref, middle_ref, own_ref = refs[-4:]
     tok_rows = query_ref.shape[0]
     key_count = tok_rows * len(key_refs)
     heads_per_group = query_ref.shape[1] // HEAD_WIDTH
@@ -86,56 +87,112 @@
     own_ref[1] = value_acc[rows(3)]
 
 
-def band_grads(query_blk, grad_blk, blocks, kv_heads):
+def band_grads(query_blk, grad_blk, kv_blocks, seg_blocks, first_kv, kv_heads, dq_buf):
     tok_rows, q_width = query_blk.shape
-    kv_width = kv_heads * HEAD_WIDTH
-    group_width = q_width // kv_heads
+    group_width = HEAD_WIDTH * GROUP_HEADS
+    half_width = kv_heads * HEAD_WIDTH
     kv_specs = []
     kv_args = []
-    for blk in blocks:
-        kv_specs.append(pl.BlockSpec((tok_rows, HEAD_WIDTH), lambda g: (0, g)))
-        kv_specs.append(pl.BlockSpec((tok_rows, HEAD_WIDTH), lambda g, n=kv_heads: (0, n + g)))
-        kv_specs.append(pl.BlockSpec((tok_rows, HEAD_WIDTH), lambda g, n=kv_heads: (0, 2 * n)))
-        kv_args += [blk, blk, blk]
+    for (blk, k_off, v_off), (seg_blk, seg_off) in zip(kv_blocks, seg_blocks):
+        kv_specs.append(pl.BlockSpec((tok_rows, HEAD_WIDTH), lambda g, o=k_off: (0, o + g)))
+        kv_specs.append(pl.BlockSpec((tok_rows, HEAD_WIDTH), lambda g, o=v_off: (0, o + g)))
+        kv_specs.append(pl.BlockSpec((tok_rows, HEAD_WIDTH), lambda g, o=seg_off: (0, o)))
+        kv_args += [blk, blk, seg_blk]
+    extra_specs = []
+    extra_args = []
+    aliases = {}
+    if dq_buf is not None:
+        extra_specs = [pl.BlockSpec(memory_space=pl.ANY)]
+        extra_args = [dq_buf]
+        aliases = {2 + len(kv_args): 0}
     return pl.pallas_call(
         band_kernel,
         grid=(kv_heads,),
         in_specs=[
-            pl.BlockSpec((tok_rows, group_width), lambda g: (0, g)),
-            pl.BlockSpec((tok_rows, group_width), lambda g: (0, g)),
+            pl.BlockSpec((tok_rows, group_width), lambda g, f=first_kv: (0, f + g)),
+            pl.BlockSpec((tok_rows, group_width), lambda g, f=first_kv: (0, f + g)),
         ]
-        + kv_specs,
+        + kv_specs
+        + extra_specs,
         out_specs=[
-            pl.BlockSpec((tok_rows, group_width), lambda g: (0, g)),
+            pl.BlockSpec((tok_rows, group_width), lambda g, f=first_kv: (0, f + g)),
             pl.BlockSpec((2, 2, tok_rows, HEAD_WIDTH), lambda g: (0, 0, 0, g)),
             pl.BlockSpec((2, tok_rows, HEAD_WIDTH), lambda g: (0, 0, g)),
             pl.BlockSpec((2, tok_rows, HEAD_WIDTH), lambda g: (0, 0, g)),
         ],
         out_shape=[
             jax.ShapeDtypeStruct((tok_rows, q_width), jnp.bfloat16),
-            jax.ShapeDtypeStruct((2, 2, tok_rows, kv_width), jnp.bfloat16),
-            jax.ShapeDtypeStruct((2, tok_rows, kv_width), jnp.float32),
-            jax.ShapeDtypeStruct((2, tok_rows, kv_width), jnp.float32),
-        ],
-    )(query_blk, grad_blk, *kv_args)
+            jax.ShapeDtypeStruct((2, 2, tok_rows, half_width), jnp.bfloat16),
+            jax.ShapeDtypeStruct((2, tok_rows, half_width), jnp.float32),
+            jax.ShapeDtypeStruct((2, tok_rows, half_width), jnp.float32),
+        ],
+        input_output_aliases=aliases,
+    )(query_blk, grad_blk, *kv_args, *extra_args)
 
 
 def body(query_rows, key_rows, value_matrix, out_grad, segments):
     tok_rows = query_rows.shape[0]
     kv_width = key_rows.shape[1]
     kv_heads = kv_width // HEAD_WIDTH
+    half = kv_heads // 2
+    w = HEAD_WIDTH
     axes = ("ctx", "fsdp")
     seg_cols = jnp.broadcast_to(segments.astype(jnp.bfloat16)[:, None], (tok_rows, HEAD_WIDTH))
     own = jnp.concatenate([key_rows, value_matrix, seg_cols], 1)
     back_one = from_behind(own, axes, 1)
     back_two = from_behind(own, axes, 2)
-    back_three = from_behind(back_two, axes, 1)
-    blocks = [back_three, back_two, back_one, own]
-    dq_part, send, middle, own_part = band_grads(query_rows, out_grad, blocks, kv_heads)
-    received = from_behind(send, axes, -1)
-    forward = (middle + received[0].astype(jnp.float32)).astype(jnp.bfloat16)
+    seg_at = 2 * kv_heads
+    two_first = jnp.concatenate(
+        [
+            back_two[:, 0 : half * w],
+            back_two[:, kv_heads * w : (kv_heads + half) * w],
+            back_two[:, seg_at * w : (seg_at + 1) * w],
+        ],
+        1,
+    )
+    two_second = jnp.concatenate(
+        [back_two[:, half * w : kv_heads * w], back_two[:, (kv_heads + half) * w : seg_at * w]],
+        1,
+    )
+    three_first = from_behind(two_first, axes, 1)
+    three_second = from_behind(two_second, axes, 1)
+    full = [(back_two, 0, kv_heads), (back_one, 0, kv_heads), (own, 0, kv_heads)]
+    segs = [(back_two, seg_at), (back_one, seg_at), (own, seg_at)]
+    dq_part, send_a, middle_a, own_a = band_grads(
+        query_rows,
+        out_grad,
+        [(three_first, 0, half)] + full,
+        [(three_first, 2 * half)] + segs,
+        0,
+        half,
+        None,
+    )
+    dq_part, send_b, middle_b, own_b = band_grads(
+        query_rows,
+        out_grad,
+        [(three_second, 0, half)] + [(b, k + half, v + half) for b, k, v in full],
+        [(three_first, 2 * half)] + segs,
+        half,
+        half,
+        dq_part,
+    )
+    received_a = from_behind(send_a, axes, -1)
+    received_b = from_behind(send_b, axes, -1)
+    forward = jnp.concatenate(
+        [
+            middle_a + received_a[0].astype(jnp.float32),
+            middle_b + received_b[0].astype(jnp.float32),
+        ],
+        2,
+    ).astype(jnp.bfloat16)
     gathered = from_behind(forward, axes, -2)
-    total = own_part + received[1].astype(jnp.float32) + gathered.astype(jnp.float32)
+    total = jnp.concatenate(
+        [
+            own_a + received_a[1].astype(jnp.float32),
+            own_b + received_b[1].astype(jnp.float32),
+        ],
+        2,
+    ) + gathered.astype(jnp.float32)
     return (
         dq_part,
         total[0].astype(jnp.bfloat16),

time: 88.6 us -> 97.1 us (1.096)
  the two profiles are of different devices: /device:TPU:56 before, /device:TPU:46 now
where the time goes in v8:
time: 97.1 us; the launch traced here: 96.8 us
  waiting for transfers between devices  48.4 us (50%)
  starting transfers between devices  26.7 us (27%)
  Pallas kernels  16.1 us (17%)
  local copies, waits for them, and re-layouts  2.84 us (3%)
  other arithmetic  1.86 us (2%)
    ppermute x7, waiting for transfers between devices, from_behind(): return lax.ppermute(block, axis, route)  48.4 us
    ppermute x7, starting transfers between devices, from_behind(): return lax.ppermute(block, axis, route)  26.7 us
    pallas_call x2, Pallas kernels, band_grads(): pl.pallas_call(band_kernel, grid=(kv_heads,), in_specs=[pl.BlockSpec((tok...  16.1 us
    unnamed x18, local copies, waits for them, and re-layouts  2.02 us
  transfers between devices with their start and end apart: 7, of which 5 were waited for; matrix products, arithmetic and copies ran while one was open for 0% of the time, Pallas kernels for 8%

profile of v8, /device:TPU:46, one launch (start us, length us, event | category | flops | bytes accessed | tf_op | source)
XLA Modules:
  0.0 96.8 jit_solution(983640934711476148)
XLA Ops:
  0.6 0.7 convert_element_type.39
  1.3 0.1 broadcast_in_dim.2
  1.4 1.0 %pad_maximum_fusion.refs_9_.refs_10_.refs_11_ = bf16[128,1152]{1,0:T(8,128)(2,1)S(1)} fusion(bf16[128,128]{1,0:T(8,128)(2,1)S(1)} %broadcast_in_dim.2, bf16[128,512]{1,0:T(8,128)(2,1)} %param.7, bf16[128,512]{1,0:T(8,128)(2,1)} %param.6), kind=kLoop, calls=%fused_computation.2 | loop fusion | flops 884736 | bytes 589824 | tf_op jit(solution)/shard_map/concatenate | solution.py:141
  2.4 0.0 copy-start
  2.4 6.1 %collective-permute-start = (bf16[128,1152]{1,0:T(8,128)(2,1)S(1)}, bf16[128,1152]{1,0:T(8,128)(2,1)S(1)}, u32[]{:S(2)}, u32[]{:S(2)}) collective-permute-start(bf16[128,1152]{1,0:T(8,128)(2,1)S(1)} %pad_maximum_fusion.refs_9_.refs_10_.refs_11_), channel_id=1, source_target_pairs={{0,2},{1,3},{2,4},{3,5},{4,6},{5,7},{6,8},{7,9},{8,10},{9,11},{10,... | collective-permute-start | bytes 884744 | tf_op jit(solution)/shard_map/ppermute | solution.py:17
  8.5 4.3 %collective-permute-start.3 = (bf16[128,1152]{1,0:T(8,128)(2,1)S(1)}, bf16[128,1152]{1,0:T(8,128)(2,1)S(1)}, u32[]{:S(2)}, u32[]{:S(2)}) collective-permute-start(bf16[128,1152]{1,0:T(8,128)(2,1)S(1)} %pad_maximum_fusion.refs_9_.refs_10_.refs_11_), channel_id=1, source_target_pairs={{0,1},{1,2},{2,3},{3,4},{4,5},{5,6},{6,7},{7,8},{8,9},{9,10},{10,1... | collective-permute-start | bytes 884744 | tf_op jit(solution)/shard_map/ppermute | solution.py:17
  12.8 8.4 %collective-permute-done.refs_3_.refs_4_.refs_5_ = bf16[128,1152]{1,0:T(8,128)(2,1)S(1)} collective-permute-done((bf16[128,1152]{1,0:T(8,128)(2,1)S(1)}, bf16[128,1152]{1,0:T(8,128)(2,1)S(1)}, u32[]{:S(2)}, u32[]{:S(2)}) %collective-permute-start) | collective-permute-done | bytes 294944 | tf_op jit(solution)/shard_map/ppermute | solution.py:17
  21.2 0.0 copy-start.1
  21.2 0.0 copy-done
  21.3 0.7 copy-done.1
  21.9 6.5 %collective-permute-start.2 = (bf16[128,640]{1,0:T(8,128)(2,1)S(1)}, bf16[128,640]{1,0:T(8,128)(2,1)S(1)}, u32[]{:S(2)}, u32[]{:S(2)}) collective-permute-start(bf16[128,640]{1,0:T(8,128)(2,1)S(1)} %pad_maximum_fusion.2), channel_id=1, source_target_pairs={{0,1},{1,2},{2,3},{3,4},{4,5},{5,6},{6,7},{7,8},{8,9},{9,10},{10,1... | collective-permute-start | bytes 491528 | tf_op jit(solution)/shard_map/ppermute | solution.py:17
  28.4 0.0 collective-permute-done.3.refs_6_.refs_7_.refs_8_
  28.5 0.0 copy-start.2
  28.5 10.0 %collective-permute-done.2.refs_0_.refs_1_.refs_2_ = bf16[128,640]{1,0:T(8,128)(2,1)S(1)} collective-permute-done((bf16[128,640]{1,0:T(8,128)(2,1)S(1)}, bf16[128,640]{1,0:T(8,128)(2,1)S(1)}, u32[]{:S(2)}, u32[]{:S(2)}) %collective-permute-start.2) | collective-permute-done | bytes 163872 | tf_op jit(solution)/shard_map/ppermute | solution.py:17
  38.4 0.0 copy-done.2
  38.4 0.0 copy-start.3
  38.4 0.7 copy-done.3
  39.1 8.0 %shard_map.76 = (bf16[128,4096]{1,0:T(8,128)(2,1)}, bf16[2,2,128,256]{3,2,1,0:T(8,128)(2,1)}, f32[2,128,256]{2,1,0:T(8,128)}, f32[2,128,256]{2,1,0:T(8,128)}) custom-call(bf16[128,4096]{1,0:T(8,128)(2,1)} %query_ref.3, bf16[128,4096]{1,0:T(8,128)(2,1)} %grad_ref.3, bf16[128,640]{1,0:T(8,128)(2,1)} %copy-done.3, bf16[128,640]{1,0:T(8,128)(2,1)} %copy-done.3, ...), custom_call_target="tpu_custom_call" | custom-call | tf_op jit(solution)/shard_map/pallas_call | solution.py:108
  47.1 4.1 %collective-permute-start.4 = (bf16[2,2,128,256]{3,2,1,0:T(8,128)(2,1)}, bf16[2,2,128,256]{3,2,1,0:T(8,128)(2,1)S(1)}, u32[]{:S(2)}, u32[]{:S(2)}) collective-permute-start(bf16[2,2,128,256]{3,2,1,0:T(8,128)(2,1)} %get-tuple-element.14), channel_id=1, source_target_pairs={{1,0},{2,1},{3,2},{4,3},{5,4},{6,5},{7,6},{8,7},{9,8},{10,9},{11,1... | collective-permute-start | bytes 786440 | tf_op jit(solution)/shard_map/ppermute | solution.py:17
  51.2 1.9 %collective-permute-start.1 = (bf16[128,512]{1,0:T(8,128)(2,1)S(1)}, bf16[128,512]{1,0:T(8,128)(2,1)S(1)}, u32[]{:S(2)}, u32[]{:S(2)}) collective-permute-start(bf16[128,512]{1,0:T(8,128)(2,1)S(1)} %pad_maximum_fusion.3), channel_id=1, source_target_pairs={{0,1},{1,2},{2,3},{3,4},{4,5},{5,6},{6,7},{7,8},{8,9},{9,10},{10,1... | collective-permute-start | bytes 393224 | tf_op jit(solution)/shard_map/ppermute | solution.py:17
  53.2 6.5 %collective-permute-done.1.refs_0_.refs_1_ = bf16[128,512]{1,0:T(8,128)(2,1)S(1)} collective-permute-done((bf16[128,512]{1,0:T(8,128)(2,1)S(1)}, bf16[128,512]{1,0:T(8,128)(2,1)S(1)}, u32[]{:S(2)}, u32[]{:S(2)}) %collective-permute-start.1) | collective-permute-done | bytes 131104 | tf_op jit(solution)/shard_map/ppermute | solution.py:17
  59.6 0.0 copy-start.4
  59.6 0.7 copy-done.4
  60.3 0.0 copy-start.5
  60.3 0.0 copy-start.6
  60.3 8.1 %shard_map.77 = (bf16[128,4096]{1,0:T(8,128)(2,1)}, bf16[2,2,128,256]{3,2,1,0:T(8,128)(2,1)}, f32[2,128,256]{2,1,0:T(8,128)}, f32[2,128,256]{2,1,0:T(8,128)}) custom-call(bf16[128,4096]{1,0:T(8,128)(2,1)} %query_ref.3, bf16[128,4096]{1,0:T(8,128)(2,1)} %grad_ref.3, bf16[128,512]{1,0:T(8,128)(2,1)} %copy-done.4, ...), custom_call_target="tpu_custom_call", output_to_operand_aliasing={{0}: (14, {})} | custom-call | tf_op jit(solution)/shard_map/pallas_call | solution.py:108
  68.4 2.0 %collective-permute-start.5 = (bf16[2,2,128,256]{3,2,1,0:T(8,128)(2,1)}, bf16[2,2,128,256]{3,2,1,0:T(8,128)(2,1)S(1)}, u32[]{:S(2)}, u32[]{:S(2)}) collective-permute-start(bf16[2,2,128,256]{3,2,1,0:T(8,128)(2,1)} %get-tuple-element.16), channel_id=1, source_target_pairs={{1,0},{2,1},{3,2},{4,3},{5,4},{6,5},{7,6},{8,7},{9,8},{10,9},{11,1... | collective-permute-start | bytes 786440 | tf_op jit(solution)/shard_map/ppermute | solution.py:17
  70.4 0.0 collective-permute-done.4
  70.4 0.0 copy-done.5
  70.4 0.0 copy-done.6
  70.4 0.0 copy-start.7
  70.4 0.0 copy-start.8
  70.4 0.1 fusion.2
  70.5 8.8 %collective-permute-done.5 = bf16[2,2,128,256]{3,2,1,0:T(8,128)(2,1)S(1)} collective-permute-done((bf16[2,2,128,256]{3,2,1,0:T(8,128)(2,1)}, bf16[2,2,128,256]{3,2,1,0:T(8,128)(2,1)S(1)}, u32[]{:S(2)}, u32[]{:S(2)}) %collective-permute-start.5) | collective-permute-done | bytes 262176 | tf_op jit(solution)/shard_map/ppermute | solution.py:17
  79.3 0.0 copy-done.7
  79.3 0.0 copy-done.8
  79.3 0.1 fusion.1
  79.4 1.9 %collective-permute-start.6 = (bf16[2,128,512]{2,1,0:T(8,128)(2,1)S(1)}, bf16[2,128,512]{2,1,0:T(8,128)(2,1)S(1)}, u32[]{:S(2)}, u32[]{:S(2)}) collective-permute-start(bf16[2,128,512]{2,1,0:T(8,128)(2,1)S(1)} %pad_maximum_fusion.1), channel_id=1, source_target_pairs={{2,0},{3,1},{4,2},{5,3},{6,4},{7,5},{8,6},{9,7},{10,8},{11,9},{12,... | collective-permute-start | bytes 786440 | tf_op jit(solution)/shard_map/ppermute | solution.py:17
  81.4 14.7 %collective-permute-done.6 = bf16[2,128,512]{2,1,0:T(8,128)(2,1)S(1)} collective-permute-done((bf16[2,128,512]{2,1,0:T(8,128)(2,1)S(1)}, bf16[2,128,512]{2,1,0:T(8,128)(2,1)S(1)}, u32[]{:S(2)}, u32[]{:S(2)}) %collective-permute-start.6) | collective-permute-done | bytes 262176 | tf_op jit(solution)/shard_map/ppermute | solution.py:17
  96.0 0.1 fusion
  96.1 0.7 slice_bitcast_fusion
  (5 shorter events, 0.1 us)
Async XLA Ops:
  2.4 18.9 %copy-start = (bf16[128,1152]{1,0:T(8,128)(2,1)}, bf16[128,1152]{1,0:T(8,128)(2,1)S(1)}, u32[]{:S(2)}) copy-start(bf16[128,1152]{1,0:T(8,128)(2,1)S(1)} %pad_maximum_fusion.refs_9_.refs_10_.refs_11_) | copy-start | bytes 884740
  2.4 18.8 %collective-permute-start = (bf16[128,1152]{1,0:T(8,128)(2,1)S(1)}, bf16[128,1152]{1,0:T(8,128)(2,1)S(1)}, u32[]{:S(2)}, u32[]{:S(2)}) collective-permute-start(bf16[128,1152]{1,0:T(8,128)(2,1)S(1)} %pad_maximum_fusion.refs_9_.refs_10_.refs_11_), channel_id=1, source_target_pairs={{0,2},{1,3},{2,4},{3,5},{4,6},{5,7},{6,8},{7,9},{8,10},{9,11},{10,... | collective-permute-start | bytes 884744 | tf_op jit(solution)/shard_map/ppermute | solution.py:17
  8.5 20.0 %collective-permute-start.3 = (bf16[128,1152]{1,0:T(8,128)(2,1)S(1)}, bf16[128,1152]{1,0:T(8,128)(2,1)S(1)}, u32[]{:S(2)}, u32[]{:S(2)}) collective-permute-start(bf16[128,1152]{1,0:T(8,128)(2,1)S(1)} %pad_maximum_fusion.refs_9_.refs_10_.refs_11_), channel_id=1, source_target_pairs={{0,1},{1,2},{2,3},{3,4},{4,5},{5,6},{6,7},{7,8},{8,9},{9,10},{10,1... | collective-permute-start | bytes 884744 | tf_op jit(solution)/shard_map/ppermute | solution.py:17
  21.2 0.7 copy-start.1
  21.9 16.5 %collective-permute-start.2 = (bf16[128,640]{1,0:T(8,128)(2,1)S(1)}, bf16[128,640]{1,0:T(8,128)(2,1)S(1)}, u32[]{:S(2)}, u32[]{:S(2)}) collective-permute-start(bf16[128,640]{1,0:T(8,128)(2,1)S(1)} %pad_maximum_fusion.2), channel_id=1, source_target_pairs={{0,1},{1,2},{2,3},{3,4},{4,5},{5,6},{6,7},{7,8},{8,9},{9,10},{10,1... | collective-permute-start | bytes 491528 | tf_op jit(solution)/shard_map/ppermute | solution.py:17
  28.5 10.0 %copy-start.2 = (bf16[128,1152]{1,0:T(8,128)(2,1)}, bf16[128,1152]{1,0:T(8,128)(2,1)S(1)}, u32[]{:S(2)}) copy-start(bf16[128,1152]{1,0:T(8,128)(2,1)S(1)} %collective-permute-done.3.refs_6_.refs_7_.refs_8_) | copy-start | bytes 884740
  38.4 0.7 copy-start.3
  47.1 23.3 %collective-permute-start.4 = (bf16[2,2,128,256]{3,2,1,0:T(8,128)(2,1)}, bf16[2,2,128,256]{3,2,1,0:T(8,128)(2,1)S(1)}, u32[]{:S(2)}, u32[]{:S(2)}) collective-permute-start(bf16[2,2,128,256]{3,2,1,0:T(8,128)(2,1)} %get-tuple-element.14), channel_id=1, source_target_pairs={{1,0},{2,1},{3,2},{4,3},{5,4},{6,5},{7,6},{8,7},{9,8},{10,9},{11,1... | collective-permute-start | bytes 786440 | tf_op jit(solution)/shard_map/ppermute | solution.py:17
  51.2 8.4 %collective-permute-start.1 = (bf16[128,512]{1,0:T(8,128)(2,1)S(1)}, bf16[128,512]{1,0:T(8,128)(2,1)S(1)}, u32[]{:S(2)}, u32[]{:S(2)}) collective-permute-start(bf16[128,512]{1,0:T(8,128)(2,1)S(1)} %pad_maximum_fusion.3), channel_id=1, source_target_pairs={{0,1},{1,2},{2,3},{3,4},{4,5},{5,6},{6,7},{7,8},{8,9},{9,10},{10,1... | collective-permute-start | bytes 393224 | tf_op jit(solution)/shard_map/ppermute | solution.py:17
  59.6 0.7 copy-start.4
  60.3 10.1 %copy-start.5 = (f32[2,128,256]{2,1,0:T(8,128)S(1)}, f32[2,128,256]{2,1,0:T(8,128)}, u32[]{:S(2)}) copy-start(f32[2,128,256]{2,1,0:T(8,128)} %get-tuple-element.17) | copy-start | bytes 786436
  60.3 10.1 %copy-start.6 = (f32[2,128,256]{2,1,0:T(8,128)S(1)}, f32[2,128,256]{2,1,0:T(8,128)}, u32[]{:S(2)}) copy-start(f32[2,128,256]{2,1,0:T(8,128)} %get-tuple-element.13) | copy-start | bytes 786436
  68.4 10.9 %collective-permute-start.5 = (bf16[2,2,128,256]{3,2,1,0:T(8,128)(2,1)}, bf16[2,2,128,256]{3,2,1,0:T(8,128)(2,1)S(1)}, u32[]{:S(2)}, u32[]{:S(2)}) collective-permute-start(bf16[2,2,128,256]{3,2,1,0:T(8,128)(2,1)} %get-tuple-element.16), channel_id=1, source_target_pairs={{1,0},{2,1},{3,2},{4,3},{5,4},{6,5},{7,6},{8,7},{9,8},{10,9},{11,1... | collective-permute-start | bytes 786440 | tf_op jit(solution)/shard_map/ppermute | solution.py:17
  70.4 8.9 %copy-start.7 = (f32[2,128,256]{2,1,0:T(8,128)S(1)}, f32[2,128,256]{2,1,0:T(8,128)}, u32[]{:S(2)}) copy-start(f32[2,128,256]{2,1,0:T(8,128)} %get-tuple-element.18) | copy-start | bytes 786436
  70.4 8.9 %copy-start.8 = (f32[2,128,256]{2,1,0:T(8,128)S(1)}, f32[2,128,256]{2,1,0:T(8,128)}, u32[]{:S(2)}) copy-start(f32[2,128,256]{2,1,0:T(8,128)} %get-tuple-element.15) | copy-start | bytes 786436
  79.4 16.6 %collective-permute-start.6 = (bf16[2,128,512]{2,1,0:T(8,128)(2,1)S(1)}, bf16[2,128,512]{2,1,0:T(8,128)(2,1)S(1)}, u32[]{:S(2)}, u32[]{:S(2)}) collective-permute-start(bf16[2,128,512]{2,1,0:T(8,128)(2,1)S(1)} %pad_maximum_fusion.1), channel_id=1, source_target_pairs={{2,0},{3,1},{4,2},{5,3},{6,4},{7,5},{8,6},{9,7},{10,8},{11,9},{12,... | collective-permute-start | bytes 786440 | tf_op jit(solution)/shard_map/ppermute | solution.py:17

commit v9 on v6

--- a/solution.py
+++ b/solution.py
@@ -37,8 +37,8 @@
     allowed = allowed & (seg_k == seg_q)
     k_head = jnp.concatenate([ref[...] for ref in key_refs], 0)
     v_head = jnp.concatenate([ref[...] for ref in value_refs], 0)
-    key_acc = jnp.zeros((key_count, HEAD_WIDTH), jnp.float32)
-    value_acc = jnp.zeros((key_count, HEAD_WIDTH), jnp.float32)
+    key_acc_t = jnp.zeros((HEAD_WIDTH, key_count), jnp.float32)
+    value_acc_t = jnp.zeros((HEAD_WIDTH, key_count), jnp.float32)
     def head_scores(head):
         cols = slice(head * HEAD_WIDTH, (head + 1) * HEAD_WIDTH)
         q_head = query_ref[:, cols]
@@ -49,12 +49,12 @@
         prob_grad = lax.dot_general(
             o_grad, v_head, (((1,), (1,)), ((), ())), preferred_element_type=jnp.float32
         )
-        return q_head, o_grad, scores, prob_grad
+        return jnp.transpose(q_head), jnp.transpose(o_grad), scores, prob_grad
 
     pending = head_scores(0)
     for head in range(heads_per_group):
         cols = slice(head * HEAD_WIDTH, (head + 1) * HEAD_WIDTH)
-        q_head, o_grad, scores, prob_grad = pending
+        q_head_t, o_grad_t, scores, prob_grad = pending
         if head + 1 < heads_per_group:
             pending = head_scores(head + 1)
         scores = jnp.where(allowed, scores * inv_root, -1e30)
@@ -67,12 +67,12 @@
         dq_ref[:, cols] = jnp.dot(
             score_grad, k_head, preferred_element_type=jnp.float32
         ).astype(jnp.bfloat16)
-        key_acc = key_acc + lax.dot_general(
-            score_grad, q_head, (((0,), (0,)), ((), ())), preferred_element_type=jnp.float32
+        key_acc_t = key_acc_t + jnp.dot(q_head_t, score_grad, preferred_element_type=jnp.float32)
+        value_acc_t = value_acc_t + jnp.dot(
+            o_grad_t, probs_low, preferred_element_type=jnp.float32
         )
-        value_acc = value_acc + lax.dot_general(
-            probs_low, o_grad, (((0,), (0,)), ((), ())), preferred_element_type=jnp.float32
-        )
+    key_acc = jnp.transpose(key_acc_t)
+    value_acc = jnp.transpose(value_acc_t)
 
     def rows(block):
         return slice(block * tok_rows, (block + 1) * tok_rows)

time: 88.6 us -> 87.7 us (0.990)
  Pallas kernels: 14.2 us -> 13.3 us
    pallas_call x1, Pallas kernels: 14.2 us -> 13.3 us  [band_grads(): pl.pallas_call(band_kernel, grid=(kv_heads,), in_specs=[pl.BlockSpec((tok...]
where the time goes in v9:
time: 87.7 us; the launch traced here: 87.4 us
  waiting for transfers between devices  35.7 us (41%)
  starting transfers between devices  33.2 us (38%)
  Pallas kernels  13.3 us (15%)
  other arithmetic  2.94 us (3%)
  local copies, waits for them, and re-layouts  1.53 us (2%)
    ppermute x5, waiting for transfers between devices, from_behind(): return lax.ppermute(block, axis, route)  35.7 us
    ppermute x5, starting transfers between devices, from_behind(): return lax.ppermute(block, axis, route)  33.2 us
    pallas_call x1, Pallas kernels, band_grads(): pl.pallas_call(band_kernel, grid=(kv_heads,), in_specs=[pl.BlockSpec((tok...  13.3 us
  transfers between devices with their start and end apart: 5, of which 4 were waited for; matrix products, arithmetic and copies ran while one was open for 0% of the time, Pallas kernels for 0%

profile of v9, /device:TPU:56, one launch (start us, length us, event | category | flops | bytes accessed | tf_op | source)
XLA Modules:
  0.0 87.4 jit_solution(1836151807405278602)
XLA Ops:
  0.6 0.7 convert_element_type.29
  1.3 0.1 broadcast_in_dim.2
  1.4 1.0 %pad_maximum_fusion.refs_9_.refs_10_.refs_11_ = bf16[128,1152]{1,0:T(8,128)(2,1)S(1)} fusion(bf16[128,128]{1,0:T(8,128)(2,1)S(1)} %broadcast_in_dim.2, bf16[128,512]{1,0:T(8,128)(2,1)} %param.7, bf16[128,512]{1,0:T(8,128)(2,1)} %param.6), kind=kLoop, calls=%fused_computation.5 | loop fusion | flops 884736 | bytes 589824 | tf_op jit(solution)/shard_map/concatenate | solution.py:129
  2.4 0.0 copy-start
  2.4 6.1 %collective-permute-start = (bf16[128,1152]{1,0:T(8,128)(2,1)S(1)}, bf16[128,1152]{1,0:T(8,128)(2,1)S(1)}, u32[]{:S(2)}, u32[]{:S(2)}) collective-permute-start(bf16[128,1152]{1,0:T(8,128)(2,1)S(1)} %pad_maximum_fusion.refs_9_.refs_10_.refs_11_), channel_id=1, source_target_pairs={{0,2},{1,3},{2,4},{3,5},{4,6},{5,7},{6,8},{7,9},{8,10},{9,11},{10,... | collective-permute-start | bytes 884744 | tf_op jit(solution)/shard_map/ppermute | solution.py:16
  8.5 4.3 %collective-permute-start.2 = (bf16[128,1152]{1,0:T(8,128)(2,1)S(1)}, bf16[128,1152]{1,0:T(8,128)(2,1)S(1)}, u32[]{:S(2)}, u32[]{:S(2)}) collective-permute-start(bf16[128,1152]{1,0:T(8,128)(2,1)S(1)} %pad_maximum_fusion.refs_9_.refs_10_.refs_11_), channel_id=1, source_target_pairs={{0,1},{1,2},{2,3},{3,4},{4,5},{5,6},{6,7},{7,8},{8,9},{9,10},{10,1... | collective-permute-start | bytes 884744 | tf_op jit(solution)/shard_map/ppermute | solution.py:16
  12.8 11.2 %collective-permute-done.refs_3_.refs_4_.refs_5_ = bf16[128,1152]{1,0:T(8,128)(2,1)S(1)} collective-permute-done((bf16[128,1152]{1,0:T(8,128)(2,1)S(1)}, bf16[128,1152]{1,0:T(8,128)(2,1)S(1)}, u32[]{:S(2)}, u32[]{:S(2)}) %collective-permute-start) | collective-permute-done | bytes 294944 | tf_op jit(solution)/shard_map/ppermute | solution.py:16
  23.9 0.0 copy-start.1
  23.9 6.5 %collective-permute-start.1 = (bf16[128,1152]{1,0:T(8,128)(2,1)S(1)}, bf16[128,1152]{1,0:T(8,128)(2,1)S(1)}, u32[]{:S(2)}, u32[]{:S(2)}) collective-permute-start(bf16[128,1152]{1,0:T(8,128)(2,1)S(1)} %collective-permute-done.refs_3_.refs_4_.refs_5_), channel_id=1, source_target_pairs={{0,1},{1,2},{2,3},{3,4},{4,5},{5,6},{6,7},{7,8},{8,9},{9,10},{10,1... | collective-permute-start | bytes 884744 | tf_op jit(solution)/shard_map/ppermute | solution.py:16
  30.4 0.0 collective-permute-done.2.refs_6_.refs_7_.refs_8_
  30.4 0.0 copy-start.2
  30.4 11.4 %collective-permute-done.1.refs_0_.refs_1_.refs_2_ = bf16[128,1152]{1,0:T(8,128)(2,1)S(1)} collective-permute-done((bf16[128,1152]{1,0:T(8,128)(2,1)S(1)}, bf16[128,1152]{1,0:T(8,128)(2,1)S(1)}, u32[]{:S(2)}, u32[]{:S(2)}) %collective-permute-start.1) | collective-permute-done | bytes 294944 | tf_op jit(solution)/shard_map/ppermute | solution.py:16
  41.8 0.0 copy-done
  41.8 0.0 copy-done.1
  41.8 0.0 copy-done.2
  41.8 0.0 copy-start.3
  41.8 0.7 copy-done.3
  42.5 13.3 %shard_map.76 = (bf16[128,4096]{1,0:T(8,128)(2,1)}, bf16[2,2,128,512]{3,2,1,0:T(8,128)(2,1)}, f32[2,128,512]{2,1,0:T(8,128)}, f32[2,128,512]{2,1,0:T(8,128)}) custom-call(bf16[128,4096]{1,0:T(8,128)(2,1)} %query_ref.1, bf16[128,4096]{1,0:T(8,128)(2,1)} %grad_ref.1, bf16[128,1152]{1,0:T(8,128)(2,1)} %copy-done.3, bf16[128,1152]{1,0:T(8,128)(2,1)} %copy-done.3, ...), custom_call_target="tpu_custom_call" | custom-call | tf_op jit(solution)/shard_map/pallas_call | solution.py:100
  55.8 5.5 %collective-permute-start.3 = (bf16[2,2,128,512]{3,2,1,0:T(8,128)(2,1)}, bf16[2,2,128,512]{3,2,1,0:T(8,128)(2,1)S(1)}, u32[]{:S(2)}, u32[]{:S(2)}) collective-permute-start(bf16[2,2,128,512]{3,2,1,0:T(8,128)(2,1)} %get-tuple-element.9), channel_id=1, source_target_pairs={{1,0},{2,1},{3,2},{4,3},{5,4},{6,5},{7,6},{8,7},{9,8},{10,9},{11,1... | collective-permute-start | bytes 1572872 | tf_op jit(solution)/shard_map/ppermute | solution.py:16
  61.3 7.0 %collective-permute-done.3 = bf16[2,2,128,512]{3,2,1,0:T(8,128)(2,1)S(1)} collective-permute-done((bf16[2,2,128,512]{3,2,1,0:T(8,128)(2,1)}, bf16[2,2,128,512]{3,2,1,0:T(8,128)(2,1)S(1)}, u32[]{:S(2)}, u32[]{:S(2)}) %collective-permute-start.3) | collective-permute-done | bytes 524320 | tf_op jit(solution)/shard_map/ppermute | solution.py:16
  68.3 0.0 copy-start.4
  68.3 1.2 %fusion = bf16[2,128,512]{2,1,0:T(8,128)(2,1)S(1)} fusion(f32[2,128,512]{2,1,0:T(8,128)} %get-tuple-element.10, bf16[2,2,128,512]{3,2,1,0:T(8,128)(2,1)S(1)} %collective-permute-done.3), kind=kLoop, calls=%fused_computation.1 | loop fusion | flops 393216 | bytes 1048576 | tf_op jit(solution)/shard_map/convert_element_type | solution.py:136
  69.5 10.9 %collective-permute-start.4 = (bf16[2,128,512]{2,1,0:T(8,128)(2,1)S(1)}, bf16[2,128,512]{2,1,0:T(8,128)(2,1)S(1)}, u32[]{:S(2)}, u32[]{:S(2)}) collective-permute-start(bf16[2,128,512]{2,1,0:T(8,128)(2,1)S(1)} %fusion), channel_id=1, source_target_pairs={{2,0},{3,1},{4,2},{5,3},{6,4},{7,5},{8,6},{9,7},{10,8},{11,9},{12,... | collective-permute-start | bytes 786440 | tf_op jit(solution)/shard_map/ppermute | solution.py:16
  80.4 6.2 %collective-permute-done.4 = bf16[2,128,512]{2,1,0:T(8,128)(2,1)S(1)} collective-permute-done((bf16[2,128,512]{2,1,0:T(8,128)(2,1)S(1)}, bf16[2,128,512]{2,1,0:T(8,128)(2,1)S(1)}, u32[]{:S(2)}, u32[]{:S(2)}) %collective-permute-start.4) | collective-permute-done | bytes 262176 | tf_op jit(solution)/shard_map/ppermute | solution.py:16
  86.5 0.0 copy-done.4
  86.5 0.1 fusion.2
  86.7 0.7 slice_bitcast_fusion.2
Async XLA Ops:
  2.4 39.4 %copy-start = (bf16[128,1152]{1,0:T(8,128)(2,1)}, bf16[128,1152]{1,0:T(8,128)(2,1)S(1)}, u32[]{:S(2)}) copy-start(bf16[128,1152]{1,0:T(8,128)(2,1)S(1)} %pad_maximum_fusion.refs_9_.refs_10_.refs_11_) | copy-start | bytes 884740
  2.4 21.5 %collective-permute-start = (bf16[128,1152]{1,0:T(8,128)(2,1)S(1)}, bf16[128,1152]{1,0:T(8,128)(2,1)S(1)}, u32[]{:S(2)}, u32[]{:S(2)}) collective-permute-start(bf16[128,1152]{1,0:T(8,128)(2,1)S(1)} %pad_maximum_fusion.refs_9_.refs_10_.refs_11_), channel_id=1, source_target_pairs={{0,2},{1,3},{2,4},{3,5},{4,6},{5,7},{6,8},{7,9},{8,10},{9,11},{10,... | collective-permute-start | bytes 884744 | tf_op jit(solution)/shard_map/ppermute | solution.py:16
  8.5 21.9 %collective-permute-start.2 = (bf16[128,1152]{1,0:T(8,128)(2,1)S(1)}, bf16[128,1152]{1,0:T(8,128)(2,1)S(1)}, u32[]{:S(2)}, u32[]{:S(2)}) collective-permute-start(bf16[128,1152]{1,0:T(8,128)(2,1)S(1)} %pad_maximum_fusion.refs_9_.refs_10_.refs_11_), channel_id=1, source_target_pairs={{0,1},{1,2},{2,3},{3,4},{4,5},{5,6},{6,7},{7,8},{8,9},{9,10},{10,1... | collective-permute-start | bytes 884744 | tf_op jit(solution)/shard_map/ppermute | solution.py:16
  23.9 17.9 %copy-start.1 = (bf16[128,1152]{1,0:T(8,128)(2,1)}, bf16[128,1152]{1,0:T(8,128)(2,1)S(1)}, u32[]{:S(2)}) copy-start(bf16[128,1152]{1,0:T(8,128)(2,1)S(1)} %collective-permute-done.refs_3_.refs_4_.refs_5_) | copy-start | bytes 884740
  23.9 17.9 %collective-permute-start.1 = (bf16[128,1152]{1,0:T(8,128)(2,1)S(1)}, bf16[128,1152]{1,0:T(8,128)(2,1)S(1)}, u32[]{:S(2)}, u32[]{:S(2)}) collective-permute-start(bf16[128,1152]{1,0:T(8,128)(2,1)S(1)} %collective-permute-done.refs_3_.refs_4_.refs_5_), channel_id=1, source_target_pairs={{0,1},{1,2},{2,3},{3,4},{4,5},{5,6},{6,7},{7,8},{8,9},{9,10},{10,1... | collective-permute-start | bytes 884744 | tf_op jit(solution)/shard_map/ppermute | solution.py:16
  30.4 11.4 %copy-start.2 = (bf16[128,1152]{1,0:T(8,128)(2,1)}, bf16[128,1152]{1,0:T(8,128)(2,1)S(1)}, u32[]{:S(2)}) copy-start(bf16[128,1152]{1,0:T(8,128)(2,1)S(1)} %collective-permute-done.2.refs_6_.refs_7_.refs_8_) | copy-start | bytes 884740
  41.8 0.7 copy-start.3
  55.8 12.5 %collective-permute-start.3 = (bf16[2,2,128,512]{3,2,1,0:T(8,128)(2,1)}, bf16[2,2,128,512]{3,2,1,0:T(8,128)(2,1)S(1)}, u32[]{:S(2)}, u32[]{:S(2)}) collective-permute-start(bf16[2,2,128,512]{3,2,1,0:T(8,128)(2,1)} %get-tuple-element.9), channel_id=1, source_target_pairs={{1,0},{2,1},{3,2},{4,3},{5,4},{6,5},{7,6},{8,7},{9,8},{10,9},{11,1... | collective-permute-start | bytes 1572872 | tf_op jit(solution)/shard_map/ppermute | solution.py:16
  68.3 18.2 %copy-start.4 = (f32[2,128,512]{2,1,0:T(8,128)S(1)}, f32[2,128,512]{2,1,0:T(8,128)}, u32[]{:S(2)}) copy-start(f32[2,128,512]{2,1,0:T(8,128)} %get-tuple-element.8) | copy-start | bytes 1572868
  69.5 17.1 %collective-permute-start.4 = (bf16[2,128,512]{2,1,0:T(8,128)(2,1)S(1)}, bf16[2,128,512]{2,1,0:T(8,128)(2,1)S(1)}, u32[]{:S(2)}, u32[]{:S(2)}) collective-permute-start(bf16[2,128,512]{2,1,0:T(8,128)(2,1)S(1)} %fusion), channel_id=1, source_target_pairs={{2,0},{3,1},{4,2},{5,3},{6,4},{7,5},{8,6},{9,7},{10,8},{11,9},{12,... | collective-permute-start | bytes 786440 | tf_op jit(solution)/shard_map/ppermute | solution.py:16

commit v10 on v9

--- a/solution.py
+++ b/solution.py
@@ -8,6 +8,7 @@
 
 HEAD_WIDTH = 128
 SPAN = 3
+KV_PER_STEP = 2
 
 
 def from_behind(block, axis, distance):
@@ -35,14 +36,20 @@
     col = lax.broadcasted_iota(jnp.int32, (tok_rows, key_count), 1)
     allowed = (col > row) & (col <= row + window) & (col >= window - position * tok_rows)
     allowed = allowed & (seg_k == seg_q)
-    k_head = jnp.concatenate([ref[...] for ref in key_refs], 0)
-    v_head = jnp.concatenate([ref[...] for ref in value_refs], 0)
-    key_acc_t = jnp.zeros((HEAD_WIDTH, key_count), jnp.float32)
-    value_acc_t = jnp.zeros((HEAD_WIDTH, key_count), jnp.float32)
+    k_all = jnp.concatenate([ref[...] for ref in key_refs], 0)
+    v_all = jnp.concatenate([ref[...] for ref in value_refs], 0)
+    kv_per_step = k_all.shape[1] // HEAD_WIDTH
+    heads_per_kv = heads_per_group // kv_per_step
+    k_heads = [k_all[:, i * HEAD_WIDTH : (i + 1) * HEAD_WIDTH] for i in range(kv_per_step)]
+    v_heads = [v_all[:, i * HEAD_WIDTH : (i + 1) * HEAD_WIDTH] for i in range(kv_per_step)]
+    key_accs = [jnp.zeros((HEAD_WIDTH, key_count), jnp.float32) for _ in range(kv_per_step)]
+    value_accs = [jnp.zeros((HEAD_WIDTH, key_count), jnp.float32) for _ in range(kv_per_step)]
     def head_scores(head):
         cols = slice(head * HEAD_WIDTH, (head + 1) * HEAD_WIDTH)
         q_head = query_ref[:, cols]
         o_grad = grad_ref[:, cols]
+        k_head = k_heads[head // heads_per_kv]
+        v_head = v_heads[head // heads_per_kv]
         scores = lax.dot_general(
             q_head, k_head, (((1,), (1,)), ((), ())), preferred_element_type=jnp.float32
         )
@@ -55,6 +62,8 @@
     for head in range(heads_per_group):
         cols = slice(head * HEAD_WIDTH, (head + 1) * HEAD_WIDTH)
         q_head_t, o_grad_t, scores, prob_grad = pending
+        kv = head // heads_per_kv
+        k_head = k_heads[kv]
         if head + 1 < heads_per_group:
             pending = head_scores(head + 1)
         scores = jnp.where(allowed, scores * inv_root, -1e30)
@@ -67,39 +76,45 @@
         dq_ref[:, cols] = jnp.dot(
             score_grad, k_head, preferred_element_type=jnp.float32
         ).astype(jnp.bfloat16)
-        key_acc_t = key_acc_t + jnp.dot(q_head_t, score_grad, preferred_element_type=jnp.float32)
-        value_acc_t = value_acc_t + jnp.dot(
+        key_accs[kv] = key_accs[kv] + jnp.dot(
+            q_head_t, score_grad, preferred_element_type=jnp.float32
+        )
+        value_accs[kv] = value_accs[kv] + jnp.dot(
             o_grad_t, probs_low, preferred_element_type=jnp.float32
         )
-    key_acc = jnp.transpose(key_acc_t)
-    value_acc = jnp.transpose(value_acc_t)
 
     def rows(block):
         return slice(block * tok_rows, (block + 1) * tok_rows)
 
-    for slot, block in enumerate((0, 2)):
-        send_ref[slot, 0] = key_acc[rows(block)].astype(jnp.bfloat16)
-        send_ref[slot, 1] = value_acc[rows(block)].astype(jnp.bfloat16)
-    middle_ref[0] = key_acc[rows(1)]
-    middle_ref[1] = value_acc[rows(1)]
-    own_ref[0] = key_acc[rows(3)]
-    own_ref[1] = value_acc[rows(3)]
+    for kv in range(kv_per_step):
+        lanes = slice(kv * HEAD_WIDTH, (kv + 1) * HEAD_WIDTH)
+        key_acc = jnp.transpose(key_accs[kv])
+        value_acc = jnp.transpose(value_accs[kv])
+        for slot, block in enumerate((0, 2)):
+            send_ref[slot, 0, :, lanes] = key_acc[rows(block)].astype(jnp.bfloat16)
+            send_ref[slot, 1, :, lanes] = value_acc[rows(block)].astype(jnp.bfloat16)
+        middle_ref[0, :, lanes] = key_acc[rows(1)]
+        middle_ref[1, :, lanes] = value_acc[rows(1)]
+        own_ref[0, :, lanes] = key_acc[rows(3)]
+        own_ref[1, :, lanes] = value_acc[rows(3)]
 
 
 def band_grads(query_blk, grad_blk, blocks, kv_heads):
     tok_rows, q_width = query_blk.shape
     kv_width = kv_heads * HEAD_WIDTH
-    group_width = q_width // kv_heads
+    steps = kv_heads // KV_PER_STEP
+    step_width = KV_PER_STEP * HEAD_WIDTH
+    group_width = q_width // steps
     kv_specs = []
     kv_args = []
     for blk in blocks:
-        kv_specs.append(pl.BlockSpec((tok_rows, HEAD_WIDTH), lambda g: (0, g)))
-        kv_specs.append(pl.BlockSpec((tok_rows, HEAD_WIDTH), lambda g, n=kv_heads: (0, n + g)))
+        kv_specs.append(pl.BlockSpec((tok_rows, step_width), lambda g: (0, g)))
+        kv_specs.append(pl.BlockSpec((tok_rows, step_width), lambda g, n=steps: (0, n + g)))
         kv_specs.append(pl.BlockSpec((tok_rows, HEAD_WIDTH), lambda g, n=kv_heads: (0, 2 * n)))
         kv_args += [blk, blk, blk]
     return pl.pallas_call(
         band_kernel,
-        grid=(kv_heads,),
+        grid=(steps,),
         in_specs=[
             pl.BlockSpec((tok_rows, group_width), lambda g: (0, g)),
             pl.BlockSpec((tok_rows, group_width), lambda g: (0, g)),
@@ -107,9 +122,9 @@
         + kv_specs,
         out_specs=[
             pl.BlockSpec((tok_rows, group_width), lambda g: (0, g)),
-            pl.BlockSpec((2, 2, tok_rows, HEAD_WIDTH), lambda g: (0, 0, 0, g)),
-            pl.BlockSpec((2, tok_rows, HEAD_WIDTH), lambda g: (0, 0, g)),
-            pl.BlockSpec((2, tok_rows, HEAD_WIDTH), lambda g: (0, 0, g)),
+            pl.BlockSpec((2, 2, tok_rows, step_width), lambda g: (0, 0, 0, g)),
+            pl.BlockSpec((2, tok_rows, step_width), lambda g: (0, 0, g)),
+            pl.BlockSpec((2, tok_rows, step_width), lambda g: (0, 0, g)),
         ],
         out_shape=[
             jax.ShapeDtypeStruct((tok_rows, q_width), jnp.bfloat16),

time: 87.7 us -> 86.9 us (level)
  no operation moved by 1% of the time
where the time goes in v10:
time: 86.9 us; the launch traced here: 86.6 us
  waiting for transfers between devices  35.7 us (41%)
  starting transfers between devices  33.2 us (38%)
  Pallas kernels  12.5 us (14%)
  other arithmetic  2.94 us (3%)
  local copies, waits for them, and re-layouts  1.53 us (2%)
    ppermute x5, waiting for transfers between devices, from_behind(): return lax.ppermute(block, axis, route)  35.7 us
    ppermute x5, starting transfers between devices, from_behind(): return lax.ppermute(block, axis, route)  33.2 us
    pallas_call x1, Pallas kernels, band_grads(): pl.pallas_call(band_kernel, grid=(steps,), in_specs=[pl.BlockSpec((tok_ro...  12.5 us
  transfers between devices with their start and end apart: 5, of which 4 were waited for; matrix products, arithmetic and copies ran while one was open for 0% of the time, Pallas kernels for 0%

profile of v10, /device:TPU:56, one launch (start us, length us, event | category | flops | bytes accessed | tf_op | source)
XLA Modules:
  0.0 86.6 jit_solution(10980197268763132547)
XLA Ops:
  0.6 0.7 convert_element_type.29
  1.3 0.1 broadcast_in_dim.2
  1.4 1.0 %pad_maximum_fusion.refs_9_.refs_10_.refs_11_ = bf16[128,1152]{1,0:T(8,128)(2,1)S(1)} fusion(bf16[128,128]{1,0:T(8,128)(2,1)S(1)} %broadcast_in_dim.2, bf16[128,512]{1,0:T(8,128)(2,1)} %param.7, bf16[128,512]{1,0:T(8,128)(2,1)} %param.6), kind=kLoop, calls=%fused_computation.5 | loop fusion | flops 884736 | bytes 589824 | tf_op jit(solution)/shard_map/concatenate | solution.py:144
  2.4 0.0 copy-start
  2.4 6.1 %collective-permute-start = (bf16[128,1152]{1,0:T(8,128)(2,1)S(1)}, bf16[128,1152]{1,0:T(8,128)(2,1)S(1)}, u32[]{:S(2)}, u32[]{:S(2)}) collective-permute-start(bf16[128,1152]{1,0:T(8,128)(2,1)S(1)} %pad_maximum_fusion.refs_9_.refs_10_.refs_11_), channel_id=1, source_target_pairs={{0,2},{1,3},{2,4},{3,5},{4,6},{5,7},{6,8},{7,9},{8,10},{9,11},{10,... | collective-permute-start | bytes 884744 | tf_op jit(solution)/shard_map/ppermute | solution.py:17
  8.5 4.3 %collective-permute-start.2 = (bf16[128,1152]{1,0:T(8,128)(2,1)S(1)}, bf16[128,1152]{1,0:T(8,128)(2,1)S(1)}, u32[]{:S(2)}, u32[]{:S(2)}) collective-permute-start(bf16[128,1152]{1,0:T(8,128)(2,1)S(1)} %pad_maximum_fusion.refs_9_.refs_10_.refs_11_), channel_id=1, source_target_pairs={{0,1},{1,2},{2,3},{3,4},{4,5},{5,6},{6,7},{7,8},{8,9},{9,10},{10,1... | collective-permute-start | bytes 884744 | tf_op jit(solution)/shard_map/ppermute | solution.py:17
  12.8 11.2 %collective-permute-done.refs_3_.refs_4_.refs_5_ = bf16[128,1152]{1,0:T(8,128)(2,1)S(1)} collective-permute-done((bf16[128,1152]{1,0:T(8,128)(2,1)S(1)}, bf16[128,1152]{1,0:T(8,128)(2,1)S(1)}, u32[]{:S(2)}, u32[]{:S(2)}) %collective-permute-start) | collective-permute-done | bytes 294944 | tf_op jit(solution)/shard_map/ppermute | solution.py:17
  23.9 0.0 copy-start.1
  23.9 6.5 %collective-permute-start.1 = (bf16[128,1152]{1,0:T(8,128)(2,1)S(1)}, bf16[128,1152]{1,0:T(8,128)(2,1)S(1)}, u32[]{:S(2)}, u32[]{:S(2)}) collective-permute-start(bf16[128,1152]{1,0:T(8,128)(2,1)S(1)} %collective-permute-done.refs_3_.refs_4_.refs_5_), channel_id=1, source_target_pairs={{0,1},{1,2},{2,3},{3,4},{4,5},{5,6},{6,7},{7,8},{8,9},{9,10},{10,1... | collective-permute-start | bytes 884744 | tf_op jit(solution)/shard_map/ppermute | solution.py:17
  30.4 0.0 collective-permute-done.2.refs_6_.refs_7_.refs_8_
  30.4 0.0 copy-start.2
  30.4 11.4 %collective-permute-done.1.refs_0_.refs_1_.refs_2_ = bf16[128,1152]{1,0:T(8,128)(2,1)S(1)} collective-permute-done((bf16[128,1152]{1,0:T(8,128)(2,1)S(1)}, bf16[128,1152]{1,0:T(8,128)(2,1)S(1)}, u32[]{:S(2)}, u32[]{:S(2)}) %collective-permute-start.1) | collective-permute-done | bytes 294944 | tf_op jit(solution)/shard_map/ppermute | solution.py:17
  41.8 0.0 copy-done
  41.8 0.0 copy-done.1
  41.8 0.0 copy-done.2
  41.8 0.0 copy-start.3
  41.8 0.7 copy-done.3
  42.5 12.5 %shard_map.76 = (bf16[128,4096]{1,0:T(8,128)(2,1)}, bf16[2,2,128,512]{3,2,1,0:T(8,128)(2,1)}, f32[2,128,512]{2,1,0:T(8,128)}, f32[2,128,512]{2,1,0:T(8,128)}) custom-call(bf16[128,4096]{1,0:T(8,128)(2,1)} %query_ref.1, bf16[128,4096]{1,0:T(8,128)(2,1)} %grad_ref.1, bf16[128,1152]{1,0:T(8,128)(2,1)} %copy-done.3, bf16[128,1152]{1,0:T(8,128)(2,1)} %copy-done.3, ...), custom_call_target="tpu_custom_call" | custom-call | tf_op jit(solution)/shard_map/pallas_call | solution.py:115
  55.1 5.5 %collective-permute-start.3 = (bf16[2,2,128,512]{3,2,1,0:T(8,128)(2,1)}, bf16[2,2,128,512]{3,2,1,0:T(8,128)(2,1)S(1)}, u32[]{:S(2)}, u32[]{:S(2)}) collective-permute-start(bf16[2,2,128,512]{3,2,1,0:T(8,128)(2,1)} %get-tuple-element.9), channel_id=1, source_target_pairs={{1,0},{2,1},{3,2},{4,3},{5,4},{6,5},{7,6},{8,7},{9,8},{10,9},{11,1... | collective-permute-start | bytes 1572872 | tf_op jit(solution)/shard_map/ppermute | solution.py:17
  60.5 7.0 %collective-permute-done.3 = bf16[2,2,128,512]{3,2,1,0:T(8,128)(2,1)S(1)} collective-permute-done((bf16[2,2,128,512]{3,2,1,0:T(8,128)(2,1)}, bf16[2,2,128,512]{3,2,1,0:T(8,128)(2,1)S(1)}, u32[]{:S(2)}, u32[]{:S(2)}) %collective-permute-start.3) | collective-permute-done | bytes 524320 | tf_op jit(solution)/shard_map/ppermute | solution.py:17
  67.5 0.0 copy-start.4
  67.5 1.2 %fusion = bf16[2,128,512]{2,1,0:T(8,128)(2,1)S(1)} fusion(f32[2,128,512]{2,1,0:T(8,128)} %get-tuple-element.10, bf16[2,2,128,512]{3,2,1,0:T(8,128)(2,1)S(1)} %collective-permute-done.3), kind=kLoop, calls=%fused_computation.1 | loop fusion | flops 393216 | bytes 1048576 | tf_op jit(solution)/shard_map/convert_element_type | solution.py:151
  68.7 10.9 %collective-permute-start.4 = (bf16[2,128,512]{2,1,0:T(8,128)(2,1)S(1)}, bf16[2,128,512]{2,1,0:T(8,128)(2,1)S(1)}, u32[]{:S(2)}, u32[]{:S(2)}) collective-permute-start(bf16[2,128,512]{2,1,0:T(8,128)(2,1)S(1)} %fusion), channel_id=1, source_target_pairs={{2,0},{3,1},{4,2},{5,3},{6,4},{7,5},{8,6},{9,7},{10,8},{11,9},{12,... | collective-permute-start | bytes 786440 | tf_op jit(solution)/shard_map/ppermute | solution.py:17
  79.6 6.2 %collective-permute-done.4 = bf16[2,128,512]{2,1,0:T(8,128)(2,1)S(1)} collective-permute-done((bf16[2,128,512]{2,1,0:T(8,128)(2,1)S(1)}, bf16[2,128,512]{2,1,0:T(8,128)(2,1)S(1)}, u32[]{:S(2)}, u32[]{:S(2)}) %collective-permute-start.4) | collective-permute-done | bytes 262176 | tf_op jit(solution)/shard_map/ppermute | solution.py:17
  85.8 0.0 copy-done.4
  85.8 0.1 fusion.2
  85.9 0.7 slice_bitcast_fusion.2
Async XLA Ops:
  2.4 39.4 %copy-start = (bf16[128,1152]{1,0:T(8,128)(2,1)}, bf16[128,1152]{1,0:T(8,128)(2,1)S(1)}, u32[]{:S(2)}) copy-start(bf16[128,1152]{1,0:T(8,128)(2,1)S(1)} %pad_maximum_fusion.refs_9_.refs_10_.refs_11_) | copy-start | bytes 884740
  2.4 21.5 %collective-permute-start = (bf16[128,1152]{1,0:T(8,128)(2,1)S(1)}, bf16[128,1152]{1,0:T(8,128)(2,1)S(1)}, u32[]{:S(2)}, u32[]{:S(2)}) collective-permute-start(bf16[128,1152]{1,0:T(8,128)(2,1)S(1)} %pad_maximum_fusion.refs_9_.refs_10_.refs_11_), channel_id=1, source_target_pairs={{0,2},{1,3},{2,4},{3,5},{4,6},{5,7},{6,8},{7,9},{8,10},{9,11},{10,... | collective-permute-start | bytes 884744 | tf_op jit(solution)/shard_map/ppermute | solution.py:17
  8.5 21.9 %collective-permute-start.2 = (bf16[128,1152]{1,0:T(8,128)(2,1)S(1)}, bf16[128,1152]{1,0:T(8,128)(2,1)S(1)}, u32[]{:S(2)}, u32[]{:S(2)}) collective-permute-start(bf16[128,1152]{1,0:T(8,128)(2,1)S(1)} %pad_maximum_fusion.refs_9_.refs_10_.refs_11_), channel_id=1, source_target_pairs={{0,1},{1,2},{2,3},{3,4},{4,5},{5,6},{6,7},{7,8},{8,9},{9,10},{10,1... | collective-permute-start | bytes 884744 | tf_op jit(solution)/shard_map/ppermute | solution.py:17
  23.9 17.9 %copy-start.1 = (bf16[128,1152]{1,0:T(8,128)(2,1)}, bf16[128,1152]{1,0:T(8,128)(2,1)S(1)}, u32[]{:S(2)}) copy-start(bf16[128,1152]{1,0:T(8,128)(2,1)S(1)} %collective-permute-done.refs_3_.refs_4_.refs_5_) | copy-start | bytes 884740
  23.9 17.9 %collective-permute-start.1 = (bf16[128,1152]{1,0:T(8,128)(2,1)S(1)}, bf16[128,1152]{1,0:T(8,128)(2,1)S(1)}, u32[]{:S(2)}, u32[]{:S(2)}) collective-permute-start(bf16[128,1152]{1,0:T(8,128)(2,1)S(1)} %collective-permute-done.refs_3_.refs_4_.refs_5_), channel_id=1, source_target_pairs={{0,1},{1,2},{2,3},{3,4},{4,5},{5,6},{6,7},{7,8},{8,9},{9,10},{10,1... | collective-permute-start | bytes 884744 | tf_op jit(solution)/shard_map/ppermute | solution.py:17
  30.4 11.4 %copy-start.2 = (bf16[128,1152]{1,0:T(8,128)(2,1)}, bf16[128,1152]{1,0:T(8,128)(2,1)S(1)}, u32[]{:S(2)}) copy-start(bf16[128,1152]{1,0:T(8,128)(2,1)S(1)} %collective-permute-done.2.refs_6_.refs_7_.refs_8_) | copy-start | bytes 884740
  41.8 0.7 copy-start.3
  55.1 12.5 %collective-permute-start.3 = (bf16[2,2,128,512]{3,2,1,0:T(8,128)(2,1)}, bf16[2,2,128,512]{3,2,1,0:T(8,128)(2,1)S(1)}, u32[]{:S(2)}, u32[]{:S(2)}) collective-permute-start(bf16[2,2,128,512]{3,2,1,0:T(8,128)(2,1)} %get-tuple-element.9), channel_id=1, source_target_pairs={{1,0},{2,1},{3,2},{4,3},{5,4},{6,5},{7,6},{8,7},{9,8},{10,9},{11,1... | collective-permute-start | bytes 1572872 | tf_op jit(solution)/shard_map/ppermute | solution.py:17
  67.5 18.3 %copy-start.4 = (f32[2,128,512]{2,1,0:T(8,128)S(1)}, f32[2,128,512]{2,1,0:T(8,128)}, u32[]{:S(2)}) copy-start(f32[2,128,512]{2,1,0:T(8,128)} %get-tuple-element.8) | copy-start | bytes 1572868
  68.7 17.1 %collective-permute-start.4 = (bf16[2,128,512]{2,1,0:T(8,128)(2,1)S(1)}, bf16[2,128,512]{2,1,0:T(8,128)(2,1)S(1)}, u32[]{:S(2)}, u32[]{:S(2)}) collective-permute-start(bf16[2,128,512]{2,1,0:T(8,128)(2,1)S(1)} %fusion), channel_id=1, source_target_pairs={{2,0},{3,1},{4,2},{5,3},{6,4},{7,5},{8,6},{9,7},{10,8},{11,9},{12,... | collective-permute-start | bytes 786440 | tf_op jit(solution)/shard_map/ppermute | solution.py:17

commit v11 on v10

--- a/solution.py
+++ b/solution.py
@@ -8,7 +8,7 @@
 
 HEAD_WIDTH = 128
 SPAN = 3
-KV_PER_STEP = 2
+KV_PER_STEP = 4
 
 
 def from_behind(block, axis, distance):

time: 86.9 us -> 87.6 us (level)
  no operation moved by 1% of the time
where the time goes in v11:
time: 87.6 us; the launch traced here: 87.3 us
  waiting for transfers between devices  35.7 us (41%)
  starting transfers between devices  33.2 us (38%)
  Pallas kernels  13.2 us (15%)
  other arithmetic  2.94 us (3%)
  local copies, waits for them, and re-layouts  1.53 us (2%)
    ppermute x5, waiting for transfers between devices, from_behind(): return lax.ppermute(block, axis, route)  35.7 us
    ppermute x5, starting transfers between devices, from_behind(): return lax.ppermute(block, axis, route)  33.2 us
    pallas_call x1, Pallas kernels, band_grads(): pl.pallas_call(band_kernel, grid=(steps,), in_specs=[pl.BlockSpec((tok_ro...  13.2 us
  transfers between devices with their start and end apart: 5, of which 4 were waited for; matrix products, arithmetic and copies ran while one was open for 0% of the time, Pallas kernels for 0%

profile of v11, /device:TPU:56, one launch (start us, length us, event | category | flops | bytes accessed | tf_op | source)
XLA Modules:
  0.0 87.3 jit_solution(7283644512004261685)
XLA Ops:
  0.6 0.7 convert_element_type.29
  1.3 0.1 broadcast_in_dim.2
  1.4 1.0 %pad_maximum_fusion.refs_9_.refs_10_.refs_11_ = bf16[128,1152]{1,0:T(8,128)(2,1)S(1)} fusion(bf16[128,128]{1,0:T(8,128)(2,1)S(1)} %broadcast_in_dim.2, bf16[128,512]{1,0:T(8,128)(2,1)} %param.7, bf16[128,512]{1,0:T(8,128)(2,1)} %param.6), kind=kLoop, calls=%fused_computation.5 | loop fusion | flops 884736 | bytes 589824 | tf_op jit(solution)/shard_map/concatenate | solution.py:144
  2.4 0.0 copy-start
  2.4 6.1 %collective-permute-start = (bf16[128,1152]{1,0:T(8,128)(2,1)S(1)}, bf16[128,1152]{1,0:T(8,128)(2,1)S(1)}, u32[]{:S(2)}, u32[]{:S(2)}) collective-permute-start(bf16[128,1152]{1,0:T(8,128)(2,1)S(1)} %pad_maximum_fusion.refs_9_.refs_10_.refs_11_), channel_id=1, source_target_pairs={{0,2},{1,3},{2,4},{3,5},{4,6},{5,7},{6,8},{7,9},{8,10},{9,11},{10,... | collective-permute-start | bytes 884744 | tf_op jit(solution)/shard_map/ppermute | solution.py:17
  8.5 4.3 %collective-permute-start.2 = (bf16[128,1152]{1,0:T(8,128)(2,1)S(1)}, bf16[128,1152]{1,0:T(8,128)(2,1)S(1)}, u32[]{:S(2)}, u32[]{:S(2)}) collective-permute-start(bf16[128,1152]{1,0:T(8,128)(2,1)S(1)} %pad_maximum_fusion.refs_9_.refs_10_.refs_11_), channel_id=1, source_target_pairs={{0,1},{1,2},{2,3},{3,4},{4,5},{5,6},{6,7},{7,8},{8,9},{9,10},{10,1... | collective-permute-start | bytes 884744 | tf_op jit(solution)/shard_map/ppermute | solution.py:17
  12.8 11.2 %collective-permute-done.refs_3_.refs_4_.refs_5_ = bf16[128,1152]{1,0:T(8,128)(2,1)S(1)} collective-permute-done((bf16[128,1152]{1,0:T(8,128)(2,1)S(1)}, bf16[128,1152]{1,0:T(8,128)(2,1)S(1)}, u32[]{:S(2)}, u32[]{:S(2)}) %collective-permute-start) | collective-permute-done | bytes 294944 | tf_op jit(solution)/shard_map/ppermute | solution.py:17
  23.9 0.0 copy-start.1
  23.9 6.5 %collective-permute-start.1 = (bf16[128,1152]{1,0:T(8,128)(2,1)S(1)}, bf16[128,1152]{1,0:T(8,128)(2,1)S(1)}, u32[]{:S(2)}, u32[]{:S(2)}) collective-permute-start(bf16[128,1152]{1,0:T(8,128)(2,1)S(1)} %collective-permute-done.refs_3_.refs_4_.refs_5_), channel_id=1, source_target_pairs={{0,1},{1,2},{2,3},{3,4},{4,5},{5,6},{6,7},{7,8},{8,9},{9,10},{10,1... | collective-permute-start | bytes 884744 | tf_op jit(solution)/shard_map/ppermute | solution.py:17
  30.4 0.0 collective-permute-done.2.refs_6_.refs_7_.refs_8_
  30.4 0.0 copy-start.2
  30.4 11.4 %collective-permute-done.1.refs_0_.refs_1_.refs_2_ = bf16[128,1152]{1,0:T(8,128)(2,1)S(1)} collective-permute-done((bf16[128,1152]{1,0:T(8,128)(2,1)S(1)}, bf16[128,1152]{1,0:T(8,128)(2,1)S(1)}, u32[]{:S(2)}, u32[]{:S(2)}) %collective-permute-start.1) | collective-permute-done | bytes 294944 | tf_op jit(solution)/shard_map/ppermute | solution.py:17
  41.8 0.0 copy-done
  41.8 0.0 copy-done.1
  41.8 0.0 copy-done.2
  41.8 0.0 copy-start.3
  41.8 0.7 copy-done.3
  42.5 13.2 %shard_map.76 = (bf16[128,4096]{1,0:T(8,128)(2,1)}, bf16[2,2,128,512]{3,2,1,0:T(8,128)(2,1)}, f32[2,128,512]{2,1,0:T(8,128)}, f32[2,128,512]{2,1,0:T(8,128)}) custom-call(bf16[128,4096]{1,0:T(8,128)(2,1)} %query_ref.1, bf16[128,4096]{1,0:T(8,128)(2,1)} %grad_ref.1, bf16[128,1152]{1,0:T(8,128)(2,1)} %copy-done.3, bf16[128,1152]{1,0:T(8,128)(2,1)} %copy-done.3, ...), custom_call_target="tpu_custom_call" | custom-call | tf_op jit(solution)/shard_map/pallas_call | solution.py:115
  55.8 5.4 %collective-permute-start.3 = (bf16[2,2,128,512]{3,2,1,0:T(8,128)(2,1)}, bf16[2,2,128,512]{3,2,1,0:T(8,128)(2,1)S(1)}, u32[]{:S(2)}, u32[]{:S(2)}) collective-permute-start(bf16[2,2,128,512]{3,2,1,0:T(8,128)(2,1)} %get-tuple-element.9), channel_id=1, source_target_pairs={{1,0},{2,1},{3,2},{4,3},{5,4},{6,5},{7,6},{8,7},{9,8},{10,9},{11,1... | collective-permute-start | bytes 1572872 | tf_op jit(solution)/shard_map/ppermute | solution.py:17
  61.2 7.0 %collective-permute-done.3 = bf16[2,2,128,512]{3,2,1,0:T(8,128)(2,1)S(1)} collective-permute-done((bf16[2,2,128,512]{3,2,1,0:T(8,128)(2,1)}, bf16[2,2,128,512]{3,2,1,0:T(8,128)(2,1)S(1)}, u32[]{:S(2)}, u32[]{:S(2)}) %collective-permute-start.3) | collective-permute-done | bytes 524320 | tf_op jit(solution)/shard_map/ppermute | solution.py:17
  68.2 0.0 copy-start.4
  68.2 1.2 %fusion = bf16[2,128,512]{2,1,0:T(8,128)(2,1)S(1)} fusion(f32[2,128,512]{2,1,0:T(8,128)} %get-tuple-element.10, bf16[2,2,128,512]{3,2,1,0:T(8,128)(2,1)S(1)} %collective-permute-done.3), kind=kLoop, calls=%fused_computation.1 | loop fusion | flops 393216 | bytes 1048576 | tf_op jit(solution)/shard_map/convert_element_type | solution.py:151
  69.4 10.9 %collective-permute-start.4 = (bf16[2,128,512]{2,1,0:T(8,128)(2,1)S(1)}, bf16[2,128,512]{2,1,0:T(8,128)(2,1)S(1)}, u32[]{:S(2)}, u32[]{:S(2)}) collective-permute-start(bf16[2,128,512]{2,1,0:T(8,128)(2,1)S(1)} %fusion), channel_id=1, source_target_pairs={{2,0},{3,1},{4,2},{5,3},{6,4},{7,5},{8,6},{9,7},{10,8},{11,9},{12,... | collective-permute-start | bytes 786440 | tf_op jit(solution)/shard_map/ppermute | solution.py:17
  80.3 6.2 %collective-permute-done.4 = bf16[2,128,512]{2,1,0:T(8,128)(2,1)S(1)} collective-permute-done((bf16[2,128,512]{2,1,0:T(8,128)(2,1)S(1)}, bf16[2,128,512]{2,1,0:T(8,128)(2,1)S(1)}, u32[]{:S(2)}, u32[]{:S(2)}) %collective-permute-start.4) | collective-permute-done | bytes 262176 | tf_op jit(solution)/shard_map/ppermute | solution.py:17
  86.5 0.0 copy-done.4
  86.5 0.1 fusion.2
  86.6 0.7 slice_bitcast_fusion.2
Async XLA Ops:
  2.4 39.4 %copy-start = (bf16[128,1152]{1,0:T(8,128)(2,1)}, bf16[128,1152]{1,0:T(8,128)(2,1)S(1)}, u32[]{:S(2)}) copy-start(bf16[128,1152]{1,0:T(8,128)(2,1)S(1)} %pad_maximum_fusion.refs_9_.refs_10_.refs_11_) | copy-start | bytes 884740
  2.4 21.5 %collective-permute-start = (bf16[128,1152]{1,0:T(8,128)(2,1)S(1)}, bf16[128,1152]{1,0:T(8,128)(2,1)S(1)}, u32[]{:S(2)}, u32[]{:S(2)}) collective-permute-start(bf16[128,1152]{1,0:T(8,128)(2,1)S(1)} %pad_maximum_fusion.refs_9_.refs_10_.refs_11_), channel_id=1, source_target_pairs={{0,2},{1,3},{2,4},{3,5},{4,6},{5,7},{6,8},{7,9},{8,10},{9,11},{10,... | collective-permute-start | bytes 884744 | tf_op jit(solution)/shard_map/ppermute | solution.py:17
  8.5 21.9 %collective-permute-start.2 = (bf16[128,1152]{1,0:T(8,128)(2,1)S(1)}, bf16[128,1152]{1,0:T(8,128)(2,1)S(1)}, u32[]{:S(2)}, u32[]{:S(2)}) collective-permute-start(bf16[128,1152]{1,0:T(8,128)(2,1)S(1)} %pad_maximum_fusion.refs_9_.refs_10_.refs_11_), channel_id=1, source_target_pairs={{0,1},{1,2},{2,3},{3,4},{4,5},{5,6},{6,7},{7,8},{8,9},{9,10},{10,1... | collective-permute-start | bytes 884744 | tf_op jit(solution)/shard_map/ppermute | solution.py:17
  23.9 17.9 %copy-start.1 = (bf16[128,1152]{1,0:T(8,128)(2,1)}, bf16[128,1152]{1,0:T(8,128)(2,1)S(1)}, u32[]{:S(2)}) copy-start(bf16[128,1152]{1,0:T(8,128)(2,1)S(1)} %collective-permute-done.refs_3_.refs_4_.refs_5_) | copy-start | bytes 884740
  23.9 17.9 %collective-permute-start.1 = (bf16[128,1152]{1,0:T(8,128)(2,1)S(1)}, bf16[128,1152]{1,0:T(8,128)(2,1)S(1)}, u32[]{:S(2)}, u32[]{:S(2)}) collective-permute-start(bf16[128,1152]{1,0:T(8,128)(2,1)S(1)} %collective-permute-done.refs_3_.refs_4_.refs_5_), channel_id=1, source_target_pairs={{0,1},{1,2},{2,3},{3,4},{4,5},{5,6},{6,7},{7,8},{8,9},{9,10},{10,1... | collective-permute-start | bytes 884744 | tf_op jit(solution)/shard_map/ppermute | solution.py:17
  30.4 11.4 %copy-start.2 = (bf16[128,1152]{1,0:T(8,128)(2,1)}, bf16[128,1152]{1,0:T(8,128)(2,1)S(1)}, u32[]{:S(2)}) copy-start(bf16[128,1152]{1,0:T(8,128)(2,1)S(1)} %collective-permute-done.2.refs_6_.refs_7_.refs_8_) | copy-start | bytes 884740
  41.8 0.7 copy-start.3
  55.8 12.4 %collective-permute-start.3 = (bf16[2,2,128,512]{3,2,1,0:T(8,128)(2,1)}, bf16[2,2,128,512]{3,2,1,0:T(8,128)(2,1)S(1)}, u32[]{:S(2)}, u32[]{:S(2)}) collective-permute-start(bf16[2,2,128,512]{3,2,1,0:T(8,128)(2,1)} %get-tuple-element.9), channel_id=1, source_target_pairs={{1,0},{2,1},{3,2},{4,3},{5,4},{6,5},{7,6},{8,7},{9,8},{10,9},{11,1... | collective-permute-start | bytes 1572872 | tf_op jit(solution)/shard_map/ppermute | solution.py:17
  68.2 18.3 %copy-start.4 = (f32[2,128,512]{2,1,0:T(8,128)S(1)}, f32[2,128,512]{2,1,0:T(8,128)}, u32[]{:S(2)}) copy-start(f32[2,128,512]{2,1,0:T(8,128)} %get-tuple-element.8) | copy-start | bytes 1572868
  69.4 17.1 %collective-permute-start.4 = (bf16[2,128,512]{2,1,0:T(8,128)(2,1)S(1)}, bf16[2,128,512]{2,1,0:T(8,128)(2,1)S(1)}, u32[]{:S(2)}, u32[]{:S(2)}) collective-permute-start(bf16[2,128,512]{2,1,0:T(8,128)(2,1)S(1)} %fusion), channel_id=1, source_target_pairs={{2,0},{3,1},{4,2},{5,3},{6,4},{7,5},{8,6},{9,7},{10,8},{11,9},{12,... | collective-permute-start | bytes 786440 | tf_op jit(solution)/shard_map/ppermute | solution.py:17

commit v12 on v10

--- a/solution.py
+++ b/solution.py
@@ -36,6 +36,7 @@
     col = lax.broadcasted_iota(jnp.int32, (tok_rows, key_count), 1)
     allowed = (col > row) & (col <= row + window) & (col >= window - position * tok_rows)
     allowed = allowed & (seg_k == seg_q)
+    bias = jnp.where(allowed, 0.0, -1e30).astype(jnp.float32)
     k_all = jnp.concatenate([ref[...] for ref in key_refs], 0)
     v_all = jnp.concatenate([ref[...] for ref in value_refs], 0)
     kv_per_step = k_all.shape[1] // HEAD_WIDTH
@@ -58,15 +59,15 @@
         )
         return jnp.transpose(q_head), jnp.transpose(o_grad), scores, prob_grad
 
-    pending = head_scores(0)
+    pending = [head_scores(head) for head in range(2)]
     for head in range(heads_per_group):
         cols = slice(head * HEAD_WIDTH, (head + 1) * HEAD_WIDTH)
-        q_head_t, o_grad_t, scores, prob_grad = pending
+        q_head_t, o_grad_t, scores, prob_grad = pending.pop(0)
         kv = head // heads_per_kv
         k_head = k_heads[kv]
-        if head + 1 < heads_per_group:
-            pending = head_scores(head + 1)
-        scores = jnp.where(allowed, scores * inv_root, -1e30)
+        if head + 2 < heads_per_group:
+            pending.append(head_scores(head + 2))
+        scores = scores * inv_root + bias
         row_max = jnp.max(scores, axis=1, keepdims=True)
         weights = jnp.exp(scores - row_max)
         probs = weights * (1.0 / jnp.sum(weights, axis=1, keepdims=True))

time: 86.9 us -> 86.1 us (level)
  no operation moved by 1% of the time
where the time goes in v12:
time: 86.1 us; the launch traced here: 85.8 us
  waiting for transfers between devices  35.7 us (41%)
  starting transfers between devices  33.2 us (39%)
  Pallas kernels  11.7 us (14%)
  other arithmetic  2.94 us (3%)
  local copies, waits for them, and re-layouts  1.53 us (2%)
    ppermute x5, waiting for transfers between devices, from_behind(): return lax.ppermute(block, axis, route)  35.7 us
    ppermute x5, starting transfers between devices, from_behind(): return lax.ppermute(block, axis, route)  33.2 us
    pallas_call x1, Pallas kernels, band_grads(): pl.pallas_call(band_kernel, grid=(steps,), in_specs=[pl.BlockSpec((tok_ro...  11.7 us
  transfers between devices with their start and end apart: 5, of which 4 were waited for; matrix products, arithmetic and copies ran while one was open for 0% of the time, Pallas kernels for 0%

profile of v12, /device:TPU:56, one launch (start us, length us, event | category | flops | bytes accessed | tf_op | source)
XLA Modules:
  0.0 85.8 jit_solution(11035101956049071869)
XLA Ops:
  0.6 0.7 convert_element_type.29
  1.3 0.1 broadcast_in_dim.2
  1.4 1.0 %pad_maximum_fusion.refs_9_.refs_10_.refs_11_ = bf16[128,1152]{1,0:T(8,128)(2,1)S(1)} fusion(bf16[128,128]{1,0:T(8,128)(2,1)S(1)} %broadcast_in_dim.2, bf16[128,512]{1,0:T(8,128)(2,1)} %param.7, bf16[128,512]{1,0:T(8,128)(2,1)} %param.6), kind=kLoop, calls=%fused_computation.5 | loop fusion | flops 884736 | bytes 589824 | tf_op jit(solution)/shard_map/concatenate | solution.py:145
  2.4 0.0 copy-start
  2.4 6.1 %collective-permute-start = (bf16[128,1152]{1,0:T(8,128)(2,1)S(1)}, bf16[128,1152]{1,0:T(8,128)(2,1)S(1)}, u32[]{:S(2)}, u32[]{:S(2)}) collective-permute-start(bf16[128,1152]{1,0:T(8,128)(2,1)S(1)} %pad_maximum_fusion.refs_9_.refs_10_.refs_11_), channel_id=1, source_target_pairs={{0,2},{1,3},{2,4},{3,5},{4,6},{5,7},{6,8},{7,9},{8,10},{9,11},{10,... | collective-permute-start | bytes 884744 | tf_op jit(solution)/shard_map/ppermute | solution.py:17
  8.5 4.3 %collective-permute-start.2 = (bf16[128,1152]{1,0:T(8,128)(2,1)S(1)}, bf16[128,1152]{1,0:T(8,128)(2,1)S(1)}, u32[]{:S(2)}, u32[]{:S(2)}) collective-permute-start(bf16[128,1152]{1,0:T(8,128)(2,1)S(1)} %pad_maximum_fusion.refs_9_.refs_10_.refs_11_), channel_id=1, source_target_pairs={{0,1},{1,2},{2,3},{3,4},{4,5},{5,6},{6,7},{7,8},{8,9},{9,10},{10,1... | collective-permute-start | bytes 884744 | tf_op jit(solution)/shard_map/ppermute | solution.py:17
  12.8 11.2 %collective-permute-done.refs_3_.refs_4_.refs_5_ = bf16[128,1152]{1,0:T(8,128)(2,1)S(1)} collective-permute-done((bf16[128,1152]{1,0:T(8,128)(2,1)S(1)}, bf16[128,1152]{1,0:T(8,128)(2,1)S(1)}, u32[]{:S(2)}, u32[]{:S(2)}) %collective-permute-start) | collective-permute-done | bytes 294944 | tf_op jit(solution)/shard_map/ppermute | solution.py:17
  23.9 0.0 copy-start.1
  23.9 6.5 %collective-permute-start.1 = (bf16[128,1152]{1,0:T(8,128)(2,1)S(1)}, bf16[128,1152]{1,0:T(8,128)(2,1)S(1)}, u32[]{:S(2)}, u32[]{:S(2)}) collective-permute-start(bf16[128,1152]{1,0:T(8,128)(2,1)S(1)} %collective-permute-done.refs_3_.refs_4_.refs_5_), channel_id=1, source_target_pairs={{0,1},{1,2},{2,3},{3,4},{4,5},{5,6},{6,7},{7,8},{8,9},{9,10},{10,1... | collective-permute-start | bytes 884744 | tf_op jit(solution)/shard_map/ppermute | solution.py:17
  30.4 0.0 collective-permute-done.2.refs_6_.refs_7_.refs_8_
  30.4 0.0 copy-start.2
  30.4 11.4 %collective-permute-done.1.refs_0_.refs_1_.refs_2_ = bf16[128,1152]{1,0:T(8,128)(2,1)S(1)} collective-permute-done((bf16[128,1152]{1,0:T(8,128)(2,1)S(1)}, bf16[128,1152]{1,0:T(8,128)(2,1)S(1)}, u32[]{:S(2)}, u32[]{:S(2)}) %collective-permute-start.1) | collective-permute-done | bytes 294944 | tf_op jit(solution)/shard_map/ppermute | solution.py:17
  41.8 0.0 copy-done
  41.8 0.0 copy-done.1
  41.8 0.0 copy-done.2
  41.8 0.0 copy-start.3
  41.8 0.7 copy-done.3
  42.5 11.7 %shard_map.76 = (bf16[128,4096]{1,0:T(8,128)(2,1)}, bf16[2,2,128,512]{3,2,1,0:T(8,128)(2,1)}, f32[2,128,512]{2,1,0:T(8,128)}, f32[2,128,512]{2,1,0:T(8,128)}) custom-call(bf16[128,4096]{1,0:T(8,128)(2,1)} %query_ref.1, bf16[128,4096]{1,0:T(8,128)(2,1)} %grad_ref.1, bf16[128,1152]{1,0:T(8,128)(2,1)} %copy-done.3, bf16[128,1152]{1,0:T(8,128)(2,1)} %copy-done.3, ...), custom_call_target="tpu_custom_call" | custom-call | tf_op jit(solution)/shard_map/pallas_call | solution.py:116
  54.2 5.5 %collective-permute-start.3 = (bf16[2,2,128,512]{3,2,1,0:T(8,128)(2,1)}, bf16[2,2,128,512]{3,2,1,0:T(8,128)(2,1)S(1)}, u32[]{:S(2)}, u32[]{:S(2)}) collective-permute-start(bf16[2,2,128,512]{3,2,1,0:T(8,128)(2,1)} %get-tuple-element.9), channel_id=1, source_target_pairs={{1,0},{2,1},{3,2},{4,3},{5,4},{6,5},{7,6},{8,7},{9,8},{10,9},{11,1... | collective-permute-start | bytes 1572872 | tf_op jit(solution)/shard_map/ppermute | solution.py:17
  59.7 7.0 %collective-permute-done.3 = bf16[2,2,128,512]{3,2,1,0:T(8,128)(2,1)S(1)} collective-permute-done((bf16[2,2,128,512]{3,2,1,0:T(8,128)(2,1)}, bf16[2,2,128,512]{3,2,1,0:T(8,128)(2,1)S(1)}, u32[]{:S(2)}, u32[]{:S(2)}) %collective-permute-start.3) | collective-permute-done | bytes 524320 | tf_op jit(solution)/shard_map/ppermute | solution.py:17
  66.7 0.0 copy-start.4
  66.7 1.2 %fusion = bf16[2,128,512]{2,1,0:T(8,128)(2,1)S(1)} fusion(f32[2,128,512]{2,1,0:T(8,128)} %get-tuple-element.10, bf16[2,2,128,512]{3,2,1,0:T(8,128)(2,1)S(1)} %collective-permute-done.3), kind=kLoop, calls=%fused_computation.1 | loop fusion | flops 393216 | bytes 1048576 | tf_op jit(solution)/shard_map/convert_element_type | solution.py:152
  67.9 10.9 %collective-permute-start.4 = (bf16[2,128,512]{2,1,0:T(8,128)(2,1)S(1)}, bf16[2,128,512]{2,1,0:T(8,128)(2,1)S(1)}, u32[]{:S(2)}, u32[]{:S(2)}) collective-permute-start(bf16[2,128,512]{2,1,0:T(8,128)(2,1)S(1)} %fusion), channel_id=1, source_target_pairs={{2,0},{3,1},{4,2},{5,3},{6,4},{7,5},{8,6},{9,7},{10,8},{11,9},{12,... | collective-permute-start | bytes 786440 | tf_op jit(solution)/shard_map/ppermute | solution.py:17
  78.8 6.2 %collective-permute-done.4 = bf16[2,128,512]{2,1,0:T(8,128)(2,1)S(1)} collective-permute-done((bf16[2,128,512]{2,1,0:T(8,128)(2,1)S(1)}, bf16[2,128,512]{2,1,0:T(8,128)(2,1)S(1)}, u32[]{:S(2)}, u32[]{:S(2)}) %collective-permute-start.4) | collective-permute-done | bytes 262176 | tf_op jit(solution)/shard_map/ppermute | solution.py:17
  85.0 0.0 copy-done.4
  85.0 0.1 fusion.2
  85.1 0.7 slice_bitcast_fusion.2
Async XLA Ops:
  2.4 39.4 %copy-start = (bf16[128,1152]{1,0:T(8,128)(2,1)}, bf16[128,1152]{1,0:T(8,128)(2,1)S(1)}, u32[]{:S(2)}) copy-start(bf16[128,1152]{1,0:T(8,128)(2,1)S(1)} %pad_maximum_fusion.refs_9_.refs_10_.refs_11_) | copy-start | bytes 884740
  2.4 21.5 %collective-permute-start = (bf16[128,1152]{1,0:T(8,128)(2,1)S(1)}, bf16[128,1152]{1,0:T(8,128)(2,1)S(1)}, u32[]{:S(2)}, u32[]{:S(2)}) collective-permute-start(bf16[128,1152]{1,0:T(8,128)(2,1)S(1)} %pad_maximum_fusion.refs_9_.refs_10_.refs_11_), channel_id=1, source_target_pairs={{0,2},{1,3},{2,4},{3,5},{4,6},{5,7},{6,8},{7,9},{8,10},{9,11},{10,... | collective-permute-start | bytes 884744 | tf_op jit(solution)/shard_map/ppermute | solution.py:17
  8.5 21.9 %collective-permute-start.2 = (bf16[128,1152]{1,0:T(8,128)(2,1)S(1)}, bf16[128,1152]{1,0:T(8,128)(2,1)S(1)}, u32[]{:S(2)}, u32[]{:S(2)}) collective-permute-start(bf16[128,1152]{1,0:T(8,128)(2,1)S(1)} %pad_maximum_fusion.refs_9_.refs_10_.refs_11_), channel_id=1, source_target_pairs={{0,1},{1,2},{2,3},{3,4},{4,5},{5,6},{6,7},{7,8},{8,9},{9,10},{10,1... | collective-permute-start | bytes 884744 | tf_op jit(solution)/shard_map/ppermute | solution.py:17
  23.9 17.9 %copy-start.1 = (bf16[128,1152]{1,0:T(8,128)(2,1)}, bf16[128,1152]{1,0:T(8,128)(2,1)S(1)}, u32[]{:S(2)}) copy-start(bf16[128,1152]{1,0:T(8,128)(2,1)S(1)} %collective-permute-done.refs_3_.refs_4_.refs_5_) | copy-start | bytes 884740
  23.9 17.9 %collective-permute-start.1 = (bf16[128,1152]{1,0:T(8,128)(2,1)S(1)}, bf16[128,1152]{1,0:T(8,128)(2,1)S(1)}, u32[]{:S(2)}, u32[]{:S(2)}) collective-permute-start(bf16[128,1152]{1,0:T(8,128)(2,1)S(1)} %collective-permute-done.refs_3_.refs_4_.refs_5_), channel_id=1, source_target_pairs={{0,1},{1,2},{2,3},{3,4},{4,5},{5,6},{6,7},{7,8},{8,9},{9,10},{10,1... | collective-permute-start | bytes 884744 | tf_op jit(solution)/shard_map/ppermute | solution.py:17
  30.4 11.4 %copy-start.2 = (bf16[128,1152]{1,0:T(8,128)(2,1)}, bf16[128,1152]{1,0:T(8,128)(2,1)S(1)}, u32[]{:S(2)}) copy-start(bf16[128,1152]{1,0:T(8,128)(2,1)S(1)} %collective-permute-done.2.refs_6_.refs_7_.refs_8_) | copy-start | bytes 884740
  41.8 0.7 copy-start.3
  54.2 12.5 %collective-permute-start.3 = (bf16[2,2,128,512]{3,2,1,0:T(8,128)(2,1)}, bf16[2,2,128,512]{3,2,1,0:T(8,128)(2,1)S(1)}, u32[]{:S(2)}, u32[]{:S(2)}) collective-permute-start(bf16[2,2,128,512]{3,2,1,0:T(8,128)(2,1)} %get-tuple-element.9), channel_id=1, source_target_pairs={{1,0},{2,1},{3,2},{4,3},{5,4},{6,5},{7,6},{8,7},{9,8},{10,9},{11,1... | collective-permute-start | bytes 1572872 | tf_op jit(solution)/shard_map/ppermute | solution.py:17
  66.7 18.3 %copy-start.4 = (f32[2,128,512]{2,1,0:T(8,128)S(1)}, f32[2,128,512]{2,1,0:T(8,128)}, u32[]{:S(2)}) copy-start(f32[2,128,512]{2,1,0:T(8,128)} %get-tuple-element.8) | copy-start | bytes 1572868
  67.9 17.1 %collective-permute-start.4 = (bf16[2,128,512]{2,1,0:T(8,128)(2,1)S(1)}, bf16[2,128,512]{2,1,0:T(8,128)(2,1)S(1)}, u32[]{:S(2)}, u32[]{:S(2)}) collective-permute-start(bf16[2,128,512]{2,1,0:T(8,128)(2,1)S(1)} %fusion), channel_id=1, source_target_pairs={{2,0},{3,1},{4,2},{5,3},{6,4},{7,5},{8,6},{9,7},{10,8},{11,9},{12,... | collective-permute-start | bytes 786440 | tf_op jit(solution)/shard_map/ppermute | solution.py:17
